TPU v7x, 256 devices: a whole 4x4x8 slice. The times are simulated.
256 devices in a mesh: row: 64 (over z, x_hi, y), col: 4 (over x_lo, core).
Axes of the slice: x: 4 (x_hi: 2, x_lo: 2; x = x_hi * 2 + x_lo), y: 4, z: 8, core: 2. Of those that a mesh axis runs over, the one named last changes fastest.
Arguments:
- upper_tiles: bfloat16 [2048, 17, 4096], P(('row', 'col')), may hold values from -0.51 to 0.51, as said below
- block_columns: int32 [2048, 17], P(('row', 'col')), may hold values from -1 to 2047, as said below
Outputs:
- new_tiles: float32 [2048, 17, 4096], P(('row', 'col'))
- occupancy: float32 [], replicated
Inputs may be any that keep to these rules, and one draw needn't show every extreme that they name: `block_columns`: slot 0 of block row i holds i. The following slots hold distinct block columns (i + s) mod 2048 with 1 <= s <= 16, in increasing s, and the remaining slots hold -1. Some block rows fill all 17 slots. `upper_tiles`: the block in slot 0 is symmetric.
All inputs are finite; a program needn't handle non-finite values.
Results may differ from a plain program's by a relative error of at most 0.0003.
Values may be sent and summed in bfloat16 or wider, within the bound.
No kernel may reach another device: no remote copies, remote signals or barrier semaphores. Data moves between devices by JAX's collectives and lax.ppermute only.
A program may use at most 128 MiB of HBM per device.

v0:
```python
import math

import jax
import jax.numpy as jnp
import numpy as np
from jax import lax
from jax.sharding import PartitionSpec as P


def from_behind(shard, axis, by):
    length = lax.axis_size(axis)
    return lax.ppermute(shard, axis, [(i, (i + by) % length) for i in range(length)])


def entry_tables(rows_dev, half):
    band_width = half + 1
    window = rows_dev + 2 * half
    zero_index = window * band_width
    flipped_base = zero_index + 1

    def lookup(row_pos, col_pos):
        if col_pos >= row_pos and col_pos - row_pos <= half:
            return row_pos * band_width + col_pos - row_pos
        if col_pos < row_pos and row_pos - col_pos <= half:
            return flipped_base + col_pos * band_width + row_pos - col_pos
        return zero_index

    left_index = np.zeros((rows_dev, window), np.int32)
    for own_row in range(rows_dev):
        for other_row in range(window):
            left_index[own_row, other_row] = lookup(half + own_row, other_row)
    right_index = np.zeros((window, rows_dev + half), np.int32)
    for other_row in range(window):
        for column_pos in range(rows_dev + half):
            right_index[other_row, column_pos] = lookup(other_row, half + column_pos)
    return (left_index, right_index)


def flip_tiles(tiles, block):
    shaped = tiles.reshape(tiles.shape[:-1] + (block, block))
    return jnp.swapaxes(shaped, -1, -2).reshape(tiles.shape)


def body(upper_tiles, block_columns):
    rows_dev, slots, tile_size = upper_tiles.shape
    half = slots - 1
    block = math.isqrt(tile_size)
    devices = lax.axis_size(("row", "col"))
    nblocks = rows_dev * devices
    span_cols = rows_dev + half
    window_rows = rows_dev + 2 * half
    first_row = lax.axis_index(("row", "col")) * rows_dev
    local_rows = jnp.arange(rows_dev, dtype=jnp.int32)
    row_ids = first_row + local_rows
    slot_range = jnp.arange(slots, dtype=jnp.int32)
    listed = block_columns >= 0
    offsets_of = jnp.mod(block_columns - row_ids[:, None], nblocks)
    pick_band = (listed[:, :, None] & (offsets_of[:, :, None] == slot_range[None, None, :])).astype(
        jnp.bfloat16
    )
    own_band = jnp.einsum(
        "rso,rst->rot", pick_band, upper_tiles, preferred_element_type=jnp.float32
    ).astype(jnp.bfloat16)
    diag_own = upper_tiles[:, 0].astype(jnp.float32).reshape(rows_dev, block, block)
    own_trace = 2.0 * jnp.sum(jnp.diagonal(diag_own, axis1=1, axis2=2))
    reach = -(-half // rows_dev)
    below = []
    above = []
    moving = own_band
    for distance in range(reach):
        moving = from_behind(moving, ("row", "col"), 1)
        below.insert(0, moving)
    moving = own_band
    for distance in range(reach):
        moving = from_behind(moving, ("row", "col"), -1)
        above.append(moving)
    stacked = jnp.concatenate(below + [own_band] + above, axis=0)
    left_np, right_np = entry_tables(rows_dev, half)
    plain = stacked.reshape(window_rows * slots, tile_size)
    blank = jnp.zeros((1, tile_size), jnp.bfloat16)
    flat = jnp.concatenate([plain, blank, flip_tiles(plain, block)], axis=0)
    left = flat[jnp.asarray(left_np)].reshape(rows_dev, window_rows, block, block)
    right = flat[jnp.asarray(right_np)].reshape(window_rows, span_cols, block, block)
    product = jnp.einsum("rjab,jkbc->rkac", left, right, preferred_element_type=jnp.float32)
    product = product.reshape(rows_dev, span_cols, tile_size)
    target = jnp.where(listed, offsets_of + local_rows[:, None], -1)
    pick_new = (target[:, :, None] == jnp.arange(span_cols, dtype=jnp.int32)[None, None, :]).astype(
        jnp.float32
    )
    picked = jnp.einsum(
        "rsk,rkt->rst",
        pick_new,
        product,
        precision=lax.Precision.HIGHEST,
        preferred_element_type=jnp.float32,
    )
    new_tiles = jnp.where(listed[:, :, None], 2.0 * upper_tiles.astype(jnp.float32) - picked, 0.0)
    diag_product = product[local_rows, local_rows].reshape(rows_dev, block, block)
    total = lax.psum(
        own_trace - jnp.sum(jnp.diagonal(diag_product, axis1=1, axis2=2)), ("row", "col")
    )
    occupancy = (total / (nblocks * block)).astype(jnp.float32)
    return (new_tiles, occupancy)


def solution(mesh):
    placed = (P(("row", "col"), None, None), P(("row", "col"), None))
    return jax.shard_map(
        body,
        mesh=mesh,
        in_specs=placed,
        out_specs=(P(("row", "col"), None, None), P()),
        check_vma=False,
    )
```

profile of v0, /device:TPU:0, one launch (start us, length us, event | category | flops | bytes accessed | tf_op | source)
XLA Modules:
  0.0 361.2 jit_solution(5644888849714854533)
XLA Ops:
  0.6 0.8 add_select_fusion.1
  1.4 2.8 convolution_convert_fusion
  4.3 1.7 copy.24
  6.0 8.2 %collective-permute-start.2 = (bf16[8,17,4096]{2,0,1:T(8,128)(2,1)}, bf16[8,17,4096]{2,0,1:T(8,128)(2,1)S(1)}, u32[]{:S(2)}, u32[]{:S(2)}) collective-permute-start(bf16[8,17,4096]{2,0,1:T(8,128)(2,1)} %copy.24), channel_id=1, source_target_pairs={{0,255},{1,0},{2,1},{3,2},{4,3},{5,4},{6,5},{7,6},{8,7},{9,8},{10,... | collective-permute-start | bytes 3342344 | tf_op jit(solution)/shard_map/ppermute | solution.py:12
  14.2 13.5 %collective-permute-done = bf16[8,17,4096]{2,0,1:T(8,128)(2,1)} collective-permute-done((bf16[8,17,4096]{2,0,1:T(8,128)(2,1)}, bf16[8,17,4096]{2,0,1:T(8,128)(2,1)}, u32[]{:S(2)}, u32[]{:S(2)}) %collective-permute-start) | collective-permute-done | bytes 1114144 | tf_op jit(solution)/shard_map/ppermute | solution.py:12
  27.7 0.8 slice_convert_fusion
  28.6 1.9 copy.34
  30.5 1.6 gather_fusion.2
  33.4 7.2 %collective-permute-start.3 = (bf16[8,17,4096]{2,0,1:T(8,128)(2,1)S(1)}, bf16[8,17,4096]{2,0,1:T(8,128)(2,1)S(1)}, u32[]{:S(2)}, u32[]{:S(2)}) collective-permute-start(bf16[8,17,4096]{2,0,1:T(8,128)(2,1)S(1)} %collective-permute-done.2), channel_id=1, source_target_pairs={{0,255},{1,0},{2,1},{3,2},{4,3},{5,4},{6,5},{7,6},{8,7},{9,8},{10,... | collective-permute-start | bytes 3342344 | tf_op jit(solution)/shard_map/ppermute | solution.py:12
  40.6 7.7 %collective-permute-done.1 = bf16[8,17,4096]{2,0,1:T(8,128)(2,1)} collective-permute-done((bf16[8,17,4096]{2,0,1:T(8,128)(2,1)}, bf16[8,17,4096]{2,0,1:T(8,128)(2,1)}, u32[]{:S(2)}, u32[]{:S(2)}) %collective-permute-start.1) | collective-permute-done | bytes 1114144 | tf_op jit(solution)/shard_map/ppermute | solution.py:12
  48.4 3.1 copy_dynamic-update-slice_fusion.3
  51.5 3.1 copy_dynamic-update-slice_fusion.2
  54.6 1.3 constant_dynamic-update-slice_fusion
  55.8 1.8 copy_dynamic-update-slice_fusion.1
  57.6 1.8 copy_dynamic-update-slice_fusion
  59.5 8.1 %reshape.33 = bf16[680,4096]{1,0:T(8,128)(2,1)} reshape(bf16[40,17,4096]{2,1,0:T(8,128)(2,1)} %copy_dynamic-update-slice_fusion) | data formatting | bytes 11141120 | tf_op jit(solution)/shard_map/reshape | solution.py:79
  67.6 16.5 %reshape_reshape.3 = bf16[680,64,64]{2,1,0:T(8,128)(2,1)} reshape(bf16[40,17,4096]{2,1,0:T(8,128)(2,1)} %copy_dynamic-update-slice_fusion) | data formatting | bytes 11141120 | tf_op jit(solution)/shard_map/reshape;reshape | solution.py:40
  84.1 19.3 %copy.30 = bf16[680,64,64]{0,2,1:T(8,128)(2,1)} copy(bf16[680,64,64]{1,2,0:T(8,128)(2,1)} %bitcast.21) | data formatting | bytes 11141120 | tf_op jit(solution)/shard_map/transpose | solution.py:41
  103.4 8.3 %copy.31 = bf16[680,4096]{1,0:T(8,128)(2,1)} copy(bf16[680,4096]{0,1:T(8,128)(2,1)} %bitcast.22) | data formatting | bytes 11141120 | tf_op jit(solution)/shard_map/reshape | solution.py:41
  111.7 51.6 %concatenate.15 = bf16[1361,4096]{1,0:T(8,128)(2,1)} concatenate(bf16[680,4096]{1,0:T(8,128)(2,1)} %reshape.33, bf16[1,4096]{1,0:T(2,128)(2,1)S(1)} %broadcast_in_dim.43, bf16[680,4096]{1,0:T(8,128)(2,1)} %copy.31), dimensions={0} | concatenate | bytes 22298624 | tf_op jit(solution)/shard_map/concatenate | solution.py:81
  163.3 13.1 %gather_fusion.1 = bf16[320,4096]{1,0:T(8,128)(2,1)S(1)} fusion(bf16[1361,4096]{1,0:T(8,128)(2,1)} %concatenate.15, s32[1024]{0:T(1024)S(1)} %get-tuple-element.11), kind=kCustom, calls=%fused_computation.1 | custom fusion | bytes 5244160 | tf_op jit(solution)/shard_map/gather | solution.py:82
  176.4 6.7 %reshape.79 = bf16[8,40,64,64,1]{3,2,1,0,4:T(8,128)(2,1)} reshape(bf16[320,4096]{1,0:T(8,128)(2,1)S(1)} %gather_fusion.1) | data formatting | bytes 5242880 | tf_op jit(solution)/shard_map/reshape | solution.py:82
  183.1 20.8 %gather_fusion = bf16[960,4096]{1,0:T(8,128)(2,1)} fusion(bf16[1361,4096]{1,0:T(8,128)(2,1)} %concatenate.15, s32[1024]{0:T(1024)S(1)} %get-tuple-element.12), kind=kCustom, calls=%fused_computation | custom fusion | bytes 15732480 | tf_op jit(solution)/shard_map/gather | solution.py:83
  203.8 22.0 %reshape.35 = bf16[40,24,64,64]{3,2,1,0:T(8,128)(2,1)} reshape(bf16[960,4096]{1,0:T(8,128)(2,1)} %gather_fusion) | data formatting | bytes 15728640 | tf_op jit(solution)/shard_map/reshape | solution.py:83
  225.8 22.3 %fusion.3 = f32[8,24,64,64]{2,3,0,1:T(8,128)} fusion(bf16[8,40,64,64,1]{3,2,1,0,4:T(8,128)(2,1)} %reshape.79, bf16[40,24,64,64]{3,2,1,0:T(8,128)(2,1)} %reshape.35), kind=kOutput, calls=%fused_computation.10 | convolution fusion | flops 4026531840 | bytes 13631488 | tf_op jit(solution)/shard_map/rjab,jkbc->rkac/dot_general | solution.py:84
  248.1 6.6 %copy.33 = f32[8,24,64,64]{3,2,1,0:T(8,128)} copy(f32[8,24,64,64]{2,3,0,1:T(8,128)} %fusion.3) | data formatting | bytes 6291456 | tf_op jit(solution)/shard_map/rjab,jkbc->rkac/transpose | solution.py:84
  254.8 4.7 %reshape.37 = f32[8,24,4096]{2,1,0:T(8,128)S(1)} reshape(f32[8,24,64,64]{3,2,1,0:T(8,128)} %copy.33) | data formatting | bytes 6291456 | tf_op jit(solution)/shard_map/reshape | solution.py:85
  259.5 5.8 %fusion.2 = f32[8,17,4096]{2,1,0:T(8,128)} fusion(f32[8,24,4096]{2,1,0:T(8,128)S(1)} %reshape.37, bf16[8,17,4096]{2,0,1:T(8,128)(2,1)} %param.4, pred[8,17]{1,0:T(8,128)(4,1)S(1)} %get-tuple-element.9, s32[8,17]{1,0:T(8,128)S(1)} %get-tuple-element.8), kind=kOutput, calls=%fused_computation.8 | convolution fusion | flops 162663616 | bytes 6488744 | tf_op jit(solution)/shard_map/rsk,rkt->rst/dot_general | solution.py:90
  265.3 0.7 gather_fusion.3
  266.6 0.9 gather_fusion.4
  268.7 4.5 %copy.36 = f32[8,17,4096]{2,0,1:T(8,128)} copy(f32[8,17,4096]{2,1,0:T(8,128)} %fusion.2) | data formatting | bytes 4456448
  273.3 86.1 %psum.7 = f32[]{:T(128)} all-reduce(f32[]{:T(128)S(6)} %sub.17), channel_id=1, replica_groups=mesh['row'=64,'col'=4] {'row','col'}, use_global_device_ids=true, to_apply=%region_2.3 | all-reduce | flops 1 | bytes 8 | tf_op jit(solution)/shard_map/psum | solution.py:99
  (16 shorter events, 1.9 us)
Async XLA Ops:
  4.2 29.1 %copy-start = (s32[960]{0:T(1024)S(1)}, s32[960]{0:T(1024)}, u32[]{:S(2)}) copy-start(s32[960]{0:T(1024)} %constant.112) | copy-start | bytes 11524
  4.3 29.1 %copy-start.1 = (s32[320]{0:T(512)S(1)}, s32[320]{0:T(512)}, u32[]{:S(2)}) copy-start(s32[320]{0:T(512)} %constant.113) | copy-start | bytes 3844
  6.0 21.7 %collective-permute-start = (bf16[8,17,4096]{2,0,1:T(8,128)(2,1)}, bf16[8,17,4096]{2,0,1:T(8,128)(2,1)}, u32[]{:S(2)}, u32[]{:S(2)}) collective-permute-start(bf16[8,17,4096]{2,0,1:T(8,128)(2,1)} %copy.24), channel_id=1, source_target_pairs={{0,1},{1,2},{2,3},{3,4},{4,5},{5,6},{6,7},{7,8},{8,9},{9,10},{10,1... | collective-permute-start | bytes 3342344 | tf_op jit(solution)/shard_map/ppermute | solution.py:12
  6.0 27.4 %collective-permute-start.2 = (bf16[8,17,4096]{2,0,1:T(8,128)(2,1)}, bf16[8,17,4096]{2,0,1:T(8,128)(2,1)S(1)}, u32[]{:S(2)}, u32[]{:S(2)}) collective-permute-start(bf16[8,17,4096]{2,0,1:T(8,128)(2,1)} %copy.24), channel_id=1, source_target_pairs={{0,255},{1,0},{2,1},{3,2},{4,3},{5,4},{6,5},{7,6},{8,7},{9,8},{10,... | collective-permute-start | bytes 3342344 | tf_op jit(solution)/shard_map/ppermute | solution.py:12
  27.7 20.7 %collective-permute-start.1 = (bf16[8,17,4096]{2,0,1:T(8,128)(2,1)}, bf16[8,17,4096]{2,0,1:T(8,128)(2,1)}, u32[]{:S(2)}, u32[]{:S(2)}) collective-permute-start(bf16[8,17,4096]{2,0,1:T(8,128)(2,1)} %collective-permute-done), channel_id=1, source_target_pairs={{0,1},{1,2},{2,3},{3,4},{4,5},{5,6},{6,7},{7,8},{8,9},{9,10},{10,1... | collective-permute-start | bytes 3342344 | tf_op jit(solution)/shard_map/ppermute | solution.py:12
  33.4 24.2 %collective-permute-start.3 = (bf16[8,17,4096]{2,0,1:T(8,128)(2,1)S(1)}, bf16[8,17,4096]{2,0,1:T(8,128)(2,1)S(1)}, u32[]{:S(2)}, u32[]{:S(2)}) collective-permute-start(bf16[8,17,4096]{2,0,1:T(8,128)(2,1)S(1)} %collective-permute-done.2), channel_id=1, source_target_pairs={{0,255},{1,0},{2,1},{3,2},{4,3},{5,4},{6,5},{7,6},{8,7},{9,8},{10,... | collective-permute-start | bytes 3342344 | tf_op jit(solution)/shard_map/ppermute | solution.py:12
where the time goes:
time: 367 us; the launch traced here: 361 us
  local copies, waits for them, and re-layouts  201 us (55%)
  blocking collectives  86.1 us (23%)
  matrix products  31 us (8%)
  waiting for transfers between devices  21.2 us (6%)
  starting transfers between devices  15.5 us (4%)
  between operations  3.83 us (1%)
    psum x1, blocking collectives, body(): lax.psum(own_trace - jnp.sum(jnp.diagonal(diag_product, axis1=1, axis2=2)...  86.1 us
    concatenate x1, local copies, waits for them, and re-layouts, body(): flat = jnp.concatenate([plain, blank, flip_tiles(plain, block)], axis=0)  51.6 us
    dot_general x1, matrix products, body(): jnp.einsum('rjab,jkbc->rkac', left, right, preferred_element_type=jnp.flo...  22.3 us
    reshape x1, local copies, waits for them, and re-layouts, body(): flat[jnp.asarray(right_np)].reshape(window_rows, span_cols, block, block)  22 us
    ppermute x4, waiting for transfers between devices, from_behind(): lax.ppermute(shard, axis, [(i, (i + by) % length) for i in range(length)])  21.2 us
    gather x1, local copies, waits for them, and re-layouts, body(): flat[jnp.asarray(right_np)].reshape(window_rows, span_cols, block, block)  20.8 us
    transpose x1, local copies, waits for them, and re-layouts, flip_tiles(): return jnp.swapaxes(shaped, -1, -2).reshape(tiles.shape)  19.3 us
    another operation x1, local copies, waits for them, and re-layouts, flip_tiles(): shaped = tiles.reshape(tiles.shape[:-1] + (block, block))  16.5 us
  transfers between devices with their start and end apart: 4, of which 2 were waited for; matrix products, arithmetic and copies ran while one was open for 4% of the time, Pallas kernels for 0%

commit v1 on v0

--- a/solution.py
+++ b/solution.py
@@ -63,6 +63,12 @@
     ).astype(jnp.bfloat16)
     diag_own = upper_tiles[:, 0].astype(jnp.float32).reshape(rows_dev, block, block)
     own_trace = 2.0 * jnp.sum(jnp.diagonal(diag_own, axis1=1, axis2=2))
+    weight = jnp.where(listed, jnp.where(slot_range[None, :] == 0, 1.0, 2.0), 0.0)
+    squares = jnp.sum(jnp.square(upper_tiles.astype(jnp.float32)), axis=2)
+    part = own_trace - jnp.sum(weight * squares)
+    spread = jnp.where(lax.broadcasted_iota(jnp.int32, (8, 128), 1) == 0, part / 8.0, 0.0)
+    parts = lax.all_gather(spread, ("row", "col"), tiled=True)
+    total = jnp.sum(parts)
     reach = -(-half // rows_dev)
     below = []
     above = []
@@ -95,10 +101,6 @@
         preferred_element_type=jnp.float32,
     )
     new_tiles = jnp.where(listed[:, :, None], 2.0 * upper_tiles.astype(jnp.float32) - picked, 0.0)
-    diag_product = product[local_rows, local_rows].reshape(rows_dev, block, block)
-    total = lax.psum(
-        own_trace - jnp.sum(jnp.diagonal(diag_product, axis1=1, axis2=2)), ("row", "col")
-    )
     occupancy = (total / (nblocks * block)).astype(jnp.float32)
     return (new_tiles, occupancy)
 

time: 367 us -> 652 us (1.78)
  waiting for transfers between devices: 21.2 us -> 372 us
  blocking collectives: 86.1 us -> 0 us
  between operations: 3.83 us -> 17.2 us
    all_gather x0 -> x1, waiting for transfers between devices: none -> 358 us  [body(): parts = lax.all_gather(spread, ('row', 'col'), tiled=True)]
    psum x1 -> x0, blocking collectives: 86.1 us -> none  [body(): lax.psum(own_trace - jnp.sum(jnp.diagonal(diag_product, axis1=1, axis2=2)...]
    ppermute x4, waiting for transfers between devices: 21.2 us -> 13.3 us  [from_behind(): lax.ppermute(shard, axis, [(i, (i + by) % length) for i in range(length)])]
    unnamed x9 -> x11, local copies, waits for them, and re-layouts: 13.8 us -> 13.2 us
  transfers between devices with their start and end apart: 4 -> 5, of which waited for: 2 -> 3; matrix products, arithmetic and copies ran while one was open for 4% -> 3% of each run, Pallas kernels for 0% -> 0%
where the time goes in v1:
time: 652 us; the launch traced here: 645 us
  waiting for transfers between devices  372 us (57%)
  local copies, waits for them, and re-layouts  203 us (31%)
  matrix products  30 us (5%)
  between operations  17.2 us (3%)
  starting transfers between devices  15.7 us (2%)
  other arithmetic  7.44 us (1%)
    all_gather x1, waiting for transfers between devices, body(): parts = lax.all_gather(spread, ('row', 'col'), tiled=True)  358 us
    concatenate x1, local copies, waits for them, and re-layouts, body(): flat = jnp.concatenate([plain, blank, flip_tiles(plain, block)], axis=0)  51.6 us
    dot_general x1, matrix products, body(): jnp.einsum('rjab,jkbc->rkac', left, right, preferred_element_type=jnp.flo...  22.3 us
    reshape x1, local copies, waits for them, and re-layouts, body(): flat[jnp.asarray(right_np)].reshape(window_rows, span_cols, block, block)  22 us
    gather x1, local copies, waits for them, and re-layouts, body(): flat[jnp.asarray(right_np)].reshape(window_rows, span_cols, block, block)  20.5 us
    transpose x1, local copies, waits for them, and re-layouts, flip_tiles(): return jnp.swapaxes(shaped, -1, -2).reshape(tiles.shape)  19.3 us
    another operation x1, local copies, waits for them, and re-layouts, flip_tiles(): shaped = tiles.reshape(tiles.shape[:-1] + (block, block))  16.5 us
    ppermute x4, starting transfers between devices, from_behind(): lax.ppermute(shard, axis, [(i, (i + by) % length) for i in range(length)])  15.7 us
  transfers between devices with their start and end apart: 5, of which 3 were waited for; matrix products, arithmetic and copies ran while one was open for 3% of the time, Pallas kernels for 0%

profile of v1, /device:TPU:0, one launch (start us, length us, event | category | flops | bytes accessed | tf_op | source)
XLA Modules:
  0.0 645.1 jit_solution(1190718418480428512)
XLA Ops:
  7.2 2.5 fusion.3
  9.8 1.4 multiply_reduce_fusion
  11.2 0.8 add_select_fusion.1
  11.9 2.8 convolution_convert_fusion
  14.8 1.7 copy.36
  16.5 1.9 copy.46
  18.4 1.6 gather_fusion.2
  22.6 8.3 %collective-permute-start.2 = (bf16[8,17,4096]{2,0,1:T(8,128)(2,1)}, bf16[8,17,4096]{2,0,1:T(8,128)(2,1)}, u32[]{:S(2)}, u32[]{:S(2)}) collective-permute-start(bf16[8,17,4096]{2,0,1:T(8,128)(2,1)} %copy.36), channel_id=1, source_target_pairs={{0,255},{1,0},{2,1},{3,2},{4,3},{5,4},{6,5},{7,6},{8,7},{9,8},{10,... | collective-permute-start | bytes 3342344 | tf_op jit(solution)/shard_map/ppermute | solution.py:12
  30.9 7.3 %collective-permute-done = bf16[8,17,4096]{2,0,1:T(8,128)(2,1)} collective-permute-done((bf16[8,17,4096]{2,0,1:T(8,128)(2,1)}, bf16[8,17,4096]{2,0,1:T(8,128)(2,1)}, u32[]{:S(2)}, u32[]{:S(2)}) %collective-permute-start) | collective-permute-done | bytes 1114144 | tf_op jit(solution)/shard_map/ppermute | solution.py:12
  38.2 6.0 collective-permute-done.2
  44.2 7.3 %collective-permute-start.3 = (bf16[8,17,4096]{2,0,1:T(8,128)(2,1)}, bf16[8,17,4096]{2,0,1:T(8,128)(2,1)}, u32[]{:S(2)}, u32[]{:S(2)}) collective-permute-start(bf16[8,17,4096]{2,0,1:T(8,128)(2,1)} %collective-permute-done.2), channel_id=1, source_target_pairs={{0,255},{1,0},{2,1},{3,2},{4,3},{5,4},{6,5},{7,6},{8,7},{9,8},{10,... | collective-permute-start | bytes 3342344 | tf_op jit(solution)/shard_map/ppermute | solution.py:12
  51.6 358.2 %all-gather.2.cloned.1.call-done = f32[2048,128]{1,0:T(8,128)} async-done(((f32[8,128]{1,0:T(8,128)}), f32[2048,128]{1,0:T(8,128)}) %all-gather.2.cloned.1.call-update) | async-done | bytes 1048592 | tf_op jit(solution)/shard_map/all_gather | solution.py:70
  409.8 2.1 reduce_sum.39
  412.5 3.1 copy_dynamic-update-slice_fusion.3
  415.7 3.1 copy_dynamic-update-slice_fusion.2
  418.8 1.2 constant_dynamic-update-slice_fusion
  420.0 3.1 copy_dynamic-update-slice_fusion.1
  423.1 3.1 copy_dynamic-update-slice_fusion
  426.2 8.1 %reshape.37 = bf16[680,4096]{1,0:T(8,128)(2,1)} reshape(bf16[40,17,4096]{2,1,0:T(8,128)(2,1)} %copy_dynamic-update-slice_fusion) | data formatting | bytes 11141120 | tf_op jit(solution)/shard_map/reshape | solution.py:85
  434.3 16.5 %reshape_reshape.3 = bf16[680,64,64]{2,1,0:T(8,128)(2,1)} reshape(bf16[40,17,4096]{2,1,0:T(8,128)(2,1)} %copy_dynamic-update-slice_fusion) | data formatting | bytes 11141120 | tf_op jit(solution)/shard_map/reshape;reshape | solution.py:40
  450.8 19.3 %copy.42 = bf16[680,64,64]{0,2,1:T(8,128)(2,1)} copy(bf16[680,64,64]{1,2,0:T(8,128)(2,1)} %bitcast.18) | data formatting | bytes 11141120 | tf_op jit(solution)/shard_map/transpose | solution.py:41
  470.1 8.4 %copy.43 = bf16[680,4096]{1,0:T(8,128)(2,1)} copy(bf16[680,4096]{0,1:T(8,128)(2,1)} %bitcast.19) | data formatting | bytes 11141120 | tf_op jit(solution)/shard_map/reshape | solution.py:41
  478.5 51.6 %concatenate.11 = bf16[1361,4096]{1,0:T(8,128)(2,1)} concatenate(bf16[680,4096]{1,0:T(8,128)(2,1)} %reshape.37, bf16[1,4096]{1,0:T(2,128)(2,1)S(1)} %broadcast_in_dim.68, bf16[680,4096]{1,0:T(8,128)(2,1)} %copy.43), dimensions={0} | concatenate | bytes 22298624 | tf_op jit(solution)/shard_map/concatenate | solution.py:87
  530.1 13.7 %gather_fusion.1 = bf16[320,4096]{1,0:T(8,128)(2,1)} fusion(bf16[1361,4096]{1,0:T(8,128)(2,1)} %concatenate.11, s32[1024]{0:T(1024)S(1)} %get-tuple-element.14), kind=kCustom, calls=%fused_computation.1 | custom fusion | bytes 5244160 | tf_op jit(solution)/shard_map/gather | solution.py:88
  543.8 20.5 %gather_fusion = bf16[960,4096]{1,0:T(8,128)(2,1)} fusion(bf16[1361,4096]{1,0:T(8,128)(2,1)} %concatenate.11, s32[1024]{0:T(1024)S(1)} %get-tuple-element.15), kind=kCustom, calls=%fused_computation | custom fusion | bytes 15732480 | tf_op jit(solution)/shard_map/gather | solution.py:89
  564.4 8.4 %reshape.70 = bf16[8,40,64,64,1]{3,2,1,0,4:T(8,128)(2,1)} reshape(bf16[320,4096]{1,0:T(8,128)(2,1)} %gather_fusion.1) | data formatting | bytes 5242880 | tf_op jit(solution)/shard_map/reshape | solution.py:88
  572.7 22.0 %reshape.39 = bf16[40,24,64,64]{3,2,1,0:T(8,128)(2,1)} reshape(bf16[960,4096]{1,0:T(8,128)(2,1)} %gather_fusion) | data formatting | bytes 15728640 | tf_op jit(solution)/shard_map/reshape | solution.py:89
  594.7 22.3 %fusion.4 = f32[8,24,64,64]{2,3,0,1:T(8,128)} fusion(bf16[8,40,64,64,1]{3,2,1,0,4:T(8,128)(2,1)} %reshape.70, bf16[40,24,64,64]{3,2,1,0:T(8,128)(2,1)} %reshape.39), kind=kOutput, calls=%fused_computation.11 | convolution fusion | flops 4026531840 | bytes 13631488 | tf_op jit(solution)/shard_map/rjab,jkbc->rkac/dot_general | solution.py:90
  617.0 6.6 %copy.45 = f32[8,24,64,64]{3,2,1,0:T(8,128)} copy(f32[8,24,64,64]{2,3,0,1:T(8,128)} %fusion.4) | data formatting | bytes 6291456 | tf_op jit(solution)/shard_map/rjab,jkbc->rkac/transpose | solution.py:90
  623.6 5.9 reshape.41
  629.5 4.9 fusion.2
  634.4 2.7 copy.47
  (21 shorter events, 1.3 us)
Async XLA Ops:
  7.2 402.6 %all-gather.2.cloned.1.call-start = ((), (), s32[]{:S(2)}) async-start(), calls=%async_computation | async-start | bytes 1052672 | tf_op jit(solution)/shard_map/all_gather | solution.py:70
  9.8 6.7 %copy-start = (bf16[8,17,4096]{2,0,1:T(8,128)(2,1)S(1)}, bf16[8,17,4096]{2,0,1:T(8,128)(2,1)}, u32[]{:S(2)}) copy-start(bf16[8,17,4096]{2,0,1:T(8,128)(2,1)} %param.4) | copy-start | bytes 3342340
  14.8 23.5 %copy-start.1 = (s32[960]{0:T(1024)S(1)}, s32[960]{0:T(1024)}, u32[]{:S(2)}) copy-start(s32[960]{0:T(1024)} %constant.87) | copy-start | bytes 11524
  14.8 23.4 %copy-start.2 = (s32[320]{0:T(512)S(1)}, s32[320]{0:T(512)}, u32[]{:S(2)}) copy-start(s32[320]{0:T(512)} %constant.88) | copy-start | bytes 3844
  16.5 21.7 %collective-permute-start = (bf16[8,17,4096]{2,0,1:T(8,128)(2,1)}, bf16[8,17,4096]{2,0,1:T(8,128)(2,1)}, u32[]{:S(2)}, u32[]{:S(2)}) collective-permute-start(bf16[8,17,4096]{2,0,1:T(8,128)(2,1)} %copy.36), channel_id=1, source_target_pairs={{0,1},{1,2},{2,3},{3,4},{4,5},{5,6},{6,7},{7,8},{8,9},{9,10},{10,1... | collective-permute-start | bytes 3342344 | tf_op jit(solution)/shard_map/ppermute | solution.py:12
  22.6 21.6 %collective-permute-start.2 = (bf16[8,17,4096]{2,0,1:T(8,128)(2,1)}, bf16[8,17,4096]{2,0,1:T(8,128)(2,1)}, u32[]{:S(2)}, u32[]{:S(2)}) collective-permute-start(bf16[8,17,4096]{2,0,1:T(8,128)(2,1)} %copy.36), channel_id=1, source_target_pairs={{0,255},{1,0},{2,1},{3,2},{4,3},{5,4},{6,5},{7,6},{8,7},{9,8},{10,... | collective-permute-start | bytes 3342344 | tf_op jit(solution)/shard_map/ppermute | solution.py:12
  38.2 374.3 %collective-permute-start.1 = (bf16[8,17,4096]{2,0,1:T(8,128)(2,1)}, bf16[8,17,4096]{2,0,1:T(8,128)(2,1)}, u32[]{:S(2)}, u32[]{:S(2)}) collective-permute-start(bf16[8,17,4096]{2,0,1:T(8,128)(2,1)} %collective-permute-done), channel_id=1, source_target_pairs={{0,1},{1,2},{2,3},{3,4},{4,5},{5,6},{6,7},{7,8},{8,9},{9,10},{10,1... | collective-permute-start | bytes 3342344 | tf_op jit(solution)/shard_map/ppermute | solution.py:12
  44.2 378.8 %collective-permute-start.3 = (bf16[8,17,4096]{2,0,1:T(8,128)(2,1)}, bf16[8,17,4096]{2,0,1:T(8,128)(2,1)}, u32[]{:S(2)}, u32[]{:S(2)}) collective-permute-start(bf16[8,17,4096]{2,0,1:T(8,128)(2,1)} %collective-permute-done.2), channel_id=1, source_target_pairs={{0,255},{1,0},{2,1},{3,2},{4,3},{5,4},{6,5},{7,6},{8,7},{9,8},{10,... | collective-permute-start | bytes 3342344 | tf_op jit(solution)/shard_map/ppermute | solution.py:12
Sparse Core Ops, SparseCore 0:
  22.7 387.0 all-gather.1

commit v2 on v0

v2 whole, which is shorter than its diff:
```python
import math

import jax
import jax.numpy as jnp
import numpy as np
from jax import lax
from jax.sharding import PartitionSpec as P

AXES = ("row", "col")


def shifted(shard, by):
    length = lax.axis_size(AXES)
    return lax.ppermute(shard, AXES, [(i, (i + by) % length) for i in range(length)])


def butterfly_sum(value):
    length = lax.axis_size(AXES)
    step = 1
    while step < length:
        other = lax.ppermute(value, AXES, [(i, i ^ step) for i in range(length)])
        value = value + other
        step *= 2
    return value


def pad_slots(piece, before, after):
    return jnp.pad(piece, ((0, 0), (before, after), (0, 0), (0, 0)))


def body(upper_tiles, block_columns):
    rows_dev, slots, tile_size = upper_tiles.shape
    half = slots - 1
    block = math.isqrt(tile_size)
    devices = lax.axis_size(AXES)
    nblocks = rows_dev * devices
    window_rows = rows_dev + 2 * half
    span_cols = rows_dev + half
    first_row = lax.axis_index(AXES) * rows_dev
    local_rows = jnp.arange(rows_dev, dtype=jnp.int32)
    row_ids = first_row + local_rows
    slot_range = jnp.arange(slots, dtype=jnp.int32)
    listed = block_columns >= 0
    offsets_of = jnp.mod(block_columns - row_ids[:, None], nblocks)

    diag_own = upper_tiles[:, 0].astype(jnp.float32).reshape(rows_dev, block, block)
    own_trace = 2.0 * jnp.sum(jnp.diagonal(diag_own, axis1=1, axis2=2))
    weight = jnp.where(listed, jnp.where(slot_range[None, :] == 0, 1.0, 2.0), 0.0)
    squares = jnp.sum(jnp.square(upper_tiles.astype(jnp.float32)), axis=2)
    total = butterfly_sum(own_trace - jnp.sum(weight * squares))
    occupancy = (total / (nblocks * block)).astype(jnp.float32)

    tiles4 = upper_tiles.reshape(rows_dev, slots, block, block)
    pick_band = (listed[:, :, None] & (offsets_of[:, :, None] == slot_range[None, None, :])).astype(
        jnp.bfloat16
    )
    band = jnp.einsum(
        "rso,rspq->ropq", pick_band, tiles4, preferred_element_type=jnp.float32
    ).astype(jnp.bfloat16)

    cut = half - rows_dev + 1
    from_prev2 = shifted(band[:, cut:], 2)
    from_prev1 = shifted(band[:, 1:], 1)
    from_next1 = shifted(band[:, : slots - 1], -1)
    from_next2 = shifted(band[:, : slots - cut], -2)
    window = jnp.concatenate(
        [
            pad_slots(from_prev2, cut, 0),
            pad_slots(from_prev1, 1, 0),
            band,
            pad_slots(from_next1, 0, 1),
            pad_slots(from_next2, 0, cut),
        ],
        axis=0,
    )

    w_idx = lax.broadcasted_iota(jnp.int32, (window_rows, slots, 1, 1), 0)
    s_idx = lax.broadcasted_iota(jnp.int32, (window_rows, slots, 1, 1), 1)
    kept = jnp.where(w_idx + s_idx < window_rows, window, jnp.zeros((), window.dtype))
    padded = jnp.pad(kept, ((0, 0), (0, window_rows + 1 - slots), (0, 0), (0, 0)))
    flat = padded.reshape(window_rows * (window_rows + 1), block, block)
    upper = flat[: window_rows * window_rows].reshape(window_rows, window_rows, block, block)

    lower = jnp.transpose(upper, (1, 0, 3, 2))
    a_idx = lax.broadcasted_iota(jnp.int32, (span_cols, window_rows, 1, 1), 0) + half
    b_idx = lax.broadcasted_iota(jnp.int32, (span_cols, window_rows, 1, 1), 1)
    strip = upper[half:] + jnp.where(b_idx < a_idx, lower[half:], jnp.zeros((), lower.dtype))

    product = jnp.einsum(
        "abpq,cbrq->apcr", strip[:rows_dev], strip, preferred_element_type=jnp.float32
    )

    target = jnp.where(listed, offsets_of + local_rows[:, None], -1)
    pick_new = (target[:, :, None] == jnp.arange(span_cols, dtype=jnp.int32)[None, None, :]).astype(
        jnp.float32
    )
    picked = jnp.einsum(
        "rsc,rpcq->rspq",
        pick_new,
        product,
        precision=lax.Precision.HIGHEST,
        preferred_element_type=jnp.float32,
    ).reshape(rows_dev, slots, tile_size)
    new_tiles = jnp.where(listed[:, :, None], 2.0 * upper_tiles.astype(jnp.float32) - picked, 0.0)
    return (new_tiles, occupancy)


def solution(mesh):
    placed = (P(AXES, None, None), P(AXES, None))
    return jax.shard_map(
        body,
        mesh=mesh,
        in_specs=placed,
        out_specs=(P(AXES, None, None), P()),
        check_vma=False,
    )
```

time: 367 us -> 285 us (0.78)
  local copies, waits for them, and re-layouts: 201 us -> 110 us
  blocking collectives: 86.1 us -> 0 us
  waiting for transfers between devices: 21.2 us -> 67.6 us
  starting transfers between devices: 15.5 us -> 46.2 us
  other arithmetic: 2.86 us -> 19 us
  between operations: 3.83 us -> 7.71 us
    psum x1 -> x0, blocking collectives: 86.1 us -> none  [body(): lax.psum(own_trace - jnp.sum(jnp.diagonal(diag_product, axis1=1, axis2=2)...]
    concatenate x2 -> x1, local copies, waits for them, and re-layouts: 53.5 us -> 1.96 us  [body(): jnp.concatenate([pad_slots(from_prev2, cut, 0), pad_slots(from_prev1, 1,...]
    ppermute x4 -> x12, waiting for transfers between devices: 21.2 us -> 67.6 us  [the longest x8 67.6 us: butterfly_sum(): other = lax.ppermute(value, AXES, [(i, i ^ step) for i in range(length)])]
    slice x0 -> x4, local copies, waits for them, and re-layouts: none -> 36.6 us  [the longest x1 18.6 us: body(): flat[:window_rows * window_rows]]
    gather x4 -> x0, local copies, waits for them, and re-layouts: 35.4 us -> none  [the longest x1 20.8 us: body(): flat[jnp.asarray(right_np)].reshape(window_rows, span_cols, block, block)]
    ppermute x4 -> x12, starting transfers between devices: 15.5 us -> 46.2 us  [the longest x8 30.4 us: butterfly_sum(): other = lax.ppermute(value, AXES, [(i, i ^ step) for i in range(length)])]
    transpose x2 -> x0, local copies, waits for them, and re-layouts: 25.9 us -> none  [the longest x1 19.3 us: flip_tiles(): return jnp.swapaxes(shaped, -1, -2).reshape(tiles.shape)]
    another operation x1 -> x0, local copies, waits for them, and re-layouts: 16.5 us -> none  [flip_tiles(): shaped = tiles.reshape(tiles.shape[:-1] + (block, block))]
  transfers between devices with their start and end apart: 4 -> 12, of which waited for: 2 -> 7; matrix products, arithmetic and copies ran while one was open for 4% -> 6% of each run, Pallas kernels for 0% -> 0%
where the time goes in v2:
time: 285 us; the launch traced here: 281 us
  local copies, waits for them, and re-layouts  110 us (39%)
  waiting for transfers between devices  67.6 us (24%)
  starting transfers between devices  46.2 us (16%)
  matrix products  31.3 us (11%)
  other arithmetic  19 us (7%)
  between operations  7.71 us (3%)
    ppermute x8, waiting for transfers between devices, butterfly_sum(): other = lax.ppermute(value, AXES, [(i, i ^ step) for i in range(length)])  67.6 us
    reshape x1, local copies, waits for them, and re-layouts, body(): flat[:window_rows * window_rows]  35.2 us
    ppermute x8, starting transfers between devices, butterfly_sum(): other = lax.ppermute(value, AXES, [(i, i ^ step) for i in range(length)])  30.4 us
    slice x1, local copies, waits for them, and re-layouts, body(): flat[:window_rows * window_rows]  18.6 us
    dot_general x1, matrix products, body(): jnp.einsum('abpq,cbrq->apcr', strip[:rows_dev], strip, preferred_element_...  18.3 us
    ppermute x4, starting transfers between devices, shifted(): lax.ppermute(shard, AXES, [(i, (i + by) % length) for i in range(length)])  15.8 us
    slice x1, local copies, waits for them, and re-layouts, body(): upper[half:]  13.3 us
    add x1, other arithmetic, body(): upper[half:]  11.5 us
  transfers between devices with their start and end apart: 12, of which 7 were waited for; matrix products, arithmetic and copies ran while one was open for 6% of the time, Pallas kernels for 0%

profile of v2, /device:TPU:0, one launch (start us, length us, event | category | flops | bytes accessed | tf_op | source)
XLA Modules:
  0.0 281.4 jit_solution(4818722093517288709)
XLA Ops:
  0.6 1.6 fusion.15
  2.2 4.5 %reshape.63 = bf16[8,17,64,64]{3,2,0,1:T(8,128)(2,1)} reshape(bf16[8,17,4096]{2,0,1:T(8,128)(2,1)} %param.2) | data formatting | bytes 2228224 | tf_op jit(solution)/shard_map/reshape | solution.py:53
  8.3 3.6 %fusion.10 = bf16[8,17,64,64]{3,1,2,0:T(8,128)(2,1)S(1)} fusion(bf16[8,17,64,64]{3,2,0,1:T(8,128)(2,1)} %reshape.63, s32[8,17]{1,0:T(8,128)S(1)} %copy.28, pred[8,17]{1,0:T(8,128)(4,1)S(1)} %copy.27), kind=kOutput, calls=%fused_computation.18 | convolution fusion | flops 19501584 | bytes 2228904 | tf_op jit(solution)/shard_map/rso,rspq->ropq/dot_general | solution.py:57
  11.9 1.7 fusion.25
  13.6 3.1 %fusion.26 = (bf16[8,16,64,64]{3,1,2,0:T(8,128)(2,1)}, bf16[8,16,64,64]{3,1,2,0:T(8,128)(2,1)}) fusion(bf16[8,17,64,64]{3,1,2,0:T(8,128)(2,1)S(1)} %fusion.10), kind=kLoop, calls=%fused_computation.46 | loop fusion | bytes 4194304 | tf_op jit(solution)/shard_map/slice | solution.py:64
  16.7 8.2 %collective-permute-start.2 = (bf16[8,16,64,64]{3,1,2,0:T(8,128)(2,1)}, bf16[8,16,64,64]{3,1,2,0:T(8,128)(2,1)}, u32[]{:S(2)}, u32[]{:S(2)}) collective-permute-start(bf16[8,16,64,64]{3,1,2,0:T(8,128)(2,1)} %get-tuple-element.8), channel_id=1, source_target_pairs={{0,255},{1,0},{2,1},{3,2},{4,3},{5,4},{6,5},{7,6},{8,7},{9,8},{10,... | collective-permute-start | bytes 3145736 | tf_op jit(solution)/shard_map/ppermute | solution.py:14
  25.8 2.0 copy.34
  27.8 1.5 gather_fusion
  32.2 7.6 %collective-permute-start.3 = (bf16[8,8,64,64]{3,1,2,0:T(8,128)(2,1)}, bf16[8,8,64,64]{3,1,2,0:T(8,128)(2,1)}, u32[]{:S(2)}, u32[]{:S(2)}) collective-permute-start(bf16[8,8,64,64]{3,1,2,0:T(8,128)(2,1)} %get-tuple-element.6), channel_id=1, source_target_pairs={{0,254},{1,255},{2,0},{3,1},{4,2},{5,3},{6,4},{7,5},{8,6},{9,7},{1... | collective-permute-start | bytes 1572872 | tf_op jit(solution)/shard_map/ppermute | solution.py:14
  41.9 63.8 %collective-permute-done.5 = f32[]{:T(128)} collective-permute-done((f32[]{:T(128)}, f32[]{:T(128)}, u32[]{:S(2)}, u32[]{:S(2)}) %collective-permute-start.5) | collective-permute-done | bytes 36 | tf_op jit(solution)/shard_map/ppermute | solution.py:21
  106.2 3.0 %collective-permute-start.6 = (f32[]{:T(128)}, f32[]{:T(128)}, u32[]{:S(2)}, u32[]{:S(2)}) collective-permute-start(f32[]{:T(128)} %add.94), channel_id=1, source_target_pairs={{0,4},{1,5},{2,6},{3,7},{4,0},{5,1},{6,2},{7,3},{8,12},{9,13},{10,... | collective-permute-start | bytes 20 | tf_op jit(solution)/shard_map/ppermute | solution.py:21
  110.6 4.3 %collective-permute-start.7 = (f32[]{:T(128)}, f32[]{:T(128)}, u32[]{:S(2)}, u32[]{:S(2)}) collective-permute-start(f32[]{:T(128)} %add.95), channel_id=1, source_target_pairs={{0,8},{1,9},{2,10},{3,11},{4,12},{5,13},{6,14},{7,15},{8,0},{9,1},... | collective-permute-start | bytes 20 | tf_op jit(solution)/shard_map/ppermute | solution.py:21
  116.4 4.4 %collective-permute-start.8 = (f32[]{:T(128)}, f32[]{:T(128)}, u32[]{:S(2)}, u32[]{:S(2)}) collective-permute-start(f32[]{:T(128)} %add.96), channel_id=1, source_target_pairs={{0,16},{1,17},{2,18},{3,19},{4,20},{5,21},{6,22},{7,23},{8,24},{9,... | collective-permute-start | bytes 20 | tf_op jit(solution)/shard_map/ppermute | solution.py:21
  122.2 3.5 %collective-permute-start.9 = (f32[]{:T(128)}, f32[]{:T(128)}, u32[]{:S(2)}, u32[]{:S(2)}) collective-permute-start(f32[]{:T(128)} %add.97), channel_id=1, source_target_pairs={{0,32},{1,33},{2,34},{3,35},{4,36},{5,37},{6,38},{7,39},{8,40},{9,... | collective-permute-start | bytes 20 | tf_op jit(solution)/shard_map/ppermute | solution.py:21
  126.7 4.7 %collective-permute-start.10 = (f32[]{:T(128)}, f32[]{:T(128)}, u32[]{:S(2)}, u32[]{:S(2)}) collective-permute-start(f32[]{:T(128)} %add.98), channel_id=1, source_target_pairs={{0,64},{1,65},{2,66},{3,67},{4,68},{5,69},{6,70},{7,71},{8,72},{9,... | collective-permute-start | bytes 20 | tf_op jit(solution)/shard_map/ppermute | solution.py:21
  132.3 8.2 %collective-permute-start.11 = (f32[]{:T(128)}, f32[]{:T(128)}, u32[]{:S(2)}, u32[]{:S(2)}) collective-permute-start(f32[]{:T(128)} %add.99), channel_id=1, source_target_pairs={{0,128},{1,129},{2,130},{3,131},{4,132},{5,133},{6,134},{7,135},{8... | collective-permute-start | bytes 20 | tf_op jit(solution)/shard_map/ppermute | solution.py:21
  141.5 2.1 pad_dynamic-update-slice_fusion.3
  143.6 2.8 %pad_dynamic-update-slice_fusion.2 = bf16[40,17,64,64]{3,1,2,0:T(8,128)(2,1)S(1)} fusion(bf16[40,17,64,64]{3,1,2,0:T(8,128)(2,1)S(1)} %pad_dynamic-update-slice_fusion.3, bf16[8,16,64,64]{3,1,2,0:T(8,128)(2,1)} %collective-permute-done.1), kind=kLoop, calls=%fused_computation.13 | loop fusion | bytes 4194304
  147.2 2.4 pad_dynamic-update-slice_fusion.1
  149.6 2.0 pad_dynamic-update-slice_fusion
  151.6 1.9 broadcast_select_fusion
  153.5 2.6 copy.39
  156.1 9.5 %pad.24.clone = bf16[40,41,64,64]{3,2,1,0:T(8,128)(2,1)} pad(bf16[40,17,64,64]{3,2,1,0:T(8,128)(2,1)S(1)} %copy.39, bf16[]{:T(256)} %constant.50.clone.1), padding=0_0x0_24x0_0x0_0 | pad | bytes 19005442 | tf_op jit(solution)/shard_map/jit(_pad)/pad | solution.py:80
  165.6 13.3 %slice.47 = bf16[960,64,64]{2,1,0:T(8,128)(2,1)} slice(bf16[1640,64,64]{2,1,0:T(8,128)(2,1)} %bitcast.38), slice={[640:1600], [0:64], [0:64]} | slice | bytes 15728640 | tf_op jit(solution)/shard_map/slice | solution.py:87
  178.9 18.6 %slice.48 = bf16[1600,64,64]{2,1,0:T(8,128)(2,1)} slice(bf16[1640,64,64]{2,1,0:T(8,128)(2,1)} %bitcast.39), slice={[0:1600], [0:64], [0:64]} | slice | bytes 26214400 | tf_op jit(solution)/shard_map/slice | solution.py:82
  197.5 35.2 %copy.31 = bf16[40,40,64,64]{2,3,0,1:T(8,128)(2,1)} copy(bf16[40,40,64,64]{3,2,1,0:T(8,128)(2,1)} %bitcast.40) | data formatting | bytes 26214400 | tf_op jit(solution)/shard_map/reshape | solution.py:82
  232.8 11.5 %fusion = bf16[24,40,64,64]{3,2,1,0:T(8,128)(2,1)S(1)} fusion(bf16[24,40,64,64]{3,2,1,0:T(8,128)(2,1)} %bitcast.42, bf16[40,40,64,64]{3,2,1,0:T(8,128)(2,1)} %bitcast.41, pred[24,40]{1,0:T(8,128)(4,1)S(1)} %iota_compare_fusion.2), kind=kLoop, calls=%fused_computation.2 | loop fusion | flops 7864320 | bytes 23593920 | tf_op jit(solution)/shard_map/add | solution.py:87
  244.3 18.3 %fusion.7 = f32[8,64,24,64]{3,1,2,0:T(8,128)} fusion(bf16[24,40,64,64]{3,2,1,0:T(8,128)(2,1)S(1)} %fusion), kind=kOutput, calls=%fused_computation.17 | convolution fusion | flops 4026531840 | bytes 24117248 | tf_op jit(solution)/shard_map/abpq,cbrq->apcr/dot_general | solution.py:89
  262.6 9.3 %fusion.3 = f32[8,17,64,64]{3,1,2,0:T(8,128)S(1)} fusion(f32[8,64,24,64]{3,1,2,0:T(8,128)} %fusion.7, s32[8,17]{1,0:T(8,128)S(1)} %copy.26), kind=kOutput, calls=%fused_computation.6 | convolution fusion | flops 160435392 | bytes 5374496 | tf_op jit(solution)/shard_map/rsc,rpcq->rspq/dot_general | solution.py:97
  272.0 2.8 %copy.33 = f32[8,17,64,64]{3,2,0,1:T(8,128)} copy(f32[8,17,64,64]{3,1,2,0:T(8,128)S(1)} %fusion.3) | data formatting | bytes 4456448 | tf_op jit(solution)/shard_map/rsc,rpcq->rspq/dot_general | solution.py:97
  274.8 3.7 %reshape.66 = f32[8,17,4096]{2,0,1:T(8,128)S(1)} reshape(f32[8,17,64,64]{3,2,0,1:T(8,128)} %copy.33) | data formatting | bytes 4456448 | tf_op jit(solution)/shard_map/reshape | solution.py:103
  278.5 1.7 fusion.14
  (32 shorter events, 10.3 us)
Async XLA Ops:
  13.6 127.8 %collective-permute-start = (bf16[8,8,64,64]{3,1,2,0:T(8,128)(2,1)}, bf16[8,8,64,64]{3,1,2,0:T(8,128)(2,1)}, u32[]{:S(2)}, u32[]{:S(2)}) collective-permute-start(bf16[8,8,64,64]{3,1,2,0:T(8,128)(2,1)} %get-tuple-element.7), channel_id=1, source_target_pairs={{0,2},{1,3},{2,4},{3,5},{4,6},{5,7},{6,8},{7,9},{8,10},{9,11},{10,... | collective-permute-start | bytes 1572872 | tf_op jit(solution)/shard_map/ppermute | solution.py:14
  16.7 130.5 %collective-permute-start.2 = (bf16[8,16,64,64]{3,1,2,0:T(8,128)(2,1)}, bf16[8,16,64,64]{3,1,2,0:T(8,128)(2,1)}, u32[]{:S(2)}, u32[]{:S(2)}) collective-permute-start(bf16[8,16,64,64]{3,1,2,0:T(8,128)(2,1)} %get-tuple-element.8), channel_id=1, source_target_pairs={{0,255},{1,0},{2,1},{3,2},{4,3},{5,4},{6,5},{7,6},{8,7},{9,8},{10,... | collective-permute-start | bytes 3145736 | tf_op jit(solution)/shard_map/ppermute | solution.py:14
  24.9 118.6 %collective-permute-start.1 = (bf16[8,16,64,64]{3,1,2,0:T(8,128)(2,1)}, bf16[8,16,64,64]{3,1,2,0:T(8,128)(2,1)}, u32[]{:S(2)}, u32[]{:S(2)}) collective-permute-start(bf16[8,16,64,64]{3,1,2,0:T(8,128)(2,1)} %get-tuple-element.9), channel_id=1, source_target_pairs={{0,1},{1,2},{2,3},{3,4},{4,5},{5,6},{6,7},{7,8},{8,9},{9,10},{10,1... | collective-permute-start | bytes 3145736 | tf_op jit(solution)/shard_map/ppermute | solution.py:14
  31.2 8.8 %collective-permute-start.4 = (f32[]{:T(128)}, f32[]{:T(128)}, u32[]{:S(2)}, u32[]{:S(2)}) collective-permute-start(f32[]{:T(128)} %sub.17), channel_id=1, source_target_pairs={{0,1},{1,0},{2,3},{3,2},{4,5},{5,4},{6,7},{7,6},{8,9},{9,8},{10,11... | collective-permute-start | bytes 20 | tf_op jit(solution)/shard_map/ppermute | solution.py:21
  32.2 117.4 %collective-permute-start.3 = (bf16[8,8,64,64]{3,1,2,0:T(8,128)(2,1)}, bf16[8,8,64,64]{3,1,2,0:T(8,128)(2,1)}, u32[]{:S(2)}, u32[]{:S(2)}) collective-permute-start(bf16[8,8,64,64]{3,1,2,0:T(8,128)(2,1)} %get-tuple-element.6), channel_id=1, source_target_pairs={{0,254},{1,255},{2,0},{3,1},{4,2},{5,3},{6,4},{7,5},{8,6},{9,7},{1... | collective-permute-start | bytes 1572872 | tf_op jit(solution)/shard_map/ppermute | solution.py:14
  40.5 65.2 %collective-permute-start.5 = (f32[]{:T(128)}, f32[]{:T(128)}, u32[]{:S(2)}, u32[]{:S(2)}) collective-permute-start(f32[]{:T(128)} %add.93), channel_id=1, source_target_pairs={{0,2},{1,3},{2,0},{3,1},{4,6},{5,7},{6,4},{7,5},{8,10},{9,11},{10,... | collective-permute-start | bytes 20 | tf_op jit(solution)/shard_map/ppermute | solution.py:21
  106.2 3.8 %collective-permute-start.6 = (f32[]{:T(128)}, f32[]{:T(128)}, u32[]{:S(2)}, u32[]{:S(2)}) collective-permute-start(f32[]{:T(128)} %add.94), channel_id=1, source_target_pairs={{0,4},{1,5},{2,6},{3,7},{4,0},{5,1},{6,2},{7,3},{8,12},{9,13},{10,... | collective-permute-start | bytes 20 | tf_op jit(solution)/shard_map/ppermute | solution.py:21
  110.6 5.3 %collective-permute-start.7 = (f32[]{:T(128)}, f32[]{:T(128)}, u32[]{:S(2)}, u32[]{:S(2)}) collective-permute-start(f32[]{:T(128)} %add.95), channel_id=1, source_target_pairs={{0,8},{1,9},{2,10},{3,11},{4,12},{5,13},{6,14},{7,15},{8,0},{9,1},... | collective-permute-start | bytes 20 | tf_op jit(solution)/shard_map/ppermute | solution.py:21
  116.4 5.3 %collective-permute-start.8 = (f32[]{:T(128)}, f32[]{:T(128)}, u32[]{:S(2)}, u32[]{:S(2)}) collective-permute-start(f32[]{:T(128)} %add.96), channel_id=1, source_target_pairs={{0,16},{1,17},{2,18},{3,19},{4,20},{5,21},{6,22},{7,23},{8,24},{9,... | collective-permute-start | bytes 20 | tf_op jit(solution)/shard_map/ppermute | solution.py:21
  122.2 3.9 %collective-permute-start.9 = (f32[]{:T(128)}, f32[]{:T(128)}, u32[]{:S(2)}, u32[]{:S(2)}) collective-permute-start(f32[]{:T(128)} %add.97), channel_id=1, source_target_pairs={{0,32},{1,33},{2,34},{3,35},{4,36},{5,37},{6,38},{7,39},{8,40},{9,... | collective-permute-start | bytes 20 | tf_op jit(solution)/shard_map/ppermute | solution.py:21
  126.7 5.0 %collective-permute-start.10 = (f32[]{:T(128)}, f32[]{:T(128)}, u32[]{:S(2)}, u32[]{:S(2)}) collective-permute-start(f32[]{:T(128)} %add.98), channel_id=1, source_target_pairs={{0,64},{1,65},{2,66},{3,67},{4,68},{5,69},{6,70},{7,71},{8,72},{9,... | collective-permute-start | bytes 20 | tf_op jit(solution)/shard_map/ppermute | solution.py:21
  132.3 8.6 %collective-permute-start.11 = (f32[]{:T(128)}, f32[]{:T(128)}, u32[]{:S(2)}, u32[]{:S(2)}) collective-permute-start(f32[]{:T(128)} %add.99), channel_id=1, source_target_pairs={{0,128},{1,129},{2,130},{3,131},{4,132},{5,133},{6,134},{7,135},{8... | collective-permute-start | bytes 20 | tf_op jit(solution)/shard_map/ppermute | solution.py:21
  272.0 6.5 %copy-start = (bf16[8,17,4096]{2,0,1:T(8,128)(2,1)S(1)}, bf16[8,17,4096]{2,0,1:T(8,128)(2,1)}, u32[]{:S(2)}) copy-start(bf16[8,17,4096]{2,0,1:T(8,128)(2,1)} %param.2) | copy-start | bytes 3342340

commit v3 on v2

v3 whole, which is shorter than its diff:
```python
import functools
import math

import jax
import jax.numpy as jnp
from jax import lax
from jax.experimental import pallas as pl
from jax.experimental.pallas import tpu as pltpu
from jax.sharding import PartitionSpec as P

AXES = ("row", "col")
SUB, LANE = 32, 128


def shifted(shard, by):
    length = lax.axis_size(AXES)
    return lax.ppermute(shard, AXES, [(i, (i + by) % length) for i in range(length)])


def strip_kernel(rows_dev, half, block, cut,
                 sel_ref, lst_ref, tiles_ref, own_ref, p2_ref, p1_ref, n1_ref, n2_ref,
                 out_ref, strip_ref, band_out_ref):
    slots = half + 1
    window_rows = rows_dev + 2 * half
    span_cols = rows_dev + half

    def tile(w, s):
        if w < rows_dev:
            return p2_ref[w, s - cut] if s >= cut else None
        if w < 2 * rows_dev:
            return p1_ref[w - rows_dev, s - 1] if s >= 1 else None
        if w < half + rows_dev:
            return own_ref[w - half, s]
        if w < half + 2 * rows_dev:
            return n1_ref[w - half - rows_dev, s] if s < slots - 1 else None
        return n2_ref[w - half - 2 * rows_dev, s] if s < slots - cut else None

    strip_ref[...] = jnp.zeros(strip_ref.shape, strip_ref.dtype)
    for w in range(window_rows):
        for s in range(slots):
            flat = tile(w, s)
            if flat is None:
                continue
            t = flat.reshape(block, block)
            if w >= half and w + s < window_rows:
                strip_ref[pl.ds((w - half) * block, block), pl.ds((w + s) * block, block)] = t
            a = w + s - half
            if s >= 1 and 0 <= a < span_cols:
                strip_ref[pl.ds(a * block, block), pl.ds(w * block, block)] = t.T

    lhs = strip_ref[pl.ds(0, rows_dev * block), :]
    width = 256
    per = width // block
    for ct in range(span_cols * block // width):
        rhs = strip_ref[pl.ds(ct * width, width), :]
        res = lax.dot_general(lhs, rhs, (((1,), (1,)), ((), ())), preferred_element_type=jnp.float32)
        for r in range(rows_dev):
            for cc in range(per):
                o = ct * per + cc - r
                if 0 <= o <= half:
                    piece = res[r * block:(r + 1) * block, cc * block:(cc + 1) * block]
                    band_out_ref[r * slots + o] = piece.reshape(SUB, LANE)

    for i in range(rows_dev * slots):
        r, s = divmod(i, slots)
        value = 2.0 * tiles_ref[r, s].astype(jnp.float32) - band_out_ref[sel_ref[i]]
        out_ref[r, s] = jnp.where(lst_ref[i] > 0, value, 0.0)


def body(upper_tiles, block_columns):
    rows_dev, slots, tile_size = upper_tiles.shape
    half = slots - 1
    block = math.isqrt(tile_size)
    devices = lax.axis_size(AXES)
    nblocks = rows_dev * devices
    window_rows = rows_dev + 2 * half
    span_cols = rows_dev + half
    cut = half - rows_dev + 1
    first_row = lax.axis_index(AXES) * rows_dev
    local_rows = jnp.arange(rows_dev, dtype=jnp.int32)
    row_ids = first_row + local_rows
    slot_range = jnp.arange(slots, dtype=jnp.int32)
    listed = block_columns >= 0
    offsets_of = jnp.mod(block_columns - row_ids[:, None], nblocks)

    diag_own = upper_tiles[:, 0].astype(jnp.float32).reshape(rows_dev, block, block)
    own_trace = 2.0 * jnp.sum(jnp.diagonal(diag_own, axis1=1, axis2=2))
    weight = jnp.where(listed, jnp.where(slot_range[None, :] == 0, 1.0, 2.0), 0.0)
    squares = jnp.sum(jnp.square(upper_tiles.astype(jnp.float32)), axis=2)
    total = lax.psum(lax.psum(own_trace - jnp.sum(weight * squares), "col"), "row")
    occupancy = (total / (nblocks * block)).astype(jnp.float32)

    tiles = upper_tiles.reshape(rows_dev, slots, SUB, LANE)
    pick_band = (listed[:, :, None] & (offsets_of[:, :, None] == slot_range[None, None, :])).astype(
        jnp.bfloat16
    )
    band = jnp.einsum(
        "rso,rsmn->romn", pick_band, tiles, preferred_element_type=jnp.float32
    ).astype(jnp.bfloat16)

    from_prev2 = shifted(band[:, cut:], 2)
    from_prev1 = shifted(band[:, 1:], 1)
    from_next1 = shifted(band[:, : slots - 1], -1)
    from_next2 = shifted(band[:, : slots - cut], -2)

    sel = jnp.where(listed, local_rows[:, None] * slots + offsets_of, 0).reshape(-1).astype(jnp.int32)
    lst = listed.reshape(-1).astype(jnp.int32)
    vmem = pl.BlockSpec(memory_space=pltpu.VMEM)
    smem = pl.BlockSpec(memory_space=pltpu.SMEM)
    flops = 2 * rows_dev * block * window_rows * block * span_cols * block
    new_tiles = pl.pallas_call(
        functools.partial(strip_kernel, rows_dev, half, block, cut),
        out_shape=jax.ShapeDtypeStruct((rows_dev, slots, SUB, LANE), jnp.float32),
        in_specs=[smem, smem] + [vmem] * 6,
        out_specs=vmem,
        scratch_shapes=[
            pltpu.VMEM((span_cols * block, window_rows * block), jnp.bfloat16),
            pltpu.VMEM((rows_dev * slots, SUB, LANE), jnp.float32),
        ],
        compiler_params=pltpu.CompilerParams(vmem_limit_bytes=48 * 1024 * 1024),
        cost_estimate=pl.CostEstimate(flops=flops, bytes_accessed=8 * 1024 * 1024, transcendentals=0),
    )(sel, lst, tiles, band, from_prev2, from_prev1, from_next1, from_next2)
    return (new_tiles.reshape(rows_dev, slots, tile_size), occupancy)


def solution(mesh):
    placed = (P(AXES, None, None), P(AXES, None))
    return jax.shard_map(
        body,
        mesh=mesh,
        in_specs=placed,
        out_specs=(P(AXES, None, None), P()),
        check_vma=False,
    )
```

time: 285 us -> 319 us (1.12)
  blocking collectives: 0 us -> 220 us
  local copies, waits for them, and re-layouts: 110 us -> 13.2 us
  waiting for transfers between devices: 67.6 us -> 0.01 us
  Pallas kernels: 0 us -> 62.8 us
  starting transfers between devices: 46.2 us -> 10.3 us
  matrix products: 31.3 us -> 1.05 us
  other arithmetic: 19 us -> 2.87 us
  between operations: 7.71 us -> 4.03 us
    psum x0 -> x2, blocking collectives: none -> 220 us  [the longest x1 189 us: body(): lax.psum(lax.psum(own_trace - jnp.sum(weight * squares), 'col'), 'row')]
    ppermute x8 -> x0, waiting for transfers between devices: 67.6 us -> none  [butterfly_sum(): other = lax.ppermute(value, AXES, [(i, i ^ step) for i in range(length)])]
    pallas_call x0 -> x1, Pallas kernels: none -> 62.8 us  [body(): pl.pallas_call(functools.partial(strip_kernel, rows_dev, half, block, cut...]
    reshape x3, local copies, waits for them, and re-layouts: 43.4 us -> 3.28 us  [the longest x1 1.76 us: body(): return (new_tiles.reshape(rows_dev, slots, tile_size), occupancy)]
    slice x2 -> x0, local copies, waits for them, and re-layouts: 31.9 us -> none  [the longest x1 18.6 us: body(): flat[:window_rows * window_rows]]
    ppermute x8 -> x0, starting transfers between devices: 30.4 us -> none  [butterfly_sum(): other = lax.ppermute(value, AXES, [(i, i ^ step) for i in range(length)])]
    dot_general x3 -> x1, matrix products: 31.3 us -> 1.05 us  [body(): jnp.einsum('rso,rsmn->romn', pick_band, tiles, preferred_element_type=jnp...]
    add x2 -> x0, other arithmetic: 11.5 us -> none  [the longest x1 11.5 us: body(): upper[half:]]
  transfers between devices with their start and end apart: 12 -> 4, of which waited for: 7 -> 0; matrix products, arithmetic and copies ran while one was open for 6% -> 2% of each run, Pallas kernels for 0% -> 0%
where the time goes in v3:
time: 319 us; the launch traced here: 315 us
  blocking collectives  220 us (69%)
  Pallas kernels  62.8 us (20%)
  local copies, waits for them, and re-layouts  13.2 us (4%)
  starting transfers between devices  10.3 us (3%)
  between operations  4.03 us (1%)
    psum x1, blocking collectives, body(): lax.psum(lax.psum(own_trace - jnp.sum(weight * squares), 'col'), 'row')  189 us
    pallas_call x1, Pallas kernels, body(): pl.pallas_call(functools.partial(strip_kernel, rows_dev, half, block, cut...  62.8 us
    psum x1, blocking collectives, body(): lax.psum(own_trace - jnp.sum(weight * squares), 'col')  31.1 us
    ppermute x4, starting transfers between devices, shifted(): lax.ppermute(shard, AXES, [(i, (i + by) % length) for i in range(length)])  10.3 us
  transfers between devices with their start and end apart: 4, of which 0 were waited for; matrix products, arithmetic and copies ran while one was open for 2% of the time, Pallas kernels for 0%

profile of v3, /device:TPU:0, one launch (start us, length us, event | category | flops | bytes accessed | tf_op | source)
XLA Modules:
  0.0 314.6 jit_solution(2444918766862655282)
XLA Ops:
  0.6 0.0 copy-start.1
  0.7 0.9 copy.23
  1.5 1.6 multiply_reduce_fusion
  3.1 0.7 multiply_reduce_fusion.1
  3.8 0.1 copy.27
  3.9 0.1 copy.28
  3.9 0.2 copy.41
  4.2 1.1 fusion
  5.3 0.2 copy.40.own_ref
  5.5 1.7 fusion.9
  7.2 8.2 %collective-permute-start.2 = (bf16[8,16,32,128]{3,2,1,0:T(8,128)(2,1)}, bf16[8,16,32,128]{3,2,1,0:T(8,128)(2,1)S(1)}, u32[]{:S(2)}, u32[]{:S(2)}) collective-permute-start(bf16[8,16,32,128]{3,2,1,0:T(8,128)(2,1)} %get-tuple-element.10), channel_id=1, source_target_pairs={{0,255},{1,0},{2,1},{3,2},{4,3},{5,4},{6,5},{7,6},{8,7},{9,8},{10,... | collective-permute-start | bytes 3145736 | tf_op jit(solution)/shard_map/ppermute | solution.py:17
  15.4 0.0 collective-permute-start.1
  15.4 1.1 fusion.8
  16.5 1.1 collective-permute-start.3
  17.6 1.0 collective-permute-start
  18.6 1.9 copy.33
  20.5 1.6 gather_fusion
  22.1 0.6 reduce_sum.27
  24.0 31.1 %psum.14 = f32[]{:T(128)} all-reduce(f32[]{:T(128)S(6)} %sub.13), channel_id=1, replica_groups=mesh['row'=64,'col'=4] {'col'}, use_global_device_ids=true, to_apply=%region_3.4 | all-reduce | flops 1 | bytes 8 | tf_op jit(solution)/shard_map/psum | solution.py:90
  55.1 189.3 %psum.15 = f32[]{:T(128)} all-reduce(f32[]{:T(128)} %psum.14), channel_id=1, replica_groups=mesh['row'=64,'col'=4] {'row'}, use_global_device_ids=true, to_apply=%region_4.5 | all-reduce | flops 1 | bytes 8 | tf_op jit(solution)/shard_map/psum | solution.py:90
  244.4 1.4 copy.31.tiles_ref
  245.8 0.1 copy.25
  245.9 0.1 reshape.38.sel_ref
  246.0 0.1 copy.26
  246.0 0.1 reshape.41.lst_ref
  246.8 0.0 collective-permute-done.3.n2_ref
  246.8 0.0 collective-permute-done.p2_ref
  246.8 0.0 collective-permute-done.2.n1_ref
  246.8 0.0 collective-permute-done.1.p1_ref
  246.8 62.8 %shard_map.41 = f32[8,17,32,128]{3,2,1,0:T(8,128)} custom-call(s32[136]{0:T(256)S(1)} %reshape.38.sel_ref, s32[136]{0:T(256)S(1)} %reshape.41.lst_ref, bf16[8,17,32,128]{3,2,1,0:T(8,128)(2,1)S(1)} %copy.31.tiles_ref, bf16[8,17,32,128]{3,2,1,0:T(8,128)(2,1)S(1)} %copy.40.own_ref, bf16[8,8,32,128]{3,2,1,0:T(8,128)(2,1)} %collective-permute-done.p2_ref, ...), custom_call_target="tpu_custom_call" | custom-call | flops 4026531840 | bytes 8388608 | tf_op jit(solution)/shard_map/pallas_call | solution.py:111
  309.7 1.9 copy.32
  311.5 1.8 reshape.40
  (9 shorter events, 0.0 us)
Async XLA Ops:
  0.6 3.3 %copy-start.1 = (bf16[8,17,4096]{2,0,1:T(8,128)(2,1)S(1)}, bf16[8,17,4096]{2,0,1:T(8,128)(2,1)}, u32[]{:S(2)}) copy-start(bf16[8,17,4096]{2,0,1:T(8,128)(2,1)} %param.2) | copy-start | bytes 3342340
  4.2 1.1 copy-start
  7.2 239.6 %collective-permute-start.2 = (bf16[8,16,32,128]{3,2,1,0:T(8,128)(2,1)}, bf16[8,16,32,128]{3,2,1,0:T(8,128)(2,1)S(1)}, u32[]{:S(2)}, u32[]{:S(2)}) collective-permute-start(bf16[8,16,32,128]{3,2,1,0:T(8,128)(2,1)} %get-tuple-element.10), channel_id=1, source_target_pairs={{0,255},{1,0},{2,1},{3,2},{4,3},{5,4},{6,5},{7,6},{8,7},{9,8},{10,... | collective-permute-start | bytes 3145736 | tf_op jit(solution)/shard_map/ppermute | solution.py:17
  15.4 231.4 %collective-permute-start.1 = (bf16[8,16,32,128]{3,2,1,0:T(8,128)(2,1)}, bf16[8,16,32,128]{3,2,1,0:T(8,128)(2,1)}, u32[]{:S(2)}, u32[]{:S(2)}) collective-permute-start(bf16[8,16,32,128]{3,2,1,0:T(8,128)(2,1)} %get-tuple-element.11), channel_id=1, source_target_pairs={{0,1},{1,2},{2,3},{3,4},{4,5},{5,6},{6,7},{7,8},{8,9},{9,10},{10,1... | collective-permute-start | bytes 3145736 | tf_op jit(solution)/shard_map/ppermute | solution.py:17
  16.5 230.2 %collective-permute-start.3 = (bf16[8,8,32,128]{3,2,1,0:T(8,128)(2,1)}, bf16[8,8,32,128]{3,2,1,0:T(8,128)(2,1)}, u32[]{:S(2)}, u32[]{:S(2)}) collective-permute-start(bf16[8,8,32,128]{3,2,1,0:T(8,128)(2,1)} %get-tuple-element.8), channel_id=1, source_target_pairs={{0,254},{1,255},{2,0},{3,1},{4,2},{5,3},{6,4},{7,5},{8,6},{9,7},{1... | collective-permute-start | bytes 1572872 | tf_op jit(solution)/shard_map/ppermute | solution.py:17
  17.6 229.2 %collective-permute-start = (bf16[8,8,32,128]{3,2,1,0:T(8,128)(2,1)}, bf16[8,8,32,128]{3,2,1,0:T(8,128)(2,1)}, u32[]{:S(2)}, u32[]{:S(2)}) collective-permute-start(bf16[8,8,32,128]{3,2,1,0:T(8,128)(2,1)} %get-tuple-element.9), channel_id=1, source_target_pairs={{0,2},{1,3},{2,4},{3,5},{4,6},{5,7},{6,8},{7,9},{8,10},{9,11},{10,... | collective-permute-start | bytes 1572872 | tf_op jit(solution)/shard_map/ppermute | solution.py:17

commit v4 on v3

v4 whole, which is shorter than its diff:
```python
import functools
import math

import jax
import jax.numpy as jnp
from jax import lax
from jax.experimental import pallas as pl
from jax.experimental.pallas import tpu as pltpu
from jax.sharding import PartitionSpec as P

AXES = ("row", "col")
SUB, LANE = 32, 128


def shifted(shard, by):
    length = lax.axis_size(AXES)
    return lax.ppermute(shard, AXES, [(i, (i + by) % length) for i in range(length)])


def strip_kernel(rows_dev, half, block, sources,
                 sel_ref, lst_ref, tiles_ref, own_ref, p2_ref, p1_ref, n1_ref, n2_ref,
                 out_ref, strip_ref, band_out_ref):
    slots = half + 1
    window_rows = rows_dev + 2 * half
    span_cols = rows_dev + half
    refs = {"p2": p2_ref, "p1": p1_ref, "own": own_ref, "n1": n1_ref, "n2": n2_ref}

    strip_ref[...] = jnp.zeros(strip_ref.shape, strip_ref.dtype)
    for w in range(window_rows):
        name, first, count = sources[w // rows_dev]
        src = refs[name]
        r = w % rows_dev
        if w >= half:
            length = min(count, window_rows - w - first)
            strip_ref[pl.ds((w - half) * block, block), pl.ds((w + first) * block, length * block)] = (
                src[r, :, pl.ds(0, length * block)]
            )
        s_lo = max(1, first, half - w)
        s_hi = min(first + count - 1, window_rows - 1 - w)
        if s_hi >= s_lo:
            n = s_hi - s_lo + 1
            chunk = src[r, :, pl.ds((s_lo - first) * block, n * block)]
            strip_ref[pl.ds((w + s_lo - half) * block, n * block), pl.ds(w * block, block)] = chunk.T

    lhs = strip_ref[pl.ds(0, rows_dev * block), :]
    width = 256
    per = width // block
    for ct in range(span_cols * block // width):
        rhs = strip_ref[pl.ds(ct * width, width), :]
        res = lax.dot_general(lhs, rhs, (((1,), (1,)), ((), ())), preferred_element_type=jnp.float32)
        for r in range(rows_dev):
            for cc in range(per):
                o = ct * per + cc - r
                if 0 <= o <= half:
                    band_out_ref[r * slots + o] = res[r * block:(r + 1) * block, cc * block:(cc + 1) * block]

    for i in range(rows_dev * slots):
        r, s = divmod(i, slots)
        value = 2.0 * tiles_ref[r, s].astype(jnp.float32) - band_out_ref[sel_ref[i]]
        out_ref[r, s] = jnp.where(lst_ref[i] > 0, value, 0.0)


def body(upper_tiles, block_columns):
    rows_dev, slots, tile_size = upper_tiles.shape
    half = slots - 1
    block = math.isqrt(tile_size)
    devices = lax.axis_size(AXES)
    nblocks = rows_dev * devices
    window_rows = rows_dev + 2 * half
    span_cols = rows_dev + half
    cut = half - rows_dev + 1
    first_row = lax.axis_index(AXES) * rows_dev
    local_rows = jnp.arange(rows_dev, dtype=jnp.int32)
    row_ids = first_row + local_rows
    slot_range = jnp.arange(slots, dtype=jnp.int32)
    listed = block_columns >= 0
    offsets_of = jnp.mod(block_columns - row_ids[:, None], nblocks)

    diag_own = upper_tiles[:, 0].astype(jnp.float32).reshape(rows_dev, block, block)
    own_trace = 2.0 * jnp.sum(jnp.diagonal(diag_own, axis1=1, axis2=2))
    weight = jnp.where(listed, jnp.where(slot_range[None, :] == 0, 1.0, 2.0), 0.0)
    squares = jnp.sum(jnp.square(upper_tiles.astype(jnp.float32)), axis=2)
    total = lax.psum(lax.psum(own_trace - jnp.sum(weight * squares), "col"), "row")
    occupancy = (total / (nblocks * block)).astype(jnp.float32)

    tiles = upper_tiles.reshape(rows_dev, slots, block, block)
    pick_band = (listed[:, :, None] & (offsets_of[:, :, None] == slot_range[None, None, :])).astype(
        jnp.bfloat16
    )
    strips = jnp.einsum(
        "rso,rspq->rpoq", pick_band, tiles, preferred_element_type=jnp.float32
    ).astype(jnp.bfloat16).reshape(rows_dev, block, slots * block)
    strips = jnp.pad(strips, ((0, 0), (0, 0), (0, block)))
    occupancy, strips = lax.optimization_barrier((occupancy, strips))

    from_prev2 = shifted(strips[:, :, cut * block : slots * block], 2)
    from_prev1 = shifted(strips[:, :, block : slots * block], 1)
    from_next1 = shifted(strips[:, :, : (slots - 1) * block], -1)
    from_next2 = shifted(strips[:, :, : (slots - cut) * block], -2)
    sources = (("p2", cut, slots - cut), ("p1", 1, slots - 1), ("own", 0, slots),
               ("n1", 0, slots - 1), ("n2", 0, slots - cut))

    sel = jnp.where(listed, local_rows[:, None] * slots + offsets_of, 0).reshape(-1).astype(jnp.int32)
    lst = listed.reshape(-1).astype(jnp.int32)
    vmem = pl.BlockSpec(memory_space=pltpu.VMEM)
    smem = pl.BlockSpec(memory_space=pltpu.SMEM)
    flops = 2 * rows_dev * block * window_rows * block * span_cols * block
    new_tiles = pl.pallas_call(
        functools.partial(strip_kernel, rows_dev, half, block, sources),
        out_shape=jax.ShapeDtypeStruct((rows_dev, slots, block, block), jnp.float32),
        in_specs=[smem, smem] + [vmem] * 6,
        out_specs=vmem,
        scratch_shapes=[
            pltpu.VMEM((span_cols * block, window_rows * block), jnp.bfloat16),
            pltpu.VMEM((rows_dev * slots, block, block), jnp.float32),
        ],
        compiler_params=pltpu.CompilerParams(vmem_limit_bytes=48 * 1024 * 1024),
        cost_estimate=pl.CostEstimate(flops=flops, bytes_accessed=8 * 1024 * 1024, transcendentals=0),
    )(sel, lst, tiles, strips, from_prev2, from_prev1, from_next1, from_next2)
    return (new_tiles.reshape(rows_dev, slots, tile_size), occupancy)


def solution(mesh):
    placed = (P(AXES, None, None), P(AXES, None))
    return jax.shard_map(
        body,
        mesh=mesh,
        in_specs=placed,
        out_specs=(P(AXES, None, None), P()),
        check_vma=False,
    )
```

time: 319 us -> 289 us (0.906)
  the two profiles are of different devices: /device:TPU:0 before, /device:TPU:9 now
where the time goes in v4:
time: 289 us
  blocking collectives  160 us (55%)
  waiting for transfers between devices  42.9 us (15%)
  starting transfers between devices  35.7 us (12%)
  local copies, waits for them, and re-layouts  26.5 us (9%)
  Pallas kernels  12.8 us (4%)
  between operations  3.83 us (1%)
  other arithmetic  3.72 us (1%)
  matrix products  3.66 us (1%)
    psum x1, blocking collectives, body(): lax.psum(lax.psum(own_trace - jnp.sum(weight * squares), 'col'), 'row')  154 us
    ppermute x4, waiting for transfers between devices, shifted(): lax.ppermute(shard, AXES, [(i, (i + by) % length) for i in range(length)])  42.9 us
    ppermute x4, starting transfers between devices, shifted(): lax.ppermute(shard, AXES, [(i, (i + by) % length) for i in range(length)])  35.7 us
    pallas_call x1, Pallas kernels, body(): pl.pallas_call(functools.partial(strip_kernel, rows_dev, half, block, sou...  12.8 us
    reshape x2, local copies, waits for them, and re-layouts, body(): return (new_tiles.reshape(rows_dev, slots, tile_size), occupancy)  6.36 us
    psum x1, blocking collectives, body(): lax.psum(own_trace - jnp.sum(weight * squares), 'col')  6.17 us
  transfers between devices with their start and end apart: 4, of which 2 were waited for; matrix products, arithmetic and copies ran while one was open for 1% of the time, Pallas kernels for 0%

profile of v4, /device:TPU:9, one launch (start us, length us, event | category | flops | bytes accessed | tf_op | source)
XLA Modules:
  0.0 288.9 jit_solution(4072657461663091316)
XLA Ops:
  0.7 1.6 multiply_reduce_fusion
  2.2 0.8 slice_convert_fusion
  3.1 3.4 %reshape.42 = bf16[8,17,64,64]{3,2,0,1:T(8,128)(2,1)S(1)} reshape(bf16[8,17,4096]{2,0,1:T(8,128)(2,1)} %param.2) | data formatting | bytes 2228224 | tf_op jit(solution)/shard_map/reshape | solution.py:86
  6.5 0.0 copy-start
  6.5 0.1 copy.24
  6.6 2.0 copy.28
  8.6 1.5 gather_fusion
  10.1 0.6 reduce_sum.27
  11.3 0.7 multiply_reduce_fusion.1
  12.7 0.1 copy.29
  12.8 6.2 %psum.14 = f32[]{:T(128)} all-reduce(f32[]{:T(128)S(6)} %sub.13), channel_id=1, replica_groups=mesh['row'=64,'col'=4] {'col'}, use_global_device_ids=true, to_apply=%region_3.4 | all-reduce | flops 1 | bytes 8 | tf_op jit(solution)/shard_map/psum | solution.py:83
  18.9 0.1 copy.30
  19.0 153.6 %psum.15 = f32[]{:T(128)} all-reduce(f32[]{:T(128)} %psum.14), channel_id=1, replica_groups=mesh['row'=64,'col'=4] {'row'}, use_global_device_ids=true, to_apply=%region_4.5 | all-reduce | flops 1 | bytes 8 | tf_op jit(solution)/shard_map/psum | solution.py:83
  172.7 3.7 %convert_bitcast_fusion = bf16[8,64,17,64]{3,2,1,0:T(8,128)(2,1)} fusion(bf16[8,17,64,64]{3,2,0,1:T(8,128)(2,1)S(1)} %reshape.42, s32[8,17]{1,0:T(8,128)S(1)} %copy.30, pred[8,17]{1,0:T(8,128)(4,1)S(1)} %copy.29), kind=kOutput, calls=%fused_computation.3 | convolution fusion | flops 19501584 | bytes 2228904 | tf_op jit(solution)/shard_map/rso,rspq->rpoq/dot_general | solution.py:90
  176.3 4.6 %copy.32 = bf16[8,64,17,64]{1,3,2,0:T(8,128)(2,1)} copy(bf16[8,64,17,64]{3,2,1,0:T(8,128)(2,1)} %convert_bitcast_fusion) | data formatting | bytes 2228224 | tf_op jit(solution)/shard_map/convert_element_type | solution.py:92
  180.9 2.8 copy.33
  184.4 0.1 pad.4.own_ref
  184.5 0.0 copy-start.1
  184.5 2.1 fusion.11
  186.6 29.2 %collective-permute-start.2 = (bf16[8,64,1024]{2,1,0:T(8,128)(2,1)}, bf16[8,64,1024]{2,1,0:T(8,128)(2,1)S(1)}, u32[]{:S(2)}, u32[]{:S(2)}) collective-permute-start(bf16[8,64,1024]{2,1,0:T(8,128)(2,1)} %get-tuple-element.14), channel_id=1, source_target_pairs={{0,255},{1,0},{2,1},{3,2},{4,3},{5,4},{6,5},{7,6},{8,7},{9,8},{10,... | collective-permute-start | bytes 3145736 | tf_op jit(solution)/shard_map/ppermute | solution.py:17
  215.8 1.2 fusion.10
  217.0 6.5 %collective-permute-start.3 = (bf16[8,64,512]{2,1,0:T(8,128)(2,1)}, bf16[8,64,512]{2,1,0:T(8,128)(2,1)}, u32[]{:S(2)}, u32[]{:S(2)}) collective-permute-start(bf16[8,64,512]{2,1,0:T(8,128)(2,1)} %get-tuple-element.12), channel_id=1, source_target_pairs={{0,254},{1,255},{2,0},{3,1},{4,2},{5,3},{6,4},{7,5},{8,6},{9,7},{1... | collective-permute-start | bytes 1572872 | tf_op jit(solution)/shard_map/ppermute | solution.py:17
  223.5 1.8 copy.34.tiles_ref
  225.3 0.1 copy.26
  225.4 0.1 reshape.41.sel_ref
  225.5 0.1 copy.27
  225.6 0.1 reshape.45.lst_ref
  225.6 27.2 %collective-permute-done.3.n2_ref = bf16[8,64,512]{2,1,0:T(8,128)(2,1)} collective-permute-done((bf16[8,64,512]{2,1,0:T(8,128)(2,1)}, bf16[8,64,512]{2,1,0:T(8,128)(2,1)}, u32[]{:S(2)}, u32[]{:S(2)}) %collective-permute-start.3) | collective-permute-done | bytes 524320 | tf_op jit(solution)/shard_map/ppermute | solution.py:17
  252.9 15.7 %collective-permute-done.p2_ref = bf16[8,64,512]{2,1,0:T(8,128)(2,1)} collective-permute-done((bf16[8,64,512]{2,1,0:T(8,128)(2,1)}, bf16[8,64,512]{2,1,0:T(8,128)(2,1)}, u32[]{:S(2)}, u32[]{:S(2)}) %collective-permute-start) | collective-permute-done | bytes 524320 | tf_op jit(solution)/shard_map/ppermute | solution.py:17
  268.6 12.8 %shard_map.41 = f32[8,17,64,64]{3,2,1,0:T(8,128)} custom-call(s32[136]{0:T(256)S(1)} %reshape.41.sel_ref, s32[136]{0:T(256)S(1)} %reshape.45.lst_ref, bf16[8,17,64,64]{3,2,1,0:T(8,128)(2,1)} %copy.34.tiles_ref, bf16[8,64,1152]{2,1,0:T(8,128)(2,1)S(1)} %pad.4.own_ref, bf16[8,64,512]{2,1,0:T(8,128)(2,1)} %collective-permute-done.p2_ref, ...), custom_call_target="tpu_custom_call" | custom-call | flops 4026531840 | bytes 8388608 | tf_op jit(solution)/shard_map/pallas_call | solution.py:108
  281.4 3.7 %reshape.54 = f32[8,17,4096]{2,1,0:T(8,128)S(1)} reshape(f32[8,17,64,64]{3,2,1,0:T(8,128)} %shard_map.41) | data formatting | bytes 4456448 | tf_op jit(solution)/shard_map/reshape | solution.py:120
  285.2 2.7 copy.37
  (13 shorter events, 0.1 us)
Async XLA Ops:
  0.7 5.9 %copy-start.2 = (s32[8,17]{1,0:T(8,128)S(1)}, s32[8,17]{1,0:T(8,128)}, u32[]{:S(2)}) copy-start(s32[8,17]{1,0:T(8,128)} %param.3) | copy-start | bytes 1636
  6.5 169.8 %copy-start = (bf16[8,17,64,64]{3,2,0,1:T(8,128)(2,1)}, bf16[8,17,64,64]{3,2,0,1:T(8,128)(2,1)S(1)}, u32[]{:S(2)}) copy-start(bf16[8,17,64,64]{3,2,0,1:T(8,128)(2,1)S(1)} %reshape.42) | copy-start | bytes 3342340
  184.5 39.0 %copy-start.1 = (bf16[8,17,64,64]{3,2,0,1:T(8,128)(2,1)S(1)}, bf16[8,17,64,64]{3,2,0,1:T(8,128)(2,1)}, u32[]{:S(2)}) copy-start(bf16[8,17,64,64]{3,2,0,1:T(8,128)(2,1)} %copy-done) | copy-start | bytes 3342340
  186.6 82.0 %collective-permute-start.2 = (bf16[8,64,1024]{2,1,0:T(8,128)(2,1)}, bf16[8,64,1024]{2,1,0:T(8,128)(2,1)S(1)}, u32[]{:S(2)}, u32[]{:S(2)}) collective-permute-start(bf16[8,64,1024]{2,1,0:T(8,128)(2,1)} %get-tuple-element.14), channel_id=1, source_target_pairs={{0,255},{1,0},{2,1},{3,2},{4,3},{5,4},{6,5},{7,6},{8,7},{9,8},{10,... | collective-permute-start | bytes 3145736 | tf_op jit(solution)/shard_map/ppermute | solution.py:17
  215.8 52.8 %collective-permute-start.1 = (bf16[8,64,1024]{2,1,0:T(8,128)(2,1)}, bf16[8,64,1024]{2,1,0:T(8,128)(2,1)S(1)}, u32[]{:S(2)}, u32[]{:S(2)}) collective-permute-start(bf16[8,64,1024]{2,1,0:T(8,128)(2,1)} %get-tuple-element.15), channel_id=1, source_target_pairs={{0,1},{1,2},{2,3},{3,4},{4,5},{5,6},{6,7},{7,8},{8,9},{9,10},{10,1... | collective-permute-start | bytes 3145736 | tf_op jit(solution)/shard_map/ppermute | solution.py:17
  217.0 35.9 %collective-permute-start.3 = (bf16[8,64,512]{2,1,0:T(8,128)(2,1)}, bf16[8,64,512]{2,1,0:T(8,128)(2,1)}, u32[]{:S(2)}, u32[]{:S(2)}) collective-permute-start(bf16[8,64,512]{2,1,0:T(8,128)(2,1)} %get-tuple-element.12), channel_id=1, source_target_pairs={{0,254},{1,255},{2,0},{3,1},{4,2},{5,3},{6,4},{7,5},{8,6},{9,7},{1... | collective-permute-start | bytes 1572872 | tf_op jit(solution)/shard_map/ppermute | solution.py:17
  223.5 45.1 %collective-permute-start = (bf16[8,64,512]{2,1,0:T(8,128)(2,1)}, bf16[8,64,512]{2,1,0:T(8,128)(2,1)}, u32[]{:S(2)}, u32[]{:S(2)}) collective-permute-start(bf16[8,64,512]{2,1,0:T(8,128)(2,1)} %get-tuple-element.13), channel_id=1, source_target_pairs={{0,2},{1,3},{2,4},{3,5},{4,6},{5,7},{6,8},{7,9},{8,10},{9,11},{10,... | collective-permute-start | bytes 1572872 | tf_op jit(solution)/shard_map/ppermute | solution.py:17

commit v5 on v4

--- a/solution.py
+++ b/solution.py
@@ -15,6 +15,29 @@
 def shifted(shard, by):
     length = lax.axis_size(AXES)
     return lax.ppermute(shard, AXES, [(i, (i + by) % length) for i in range(length)])
+
+
+def butterfly_sum(value):
+    length = lax.axis_size(AXES)
+    me = lax.axis_index(AXES)
+    stride = 1
+    while stride < length:
+        radix = min(4, length // stride)
+        digit = (me // stride) % radix
+        got = [value]
+        for j in range(1, radix):
+            pairs = []
+            for i in range(length):
+                d = (i // stride) % radix
+                pairs.append((i, i + (((d + j) % radix) - d) * stride))
+            got.append(lax.ppermute(value, AXES, pairs))
+        stacked = jnp.stack(got)
+        ordered = [stacked[(digit - k) % radix] for k in range(radix)]
+        while len(ordered) > 1:
+            ordered = [ordered[i] + ordered[i + 1] for i in range(0, len(ordered), 2)]
+        value = ordered[0]
+        stride *= radix
+    return value
 
 
 def strip_kernel(rows_dev, half, block, sources,
@@ -80,7 +103,7 @@
     own_trace = 2.0 * jnp.sum(jnp.diagonal(diag_own, axis1=1, axis2=2))
     weight = jnp.where(listed, jnp.where(slot_range[None, :] == 0, 1.0, 2.0), 0.0)
     squares = jnp.sum(jnp.square(upper_tiles.astype(jnp.float32)), axis=2)
-    total = lax.psum(lax.psum(own_trace - jnp.sum(weight * squares), "col"), "row")
+    total = butterfly_sum(own_trace - jnp.sum(weight * squares))
     occupancy = (total / (nblocks * block)).astype(jnp.float32)
 
     tiles = upper_tiles.reshape(rows_dev, slots, block, block)

time: 289 us -> 158 us (0.55)
  blocking collectives: 160 us -> 0 us
  between operations: 3.83 us -> 13.4 us
  other arithmetic: 3.72 us -> 11.6 us
  starting transfers between devices: 35.7 us -> 41.8 us
  waiting for transfers between devices: 42.9 us -> 47.5 us
    psum x2 -> x0, blocking collectives: 160 us -> none  [the longest x1 154 us: body(): lax.psum(lax.psum(own_trace - jnp.sum(weight * squares), 'col'), 'row')]
    ppermute x0 -> x12, starting transfers between devices: none -> 31.2 us  [butterfly_sum(): got.append(lax.ppermute(value, AXES, pairs))]
    ppermute x4, starting transfers between devices: 35.7 us -> 10.7 us  [shifted(): lax.ppermute(shard, AXES, [(i, (i + by) % length) for i in range(length)])]
    another operation x0 -> x4, other arithmetic: none -> 7.83 us  [butterfly_sum(): stacked = jnp.stack(got)]
    ppermute x0 -> x12, waiting for transfers between devices: none -> 4.87 us  [butterfly_sum(): got.append(lax.ppermute(value, AXES, pairs))]
  transfers between devices with their start and end apart: 4 -> 16, of which waited for: 2 -> 5; matrix products, arithmetic and copies ran while one was open for 1% -> 11% of each run, Pallas kernels for 0% -> 0%
where the time goes in v5:
time: 158 us
  waiting for transfers between devices  47.5 us (30%)
  starting transfers between devices  41.8 us (26%)
  local copies, waits for them, and re-layouts  26.8 us (17%)
  between operations  13.4 us (8%)
  Pallas kernels  12.8 us (8%)
  other arithmetic  11.6 us (7%)
  matrix products  3.64 us (2%)
    ppermute x4, waiting for transfers between devices, shifted(): lax.ppermute(shard, AXES, [(i, (i + by) % length) for i in range(length)])  42.6 us
    ppermute x12, starting transfers between devices, butterfly_sum(): got.append(lax.ppermute(value, AXES, pairs))  31.2 us
    pallas_call x1, Pallas kernels, body(): pl.pallas_call(functools.partial(strip_kernel, rows_dev, half, block, sou...  12.8 us
    ppermute x4, starting transfers between devices, shifted(): lax.ppermute(shard, AXES, [(i, (i + by) % length) for i in range(length)])  10.7 us
    another operation x4, other arithmetic, butterfly_sum(): stacked = jnp.stack(got)  7.83 us
    reshape x2, local copies, waits for them, and re-layouts, body(): return (new_tiles.reshape(rows_dev, slots, tile_size), occupancy)  6.36 us
    ppermute x12, waiting for transfers between devices, butterfly_sum(): got.append(lax.ppermute(value, AXES, pairs))  4.87 us
    convert_element_type x1, local copies, waits for them, and re-layouts, body(): strips = jnp.einsum('rso,rspq->rpoq', pick_band, tiles, preferred_element...  4.56 us
  transfers between devices with their start and end apart: 16, of which 5 were waited for; matrix products, arithmetic and copies ran while one was open for 11% of the time, Pallas kernels for 0%

profile of v5, /device:TPU:9, one launch (start us, length us, event | category | flops | bytes accessed | tf_op | source)
XLA Modules:
  0.0 157.6 jit_solution(10483221668492584066)
XLA Ops:
  0.7 1.6 %multiply_reduce_fusion = f32[8,17]{0,1:T(8,128)S(1)} fusion(bf16[8,17,4096]{2,0,1:T(8,128)(2,1)} %param.2), kind=kLoop, calls=%fused_computation.4 | loop fusion | flops 1671032 | bytes 1114656 | tf_op jit(solution)/shard_map/reduce_sum | solution.py:105
  8.0 1.7 %collective-permute-start.2 = (f32[]{:T(128)}, f32[]{:T(128)}, u32[]{:S(2)}, u32[]{:S(2)}) collective-permute-start(f32[]{:T(128)} %sub.60), channel_id=1, source_target_pairs={{0,3},{1,0},{2,1},{3,2},{4,7},{5,4},{6,5},{7,6},{8,11},{9,8},{10,9... | collective-permute-start | bytes 20 | tf_op jit(solution)/shard_map/ppermute | solution.py:33
  9.7 1.9 %collective-permute-start.1 = (f32[]{:T(128)}, f32[]{:T(128)}, u32[]{:S(2)}, u32[]{:S(2)}) collective-permute-start(f32[]{:T(128)} %sub.60), channel_id=1, source_target_pairs={{0,2},{1,3},{2,0},{3,1},{4,6},{5,7},{6,4},{7,5},{8,10},{9,11},{10,... | collective-permute-start | bytes 20 | tf_op jit(solution)/shard_map/ppermute | solution.py:33
  11.6 3.0 %collective-permute-start = (f32[]{:T(128)}, f32[]{:T(128)}, u32[]{:S(2)}, u32[]{:S(2)}) collective-permute-start(f32[]{:T(128)} %sub.60), channel_id=1, source_target_pairs={{0,1},{1,2},{2,3},{3,0},{4,5},{5,6},{6,7},{7,4},{8,9},{9,10},{10,1... | collective-permute-start | bytes 20 | tf_op jit(solution)/shard_map/ppermute | solution.py:33
  14.6 2.3 %reshape.59 = bf16[8,17,64,64]{3,2,0,1:T(8,128)(2,1)S(1)} reshape(bf16[8,17,4096]{2,0,1:T(8,128)(2,1)S(1)} %copy-done.2) | data formatting | bytes 2228224 | tf_op jit(solution)/shard_map/reshape | solution.py:109
  17.2 3.6 %convert_bitcast_fusion = bf16[8,64,17,64]{3,2,1,0:T(8,128)(2,1)} fusion(bf16[8,17,64,64]{3,2,0,1:T(8,128)(2,1)S(1)} %reshape.59, s32[8,17]{1,0:T(8,128)S(1)} %copy.30, pred[8,17]{1,0:T(8,128)(4,1)S(1)} %copy.29), kind=kOutput, calls=%fused_computation.3 | convolution fusion | flops 19501584 | bytes 2228904 | tf_op jit(solution)/shard_map/rso,rspq->rpoq/dot_general | solution.py:113
  20.9 4.6 %copy.32 = bf16[8,64,17,64]{1,3,2,0:T(8,128)(2,1)} copy(bf16[8,64,17,64]{3,2,1,0:T(8,128)(2,1)} %convert_bitcast_fusion) | data formatting | bytes 2228224 | tf_op jit(solution)/shard_map/convert_element_type | solution.py:115
  25.4 2.8 %copy.33 = bf16[8,64,1088]{2,1,0:T(8,128)(2,1)S(1)} copy(bf16[8,64,1088]{1,2,0:T(8,128)(2,1)} %bitcast.32) | data formatting | bytes 2228224 | tf_op jit(solution)/shard_map/reshape | solution.py:115
  28.5 2.0 %pad_maximum_fusion = f32[4]{0:T(128)S(1)} fusion(f32[1]{0:T(128)} %bitcast.5, f32[1]{0:T(128)} %bitcast.4, f32[1]{0:T(128)} %bitcast.3, f32[1]{0:T(128)} %bitcast.2), kind=kLoop, calls=%fused_computation.19 | loop fusion | flops 12 | bytes 32 | tf_op jit(solution)/shard_map/stack | solution.py:34
  33.7 1.8 %collective-permute-start.5 = (f32[]{:T(128)}, f32[]{:T(128)}, u32[]{:S(2)}, u32[]{:S(2)}) collective-permute-start(f32[]{:T(128)} %bitcast.6), channel_id=1, source_target_pairs={{0,12},{1,13},{2,14},{3,15},{4,0},{5,1},{6,2},{7,3},{8,4},{9,5},{1... | collective-permute-start | bytes 20 | tf_op jit(solution)/shard_map/ppermute | solution.py:33
  35.4 2.2 %collective-permute-start.4 = (f32[]{:T(128)}, f32[]{:T(128)}, u32[]{:S(2)}, u32[]{:S(2)}) collective-permute-start(f32[]{:T(128)} %bitcast.6), channel_id=1, source_target_pairs={{0,8},{1,9},{2,10},{3,11},{4,12},{5,13},{6,14},{7,15},{8,0},{9,1},... | collective-permute-start | bytes 20 | tf_op jit(solution)/shard_map/ppermute | solution.py:33
  37.7 2.3 %collective-permute-start.3 = (f32[]{:T(128)}, f32[]{:T(128)}, u32[]{:S(2)}, u32[]{:S(2)}) collective-permute-start(f32[]{:T(128)} %bitcast.6), channel_id=1, source_target_pairs={{0,4},{1,5},{2,6},{3,7},{4,8},{5,9},{6,10},{7,11},{8,12},{9,13},{1... | collective-permute-start | bytes 20 | tf_op jit(solution)/shard_map/ppermute | solution.py:33
  40.1 1.9 %pad_maximum_fusion.1 = f32[4]{0:T(128)S(1)} fusion(f32[1]{0:T(128)} %bitcast.9, f32[1]{0:T(128)} %bitcast.8, f32[1]{0:T(128)} %bitcast.7, f32[1]{0:T(128)} %add.230), kind=kLoop, calls=%fused_computation.20 | loop fusion | flops 12 | bytes 32 | tf_op jit(solution)/shard_map/stack | solution.py:34
  45.2 4.6 %collective-permute-start.8 = (f32[]{:T(128)}, f32[]{:T(128)}, u32[]{:S(2)}, u32[]{:S(2)}) collective-permute-start(f32[]{:T(128)} %bitcast.10), channel_id=1, source_target_pairs={{0,48},{1,49},{2,50},{3,51},{4,52},{5,53},{6,54},{7,55},{8,56},{9,... | collective-permute-start | bytes 20 | tf_op jit(solution)/shard_map/ppermute | solution.py:33
  50.5 1.5 collective-permute-start.6
  52.2 3.1 %collective-permute-done.6 = f32[]{:T(128)} collective-permute-done((f32[]{:T(128)}, f32[]{:T(128)}, u32[]{:S(2)}, u32[]{:S(2)}) %collective-permute-start.6) | collective-permute-done | bytes 36 | tf_op jit(solution)/shard_map/ppermute | solution.py:33
  55.3 1.9 %pad_maximum_fusion.2 = f32[4]{0:T(128)S(1)} fusion(f32[1]{0:T(128)} %bitcast.13, f32[1]{0:T(128)} %bitcast.12, f32[1]{0:T(128)} %bitcast.11, f32[1]{0:T(128)} %add.243), kind=kLoop, calls=%fused_computation.21 | loop fusion | flops 12 | bytes 32 | tf_op jit(solution)/shard_map/stack | solution.py:34
  60.4 6.6 %collective-permute-start.11 = (f32[]{:T(128)}, f32[]{:T(128)}, u32[]{:S(2)}, u32[]{:S(2)}) collective-permute-start(f32[]{:T(128)} %bitcast.14), channel_id=1, source_target_pairs={{0,192},{1,193},{2,194},{3,195},{4,196},{5,197},{6,198},{7,199},{8... | collective-permute-start | bytes 20 | tf_op jit(solution)/shard_map/ppermute | solution.py:33
  67.1 1.6 %collective-permute-start.10 = (f32[]{:T(128)}, f32[]{:T(128)}, u32[]{:S(2)}, u32[]{:S(2)}) collective-permute-start(f32[]{:T(128)} %bitcast.14), channel_id=1, source_target_pairs={{0,128},{1,129},{2,130},{3,131},{4,132},{5,133},{6,134},{7,135},{8... | collective-permute-start | bytes 20 | tf_op jit(solution)/shard_map/ppermute | solution.py:33
  68.7 3.1 %collective-permute-start.9 = (f32[]{:T(128)}, f32[]{:T(128)}, u32[]{:S(2)}, u32[]{:S(2)}) collective-permute-start(f32[]{:T(128)} %bitcast.14), channel_id=1, source_target_pairs={{0,64},{1,65},{2,66},{3,67},{4,68},{5,69},{6,70},{7,71},{8,72},{9,... | collective-permute-start | bytes 20 | tf_op jit(solution)/shard_map/ppermute | solution.py:33
  71.8 1.6 collective-permute-done.10
  73.4 1.9 %pad_maximum_fusion.3 = f32[4]{0:T(128)S(1)} fusion(f32[1]{0:T(128)} %bitcast.17, f32[1]{0:T(128)} %bitcast.16, f32[1]{0:T(128)} %bitcast.15, f32[1]{0:T(128)} %add.256), kind=kLoop, calls=%fused_computation.22 | loop fusion | flops 12 | bytes 32 | tf_op jit(solution)/shard_map/stack | solution.py:34
  78.5 2.1 %fusion.11 = (bf16[8,64,1024]{2,1,0:T(8,128)(2,1)}, bf16[8,64,1024]{2,1,0:T(8,128)(2,1)}) fusion(bf16[8,64,1152]{2,1,0:T(8,128)(2,1)S(1)} %pad.4.own_ref), kind=kLoop, calls=%fused_computation.27 | loop fusion | bytes 4194304 | tf_op jit(solution)/shard_map/slice | solution.py:121
  80.6 8.0 %collective-permute-start.14 = (bf16[8,64,1024]{2,1,0:T(8,128)(2,1)}, bf16[8,64,1024]{2,1,0:T(8,128)(2,1)S(1)}, u32[]{:S(2)}, u32[]{:S(2)}) collective-permute-start(bf16[8,64,1024]{2,1,0:T(8,128)(2,1)} %get-tuple-element.14), channel_id=1, source_target_pairs={{0,255},{1,0},{2,1},{3,2},{4,3},{5,4},{6,5},{7,6},{8,7},{9,8},{10,... | collective-permute-start | bytes 3145736 | tf_op jit(solution)/shard_map/ppermute | solution.py:17
  88.8 1.2 fusion.10
  90.0 2.1 %collective-permute-start.15 = (bf16[8,64,512]{2,1,0:T(8,128)(2,1)}, bf16[8,64,512]{2,1,0:T(8,128)(2,1)}, u32[]{:S(2)}, u32[]{:S(2)}) collective-permute-start(bf16[8,64,512]{2,1,0:T(8,128)(2,1)} %get-tuple-element.12), channel_id=1, source_target_pairs={{0,254},{1,255},{2,0},{3,1},{4,2},{5,3},{6,4},{7,5},{8,6},{9,7},{1... | collective-permute-start | bytes 1572872 | tf_op jit(solution)/shard_map/ppermute | solution.py:17
  92.5 1.8 %copy.34.tiles_ref = bf16[8,17,64,64]{3,2,1,0:T(8,128)(2,1)} copy(bf16[8,17,64,64]{3,2,0,1:T(8,128)(2,1)S(1)} %copy-done.1) | data formatting | bytes 2228224 | tf_op jit(solution)/shard_map/reshape | solution.py:109
  94.7 31.9 %collective-permute-done.15.n2_ref = bf16[8,64,512]{2,1,0:T(8,128)(2,1)} collective-permute-done((bf16[8,64,512]{2,1,0:T(8,128)(2,1)}, bf16[8,64,512]{2,1,0:T(8,128)(2,1)}, u32[]{:S(2)}, u32[]{:S(2)}) %collective-permute-start.15) | collective-permute-done | bytes 524320 | tf_op jit(solution)/shard_map/ppermute | solution.py:17
  126.6 10.7 %collective-permute-done.12.p2_ref = bf16[8,64,512]{2,1,0:T(8,128)(2,1)} collective-permute-done((bf16[8,64,512]{2,1,0:T(8,128)(2,1)}, bf16[8,64,512]{2,1,0:T(8,128)(2,1)}, u32[]{:S(2)}, u32[]{:S(2)}) %collective-permute-start.12) | collective-permute-done | bytes 524320 | tf_op jit(solution)/shard_map/ppermute | solution.py:17
  137.3 12.8 %shard_map.41 = f32[8,17,64,64]{3,2,1,0:T(8,128)} custom-call(s32[136]{0:T(256)S(1)} %reshape.58.sel_ref, s32[136]{0:T(256)S(1)} %reshape.62.lst_ref, bf16[8,17,64,64]{3,2,1,0:T(8,128)(2,1)} %copy.34.tiles_ref, bf16[8,64,1152]{2,1,0:T(8,128)(2,1)S(1)} %pad.4.own_ref, bf16[8,64,512]{2,1,0:T(8,128)(2,1)} %collective-permute-done.12.p2_ref, ...), custom_call_target="tpu_custom_call" | custom-call | flops 4026531840 | bytes 8388608 | tf_op jit(solution)/shard_map/pallas_call | solution.py:131
  150.1 3.7 %reshape.71 = f32[8,17,4096]{2,1,0:T(8,128)S(1)} reshape(f32[8,17,64,64]{3,2,1,0:T(8,128)} %shard_map.41) | data formatting | bytes 4456448 | tf_op jit(solution)/shard_map/reshape | solution.py:143
  153.8 2.7 %copy.37 = f32[8,17,4096]{2,0,1:T(8,128)} copy(f32[8,17,4096]{2,1,0:T(8,128)S(1)} %reshape.71) | data formatting | bytes 4456448 | tf_op jit(solution)/shard_map/reshape | solution.py:143
  (43 shorter events, 9.2 us)
Async XLA Ops:
  0.6 14.0 %copy-start.2 = (bf16[8,17,4096]{2,0,1:T(8,128)(2,1)S(1)}, bf16[8,17,4096]{2,0,1:T(8,128)(2,1)}, u32[]{:S(2)}) copy-start(bf16[8,17,4096]{2,0,1:T(8,128)(2,1)} %param.2) | copy-start | bytes 3342340
  8.0 20.5 %collective-permute-start.2 = (f32[]{:T(128)}, f32[]{:T(128)}, u32[]{:S(2)}, u32[]{:S(2)}) collective-permute-start(f32[]{:T(128)} %sub.60), channel_id=1, source_target_pairs={{0,3},{1,0},{2,1},{3,2},{4,7},{5,4},{6,5},{7,6},{8,11},{9,8},{10,9... | collective-permute-start | bytes 20 | tf_op jit(solution)/shard_map/ppermute | solution.py:33
  9.7 18.8 %collective-permute-start.1 = (f32[]{:T(128)}, f32[]{:T(128)}, u32[]{:S(2)}, u32[]{:S(2)}) collective-permute-start(f32[]{:T(128)} %sub.60), channel_id=1, source_target_pairs={{0,2},{1,3},{2,0},{3,1},{4,6},{5,7},{6,4},{7,5},{8,10},{9,11},{10,... | collective-permute-start | bytes 20 | tf_op jit(solution)/shard_map/ppermute | solution.py:33
  11.6 16.8 %collective-permute-start = (f32[]{:T(128)}, f32[]{:T(128)}, u32[]{:S(2)}, u32[]{:S(2)}) collective-permute-start(f32[]{:T(128)} %sub.60), channel_id=1, source_target_pairs={{0,1},{1,2},{2,3},{3,0},{4,5},{5,6},{6,7},{7,4},{8,9},{9,10},{10,1... | collective-permute-start | bytes 20 | tf_op jit(solution)/shard_map/ppermute | solution.py:33
  17.0 3.9 %copy-start = (bf16[8,17,64,64]{3,2,0,1:T(8,128)(2,1)}, bf16[8,17,64,64]{3,2,0,1:T(8,128)(2,1)S(1)}, u32[]{:S(2)}) copy-start(bf16[8,17,64,64]{3,2,0,1:T(8,128)(2,1)S(1)} %reshape.59) | copy-start | bytes 3342340
  33.7 6.3 %collective-permute-start.5 = (f32[]{:T(128)}, f32[]{:T(128)}, u32[]{:S(2)}, u32[]{:S(2)}) collective-permute-start(f32[]{:T(128)} %bitcast.6), channel_id=1, source_target_pairs={{0,12},{1,13},{2,14},{3,15},{4,0},{5,1},{6,2},{7,3},{8,4},{9,5},{1... | collective-permute-start | bytes 20 | tf_op jit(solution)/shard_map/ppermute | solution.py:33
  35.4 4.6 %collective-permute-start.4 = (f32[]{:T(128)}, f32[]{:T(128)}, u32[]{:S(2)}, u32[]{:S(2)}) collective-permute-start(f32[]{:T(128)} %bitcast.6), channel_id=1, source_target_pairs={{0,8},{1,9},{2,10},{3,11},{4,12},{5,13},{6,14},{7,15},{8,0},{9,1},... | collective-permute-start | bytes 20 | tf_op jit(solution)/shard_map/ppermute | solution.py:33
  37.7 2.4 %collective-permute-start.3 = (f32[]{:T(128)}, f32[]{:T(128)}, u32[]{:S(2)}, u32[]{:S(2)}) collective-permute-start(f32[]{:T(128)} %bitcast.6), channel_id=1, source_target_pairs={{0,4},{1,5},{2,6},{3,7},{4,8},{5,9},{6,10},{7,11},{8,12},{9,13},{1... | collective-permute-start | bytes 20 | tf_op jit(solution)/shard_map/ppermute | solution.py:33
  45.2 6.9 %collective-permute-start.8 = (f32[]{:T(128)}, f32[]{:T(128)}, u32[]{:S(2)}, u32[]{:S(2)}) collective-permute-start(f32[]{:T(128)} %bitcast.10), channel_id=1, source_target_pairs={{0,48},{1,49},{2,50},{3,51},{4,52},{5,53},{6,54},{7,55},{8,56},{9,... | collective-permute-start | bytes 20 | tf_op jit(solution)/shard_map/ppermute | solution.py:33
  49.8 2.4 %collective-permute-start.7 = (f32[]{:T(128)}, f32[]{:T(128)}, u32[]{:S(2)}, u32[]{:S(2)}) collective-permute-start(f32[]{:T(128)} %bitcast.10), channel_id=1, source_target_pairs={{0,32},{1,33},{2,34},{3,35},{4,36},{5,37},{6,38},{7,39},{8,40},{9,... | collective-permute-start | bytes 20 | tf_op jit(solution)/shard_map/ppermute | solution.py:33
  50.5 4.8 %collective-permute-start.6 = (f32[]{:T(128)}, f32[]{:T(128)}, u32[]{:S(2)}, u32[]{:S(2)}) collective-permute-start(f32[]{:T(128)} %bitcast.10), channel_id=1, source_target_pairs={{0,16},{1,17},{2,18},{3,19},{4,20},{5,21},{6,22},{7,23},{8,24},{9,... | collective-permute-start | bytes 20 | tf_op jit(solution)/shard_map/ppermute | solution.py:33
  60.4 11.4 %collective-permute-start.11 = (f32[]{:T(128)}, f32[]{:T(128)}, u32[]{:S(2)}, u32[]{:S(2)}) collective-permute-start(f32[]{:T(128)} %bitcast.14), channel_id=1, source_target_pairs={{0,192},{1,193},{2,194},{3,195},{4,196},{5,197},{6,198},{7,199},{8... | collective-permute-start | bytes 20 | tf_op jit(solution)/shard_map/ppermute | solution.py:33
  67.1 6.3 %collective-permute-start.10 = (f32[]{:T(128)}, f32[]{:T(128)}, u32[]{:S(2)}, u32[]{:S(2)}) collective-permute-start(f32[]{:T(128)} %bitcast.14), channel_id=1, source_target_pairs={{0,128},{1,129},{2,130},{3,131},{4,132},{5,133},{6,134},{7,135},{8... | collective-permute-start | bytes 20 | tf_op jit(solution)/shard_map/ppermute | solution.py:33
  68.7 4.7 %collective-permute-start.9 = (f32[]{:T(128)}, f32[]{:T(128)}, u32[]{:S(2)}, u32[]{:S(2)}) collective-permute-start(f32[]{:T(128)} %bitcast.14), channel_id=1, source_target_pairs={{0,64},{1,65},{2,66},{3,67},{4,68},{5,69},{6,70},{7,71},{8,72},{9,... | collective-permute-start | bytes 20 | tf_op jit(solution)/shard_map/ppermute | solution.py:33
  78.5 14.0 %copy-start.1 = (bf16[8,17,64,64]{3,2,0,1:T(8,128)(2,1)S(1)}, bf16[8,17,64,64]{3,2,0,1:T(8,128)(2,1)}, u32[]{:S(2)}) copy-start(bf16[8,17,64,64]{3,2,0,1:T(8,128)(2,1)} %copy-done) | copy-start | bytes 3342340
  80.6 56.6 %collective-permute-start.14 = (bf16[8,64,1024]{2,1,0:T(8,128)(2,1)}, bf16[8,64,1024]{2,1,0:T(8,128)(2,1)S(1)}, u32[]{:S(2)}, u32[]{:S(2)}) collective-permute-start(bf16[8,64,1024]{2,1,0:T(8,128)(2,1)} %get-tuple-element.14), channel_id=1, source_target_pairs={{0,255},{1,0},{2,1},{3,2},{4,3},{5,4},{6,5},{7,6},{8,7},{9,8},{10,... | collective-permute-start | bytes 3145736 | tf_op jit(solution)/shard_map/ppermute | solution.py:17
  88.6 48.6 %collective-permute-start.13 = (bf16[8,64,1024]{2,1,0:T(8,128)(2,1)}, bf16[8,64,1024]{2,1,0:T(8,128)(2,1)S(1)}, u32[]{:S(2)}, u32[]{:S(2)}) collective-permute-start(bf16[8,64,1024]{2,1,0:T(8,128)(2,1)} %get-tuple-element.15), channel_id=1, source_target_pairs={{0,1},{1,2},{2,3},{3,4},{4,5},{5,6},{6,7},{7,8},{8,9},{9,10},{10,1... | collective-permute-start | bytes 3145736 | tf_op jit(solution)/shard_map/ppermute | solution.py:17
  90.0 36.5 %collective-permute-start.15 = (bf16[8,64,512]{2,1,0:T(8,128)(2,1)}, bf16[8,64,512]{2,1,0:T(8,128)(2,1)}, u32[]{:S(2)}, u32[]{:S(2)}) collective-permute-start(bf16[8,64,512]{2,1,0:T(8,128)(2,1)} %get-tuple-element.12), channel_id=1, source_target_pairs={{0,254},{1,255},{2,0},{3,1},{4,2},{5,3},{6,4},{7,5},{8,6},{9,7},{1... | collective-permute-start | bytes 1572872 | tf_op jit(solution)/shard_map/ppermute | solution.py:17
  92.1 45.2 %collective-permute-start.12 = (bf16[8,64,512]{2,1,0:T(8,128)(2,1)}, bf16[8,64,512]{2,1,0:T(8,128)(2,1)}, u32[]{:S(2)}, u32[]{:S(2)}) collective-permute-start(bf16[8,64,512]{2,1,0:T(8,128)(2,1)} %get-tuple-element.13), channel_id=1, source_target_pairs={{0,2},{1,3},{2,4},{3,5},{4,6},{5,7},{6,8},{7,9},{8,10},{9,11},{10,... | collective-permute-start | bytes 1572872 | tf_op jit(solution)/shard_map/ppermute | solution.py:17

commit v6 on v4

--- a/solution.py
+++ b/solution.py
@@ -15,6 +15,15 @@
 def shifted(shard, by):
     length = lax.axis_size(AXES)
     return lax.ppermute(shard, AXES, [(i, (i + by) % length) for i in range(length)])
+
+
+def butterfly_sum(value):
+    length = lax.axis_size(AXES)
+    stride = 1
+    while stride < length:
+        value = value + lax.ppermute(value, AXES, [(i, i ^ stride) for i in range(length)])
+        stride *= 2
+    return value
 
 
 def strip_kernel(rows_dev, half, block, sources,
@@ -80,7 +89,7 @@
     own_trace = 2.0 * jnp.sum(jnp.diagonal(diag_own, axis1=1, axis2=2))
     weight = jnp.where(listed, jnp.where(slot_range[None, :] == 0, 1.0, 2.0), 0.0)
     squares = jnp.sum(jnp.square(upper_tiles.astype(jnp.float32)), axis=2)
-    total = lax.psum(lax.psum(own_trace - jnp.sum(weight * squares), "col"), "row")
+    total = butterfly_sum(own_trace - jnp.sum(weight * squares))
     occupancy = (total / (nblocks * block)).astype(jnp.float32)
 
     tiles = upper_tiles.reshape(rows_dev, slots, block, block)
@@ -93,11 +102,11 @@
     strips = jnp.pad(strips, ((0, 0), (0, 0), (0, block)))
     occupancy, strips = lax.optimization_barrier((occupancy, strips))
 
-    from_prev2 = shifted(strips[:, :, cut * block : slots * block], 2)
-    from_prev1 = shifted(strips[:, :, block : slots * block], 1)
+    from_prev2 = shifted(strips[:, :, (cut - 1) * block :], 2)
+    from_prev1 = shifted(strips, 1)
     from_next1 = shifted(strips[:, :, : (slots - 1) * block], -1)
     from_next2 = shifted(strips[:, :, : (slots - cut) * block], -2)
-    sources = (("p2", cut, slots - cut), ("p1", 1, slots - 1), ("own", 0, slots),
+    sources = (("p2", cut - 1, slots - cut + 1), ("p1", 0, slots), ("own", 0, slots),
                ("n1", 0, slots - 1), ("n2", 0, slots - cut))
 
     sel = jnp.where(listed, local_rows[:, None] * slots + offsets_of, 0).reshape(-1).astype(jnp.int32)

time: 289 us -> 137 us (0.47)
  the two profiles are of different devices: /device:TPU:9 before, /device:TPU:0 now
where the time goes in v6:
time: 137 us; the launch traced here: 134 us
  waiting for transfers between devices  46.5 us (34%)
  starting transfers between devices  35.5 us (26%)
  local copies, waits for them, and re-layouts  23.8 us (17%)
  Pallas kernels  12.6 us (9%)
  between operations  8.24 us (6%)
  other arithmetic  3.8 us (3%)
  matrix products  3.64 us (3%)
    ppermute x4, waiting for transfers between devices, shifted(): lax.ppermute(shard, AXES, [(i, (i + by) % length) for i in range(length)])  33.1 us
    ppermute x8, starting transfers between devices, butterfly_sum(): lax.ppermute(value, AXES, [(i, i ^ stride) for i in range(length)])  20.8 us
    ppermute x4, starting transfers between devices, shifted(): lax.ppermute(shard, AXES, [(i, (i + by) % length) for i in range(length)])  14.7 us
    ppermute x8, waiting for transfers between devices, butterfly_sum(): lax.ppermute(value, AXES, [(i, i ^ stride) for i in range(length)])  13.3 us
    pallas_call x1, Pallas kernels, body(): pl.pallas_call(functools.partial(strip_kernel, rows_dev, half, block, sou...  12.6 us
    reshape x2, local copies, waits for them, and re-layouts, body(): return (new_tiles.reshape(rows_dev, slots, tile_size), occupancy)  6.36 us
    convert_element_type x1, local copies, waits for them, and re-layouts, body(): strips = jnp.einsum('rso,rspq->rpoq', pick_band, tiles, preferred_element...  4.61 us
    reshape x2, local copies, waits for them, and re-layouts, body(): tiles = upper_tiles.reshape(rows_dev, slots, block, block)  4.16 us
  transfers between devices with their start and end apart: 12, of which 8 were waited for; matrix products, arithmetic and copies ran while one was open for 14% of the time, Pallas kernels for 0%

profile of v6, /device:TPU:0, one launch (start us, length us, event | category | flops | bytes accessed | tf_op | source)
XLA Modules:
  0.0 134.0 jit_solution(15555058137961569254)
XLA Ops:
  0.7 1.6 %multiply_reduce_fusion = f32[8,17]{0,1:T(8,128)S(1)} fusion(bf16[8,17,4096]{2,0,1:T(8,128)(2,1)} %param.2), kind=kLoop, calls=%fused_computation.4 | loop fusion | flops 1671032 | bytes 1114656 | tf_op jit(solution)/shard_map/reduce_sum | solution.py:91
  2.3 0.8 slice_convert_fusion
  3.2 0.8 copy.24
  4.5 0.9 gather_fusion
  8.0 1.0 collective-permute-start
  9.1 2.3 %reshape.42 = bf16[8,17,64,64]{3,2,0,1:T(8,128)(2,1)S(1)} reshape(bf16[8,17,4096]{2,0,1:T(8,128)(2,1)S(1)} %copy-done.2) | data formatting | bytes 2228224 | tf_op jit(solution)/shard_map/reshape | solution.py:95
  11.6 3.6 %convert_bitcast_fusion = bf16[8,64,17,64]{3,2,1,0:T(8,128)(2,1)} fusion(bf16[8,17,64,64]{3,2,0,1:T(8,128)(2,1)S(1)} %reshape.42, s32[8,17]{1,0:T(8,128)S(1)} %copy.30, pred[8,17]{1,0:T(8,128)(4,1)S(1)} %copy.29), kind=kOutput, calls=%fused_computation.3 | convolution fusion | flops 19501584 | bytes 2228904 | tf_op jit(solution)/shard_map/rso,rspq->rpoq/dot_general | solution.py:99
  15.3 4.6 %copy.32 = bf16[8,64,17,64]{1,3,2,0:T(8,128)(2,1)} copy(bf16[8,64,17,64]{3,2,1,0:T(8,128)(2,1)} %convert_bitcast_fusion) | data formatting | bytes 2228224 | tf_op jit(solution)/shard_map/convert_element_type | solution.py:101
  19.9 2.8 %copy.33 = bf16[8,64,1088]{2,1,0:T(8,128)(2,1)S(1)} copy(bf16[8,64,1088]{1,2,0:T(8,128)(2,1)} %bitcast.15) | data formatting | bytes 2228224 | tf_op jit(solution)/shard_map/reshape | solution.py:101
  23.5 1.4 %collective-permute-start.1 = (f32[]{:T(128)}, f32[]{:T(128)}, u32[]{:S(2)}, u32[]{:S(2)}) collective-permute-start(f32[]{:T(128)} %add.63), channel_id=1, source_target_pairs={{0,2},{1,3},{2,0},{3,1},{4,6},{5,7},{6,4},{7,5},{8,10},{9,11},{10,... | collective-permute-start | bytes 20 | tf_op jit(solution)/shard_map/ppermute | solution.py:24
  24.9 2.2 %collective-permute-done.1 = f32[]{:T(128)} collective-permute-done((f32[]{:T(128)}, f32[]{:T(128)}, u32[]{:S(2)}, u32[]{:S(2)}) %collective-permute-start.1) | collective-permute-done | bytes 36 | tf_op jit(solution)/shard_map/ppermute | solution.py:24
  27.7 1.4 %collective-permute-start.2 = (f32[]{:T(128)}, f32[]{:T(128)}, u32[]{:S(2)}, u32[]{:S(2)}) collective-permute-start(f32[]{:T(128)} %add.64), channel_id=1, source_target_pairs={{0,4},{1,5},{2,6},{3,7},{4,0},{5,1},{6,2},{7,3},{8,12},{9,13},{10,... | collective-permute-start | bytes 20 | tf_op jit(solution)/shard_map/ppermute | solution.py:24
  29.1 2.2 %collective-permute-done.2 = f32[]{:T(128)} collective-permute-done((f32[]{:T(128)}, f32[]{:T(128)}, u32[]{:S(2)}, u32[]{:S(2)}) %collective-permute-start.2) | collective-permute-done | bytes 36 | tf_op jit(solution)/shard_map/ppermute | solution.py:24
  31.9 2.9 %collective-permute-start.3 = (f32[]{:T(128)}, f32[]{:T(128)}, u32[]{:S(2)}, u32[]{:S(2)}) collective-permute-start(f32[]{:T(128)} %add.65), channel_id=1, source_target_pairs={{0,8},{1,9},{2,10},{3,11},{4,12},{5,13},{6,14},{7,15},{8,0},{9,1},... | collective-permute-start | bytes 20 | tf_op jit(solution)/shard_map/ppermute | solution.py:24
  34.8 2.2 %collective-permute-done.3 = f32[]{:T(128)} collective-permute-done((f32[]{:T(128)}, f32[]{:T(128)}, u32[]{:S(2)}, u32[]{:S(2)}) %collective-permute-start.3) | collective-permute-done | bytes 36 | tf_op jit(solution)/shard_map/ppermute | solution.py:24
  37.7 2.7 %collective-permute-start.4 = (f32[]{:T(128)}, f32[]{:T(128)}, u32[]{:S(2)}, u32[]{:S(2)}) collective-permute-start(f32[]{:T(128)} %add.66), channel_id=1, source_target_pairs={{0,16},{1,17},{2,18},{3,19},{4,20},{5,21},{6,22},{7,23},{8,24},{9,... | collective-permute-start | bytes 20 | tf_op jit(solution)/shard_map/ppermute | solution.py:24
  40.4 2.4 %collective-permute-done.4 = f32[]{:T(128)} collective-permute-done((f32[]{:T(128)}, f32[]{:T(128)}, u32[]{:S(2)}, u32[]{:S(2)}) %collective-permute-start.4) | collective-permute-done | bytes 36 | tf_op jit(solution)/shard_map/ppermute | solution.py:24
  43.4 1.6 %collective-permute-start.5 = (f32[]{:T(128)}, f32[]{:T(128)}, u32[]{:S(2)}, u32[]{:S(2)}) collective-permute-start(f32[]{:T(128)} %add.67), channel_id=1, source_target_pairs={{0,32},{1,33},{2,34},{3,35},{4,36},{5,37},{6,38},{7,39},{8,40},{9,... | collective-permute-start | bytes 20 | tf_op jit(solution)/shard_map/ppermute | solution.py:24
  45.0 2.0 %collective-permute-done.5 = f32[]{:T(128)} collective-permute-done((f32[]{:T(128)}, f32[]{:T(128)}, u32[]{:S(2)}, u32[]{:S(2)}) %collective-permute-start.5) | collective-permute-done | bytes 36 | tf_op jit(solution)/shard_map/ppermute | solution.py:24
  47.7 2.9 %collective-permute-start.6 = (f32[]{:T(128)}, f32[]{:T(128)}, u32[]{:S(2)}, u32[]{:S(2)}) collective-permute-start(f32[]{:T(128)} %add.68), channel_id=1, source_target_pairs={{0,64},{1,65},{2,66},{3,67},{4,68},{5,69},{6,70},{7,71},{8,72},{9,... | collective-permute-start | bytes 20 | tf_op jit(solution)/shard_map/ppermute | solution.py:24
  50.6 1.6 %collective-permute-done.6 = f32[]{:T(128)} collective-permute-done((f32[]{:T(128)}, f32[]{:T(128)}, u32[]{:S(2)}, u32[]{:S(2)}) %collective-permute-start.6) | collective-permute-done | bytes 36 | tf_op jit(solution)/shard_map/ppermute | solution.py:24
  52.8 6.9 %collective-permute-start.7 = (f32[]{:T(128)}, f32[]{:T(128)}, u32[]{:S(2)}, u32[]{:S(2)}) collective-permute-start(f32[]{:T(128)} %add.69), channel_id=1, source_target_pairs={{0,128},{1,129},{2,130},{3,131},{4,132},{5,133},{6,134},{7,135},{8... | collective-permute-start | bytes 20 | tf_op jit(solution)/shard_map/ppermute | solution.py:24
  61.1 1.1 slice.14
  62.2 7.2 %collective-permute-start.10 = (bf16[8,64,1024]{2,1,0:T(8,128)(2,1)}, bf16[8,64,1024]{2,1,0:T(8,128)(2,1)S(1)}, u32[]{:S(2)}, u32[]{:S(2)}) collective-permute-start(bf16[8,64,1024]{2,1,0:T(8,128)(2,1)} %slice.14), channel_id=1, source_target_pairs={{0,255},{1,0},{2,1},{3,2},{4,3},{5,4},{6,5},{7,6},{8,7},{9,8},{10,... | collective-permute-start | bytes 3145736 | tf_op jit(solution)/shard_map/ppermute | solution.py:17
  69.3 0.9 slice.13
  70.3 0.9 slice.15
  71.1 7.5 %collective-permute-start.11 = (bf16[8,64,512]{2,1,0:T(8,128)(2,1)}, bf16[8,64,512]{2,1,0:T(8,128)(2,1)}, u32[]{:S(2)}, u32[]{:S(2)}) collective-permute-start(bf16[8,64,512]{2,1,0:T(8,128)(2,1)} %slice.15), channel_id=1, source_target_pairs={{0,254},{1,255},{2,0},{3,1},{4,2},{5,3},{6,4},{7,5},{8,6},{9,7},{1... | collective-permute-start | bytes 1572872 | tf_op jit(solution)/shard_map/ppermute | solution.py:17
  78.6 1.8 %copy.34.tiles_ref = bf16[8,17,64,64]{3,2,1,0:T(8,128)(2,1)} copy(bf16[8,17,64,64]{3,2,0,1:T(8,128)(2,1)S(1)} %copy-done.1) | data formatting | bytes 2228224 | tf_op jit(solution)/shard_map/reshape | solution.py:95
  80.7 33.1 %collective-permute-done.11.n2_ref = bf16[8,64,512]{2,1,0:T(8,128)(2,1)} collective-permute-done((bf16[8,64,512]{2,1,0:T(8,128)(2,1)}, bf16[8,64,512]{2,1,0:T(8,128)(2,1)}, u32[]{:S(2)}, u32[]{:S(2)}) %collective-permute-start.11) | collective-permute-done | bytes 524320 | tf_op jit(solution)/shard_map/ppermute | solution.py:17
  113.9 12.6 %shard_map.41 = f32[8,17,64,64]{3,2,1,0:T(8,128)} custom-call(s32[136]{0:T(256)S(1)} %reshape.41.sel_ref, s32[136]{0:T(256)S(1)} %reshape.45.lst_ref, bf16[8,17,64,64]{3,2,1,0:T(8,128)(2,1)} %copy.34.tiles_ref, bf16[8,64,1152]{2,1,0:T(8,128)(2,1)S(1)} %pad.4.own_ref, bf16[8,64,640]{2,1,0:T(8,128)(2,1)} %collective-permute-done.8.p2_ref, ...), custom_call_target="tpu_custom_call" | custom-call | flops 4026531840 | bytes 8388608 | tf_op jit(solution)/shard_map/pallas_call | solution.py:117
  126.5 3.7 %reshape.54 = f32[8,17,4096]{2,1,0:T(8,128)S(1)} reshape(f32[8,17,64,64]{3,2,1,0:T(8,128)} %shard_map.41) | data formatting | bytes 4456448 | tf_op jit(solution)/shard_map/reshape | solution.py:129
  130.2 2.7 %copy.37 = f32[8,17,4096]{2,0,1:T(8,128)} copy(f32[8,17,4096]{2,1,0:T(8,128)S(1)} %reshape.54) | data formatting | bytes 4456448 | tf_op jit(solution)/shard_map/reshape | solution.py:129
  (28 shorter events, 3.3 us)
Async XLA Ops:
  0.6 8.4 %copy-start.2 = (bf16[8,17,4096]{2,0,1:T(8,128)(2,1)S(1)}, bf16[8,17,4096]{2,0,1:T(8,128)(2,1)}, u32[]{:S(2)}) copy-start(bf16[8,17,4096]{2,0,1:T(8,128)(2,1)} %param.2) | copy-start | bytes 3342340
  8.0 14.8 %collective-permute-start = (f32[]{:T(128)}, f32[]{:T(128)}, u32[]{:S(2)}, u32[]{:S(2)}) collective-permute-start(f32[]{:T(128)} %sub.13), channel_id=1, source_target_pairs={{0,1},{1,0},{2,3},{3,2},{4,5},{5,4},{6,7},{7,6},{8,9},{9,8},{10,11... | collective-permute-start | bytes 20 | tf_op jit(solution)/shard_map/ppermute | solution.py:24
  11.4 3.9 %copy-start = (bf16[8,17,64,64]{3,2,0,1:T(8,128)(2,1)}, bf16[8,17,64,64]{3,2,0,1:T(8,128)(2,1)S(1)}, u32[]{:S(2)}) copy-start(bf16[8,17,64,64]{3,2,0,1:T(8,128)(2,1)S(1)} %reshape.42) | copy-start | bytes 3342340
  23.5 3.6 %collective-permute-start.1 = (f32[]{:T(128)}, f32[]{:T(128)}, u32[]{:S(2)}, u32[]{:S(2)}) collective-permute-start(f32[]{:T(128)} %add.63), channel_id=1, source_target_pairs={{0,2},{1,3},{2,0},{3,1},{4,6},{5,7},{6,4},{7,5},{8,10},{9,11},{10,... | collective-permute-start | bytes 20 | tf_op jit(solution)/shard_map/ppermute | solution.py:24
  27.7 3.6 %collective-permute-start.2 = (f32[]{:T(128)}, f32[]{:T(128)}, u32[]{:S(2)}, u32[]{:S(2)}) collective-permute-start(f32[]{:T(128)} %add.64), channel_id=1, source_target_pairs={{0,4},{1,5},{2,6},{3,7},{4,0},{5,1},{6,2},{7,3},{8,12},{9,13},{10,... | collective-permute-start | bytes 20 | tf_op jit(solution)/shard_map/ppermute | solution.py:24
  31.9 5.1 %collective-permute-start.3 = (f32[]{:T(128)}, f32[]{:T(128)}, u32[]{:S(2)}, u32[]{:S(2)}) collective-permute-start(f32[]{:T(128)} %add.65), channel_id=1, source_target_pairs={{0,8},{1,9},{2,10},{3,11},{4,12},{5,13},{6,14},{7,15},{8,0},{9,1},... | collective-permute-start | bytes 20 | tf_op jit(solution)/shard_map/ppermute | solution.py:24
  37.7 5.1 %collective-permute-start.4 = (f32[]{:T(128)}, f32[]{:T(128)}, u32[]{:S(2)}, u32[]{:S(2)}) collective-permute-start(f32[]{:T(128)} %add.66), channel_id=1, source_target_pairs={{0,16},{1,17},{2,18},{3,19},{4,20},{5,21},{6,22},{7,23},{8,24},{9,... | collective-permute-start | bytes 20 | tf_op jit(solution)/shard_map/ppermute | solution.py:24
  43.4 3.6 %collective-permute-start.5 = (f32[]{:T(128)}, f32[]{:T(128)}, u32[]{:S(2)}, u32[]{:S(2)}) collective-permute-start(f32[]{:T(128)} %add.67), channel_id=1, source_target_pairs={{0,32},{1,33},{2,34},{3,35},{4,36},{5,37},{6,38},{7,39},{8,40},{9,... | collective-permute-start | bytes 20 | tf_op jit(solution)/shard_map/ppermute | solution.py:24
  47.7 4.5 %collective-permute-start.6 = (f32[]{:T(128)}, f32[]{:T(128)}, u32[]{:S(2)}, u32[]{:S(2)}) collective-permute-start(f32[]{:T(128)} %add.68), channel_id=1, source_target_pairs={{0,64},{1,65},{2,66},{3,67},{4,68},{5,69},{6,70},{7,71},{8,72},{9,... | collective-permute-start | bytes 20 | tf_op jit(solution)/shard_map/ppermute | solution.py:24
  52.8 7.5 %collective-permute-start.7 = (f32[]{:T(128)}, f32[]{:T(128)}, u32[]{:S(2)}, u32[]{:S(2)}) collective-permute-start(f32[]{:T(128)} %add.69), channel_id=1, source_target_pairs={{0,128},{1,129},{2,130},{3,131},{4,132},{5,133},{6,134},{7,135},{8... | collective-permute-start | bytes 20 | tf_op jit(solution)/shard_map/ppermute | solution.py:24
  61.0 17.6 %copy-start.1 = (bf16[8,17,64,64]{3,2,0,1:T(8,128)(2,1)S(1)}, bf16[8,17,64,64]{3,2,0,1:T(8,128)(2,1)}, u32[]{:S(2)}) copy-start(bf16[8,17,64,64]{3,2,0,1:T(8,128)(2,1)} %copy-done) | copy-start | bytes 3342340
  61.0 52.9 %collective-permute-start.9 = (bf16[8,64,1152]{2,1,0:T(8,128)(2,1)S(1)}, bf16[8,64,1152]{2,1,0:T(8,128)(2,1)S(1)}, u32[]{:S(2)}, u32[]{:S(2)}) collective-permute-start(bf16[8,64,1152]{2,1,0:T(8,128)(2,1)S(1)} %pad.4.own_ref), channel_id=1, source_target_pairs={{0,1},{1,2},{2,3},{3,4},{4,5},{5,6},{6,7},{7,8},{8,9},{9,10},{10,1... | collective-permute-start | bytes 3538952 | tf_op jit(solution)/shard_map/ppermute | solution.py:17
  62.2 51.7 %collective-permute-start.10 = (bf16[8,64,1024]{2,1,0:T(8,128)(2,1)}, bf16[8,64,1024]{2,1,0:T(8,128)(2,1)S(1)}, u32[]{:S(2)}, u32[]{:S(2)}) collective-permute-start(bf16[8,64,1024]{2,1,0:T(8,128)(2,1)} %slice.14), channel_id=1, source_target_pairs={{0,255},{1,0},{2,1},{3,2},{4,3},{5,4},{6,5},{7,6},{8,7},{9,8},{10,... | collective-permute-start | bytes 3145736 | tf_op jit(solution)/shard_map/ppermute | solution.py:17
  70.3 43.6 %collective-permute-start.8 = (bf16[8,64,640]{2,1,0:T(8,128)(2,1)}, bf16[8,64,640]{2,1,0:T(8,128)(2,1)}, u32[]{:S(2)}, u32[]{:S(2)}) collective-permute-start(bf16[8,64,640]{2,1,0:T(8,128)(2,1)} %slice.13), channel_id=1, source_target_pairs={{0,2},{1,3},{2,4},{3,5},{4,6},{5,7},{6,8},{7,9},{8,10},{9,11},{10,... | collective-permute-start | bytes 1966088 | tf_op jit(solution)/shard_map/ppermute | solution.py:17
  71.1 42.7 %collective-permute-start.11 = (bf16[8,64,512]{2,1,0:T(8,128)(2,1)}, bf16[8,64,512]{2,1,0:T(8,128)(2,1)}, u32[]{:S(2)}, u32[]{:S(2)}) collective-permute-start(bf16[8,64,512]{2,1,0:T(8,128)(2,1)} %slice.15), channel_id=1, source_target_pairs={{0,254},{1,255},{2,0},{3,1},{4,2},{5,3},{6,4},{7,5},{8,6},{9,7},{1... | collective-permute-start | bytes 1572872 | tf_op jit(solution)/shard_map/ppermute | solution.py:17

commit v7 on v6

--- a/solution.py
+++ b/solution.py
@@ -100,7 +100,6 @@
         "rso,rspq->rpoq", pick_band, tiles, preferred_element_type=jnp.float32
     ).astype(jnp.bfloat16).reshape(rows_dev, block, slots * block)
     strips = jnp.pad(strips, ((0, 0), (0, 0), (0, block)))
-    occupancy, strips = lax.optimization_barrier((occupancy, strips))
 
     from_prev2 = shifted(strips[:, :, (cut - 1) * block :], 2)
     from_prev1 = shifted(strips, 1)

time: 137 us -> 129 us (0.942)
  waiting for transfers between devices: 46.5 us -> 26.2 us
  local copies, waits for them, and re-layouts: 23.8 us -> 31 us
  starting transfers between devices: 35.5 us -> 41.4 us
    ppermute x4, waiting for transfers between devices: 33.1 us -> 0.01 us  [shifted(): lax.ppermute(shard, AXES, [(i, (i + by) % length) for i in range(length)])]
    ppermute x8, waiting for transfers between devices: 13.3 us -> 26.2 us  [butterfly_sum(): lax.ppermute(value, AXES, [(i, i ^ stride) for i in range(length)])]
    ppermute x8, starting transfers between devices: 20.8 us -> 31.2 us  [butterfly_sum(): lax.ppermute(value, AXES, [(i, i ^ stride) for i in range(length)])]
    ppermute x4, starting transfers between devices: 14.7 us -> 10.3 us  [shifted(): lax.ppermute(shard, AXES, [(i, (i + by) % length) for i in range(length)])]
    reshape x2, local copies, waits for them, and re-layouts: 4.16 us -> 6.96 us  [body(): tiles = upper_tiles.reshape(rows_dev, slots, block, block)]
  transfers between devices with their start and end apart: 12 -> 12, of which waited for: 8 -> 7; matrix products, arithmetic and copies ran while one was open for 14% -> 11% of each run, Pallas kernels for 0% -> 0%
where the time goes in v7:
time: 129 us; the launch traced here: 127 us
  starting transfers between devices  41.4 us (32%)
  local copies, waits for them, and re-layouts  31 us (24%)
  waiting for transfers between devices  26.2 us (20%)
  Pallas kernels  12.6 us (10%)
  between operations  8.27 us (6%)
  other arithmetic  3.97 us (3%)
  matrix products  3.63 us (3%)
    ppermute x8, starting transfers between devices, butterfly_sum(): lax.ppermute(value, AXES, [(i, i ^ stride) for i in range(length)])  31.2 us
    ppermute x8, waiting for transfers between devices, butterfly_sum(): lax.ppermute(value, AXES, [(i, i ^ stride) for i in range(length)])  26.2 us
    pallas_call x1, Pallas kernels, body(): pl.pallas_call(functools.partial(strip_kernel, rows_dev, half, block, sou...  12.6 us
    ppermute x4, starting transfers between devices, shifted(): lax.ppermute(shard, AXES, [(i, (i + by) % length) for i in range(length)])  10.3 us
    reshape x2, local copies, waits for them, and re-layouts, body(): tiles = upper_tiles.reshape(rows_dev, slots, block, block)  6.96 us
    reshape x2, local copies, waits for them, and re-layouts, body(): return (new_tiles.reshape(rows_dev, slots, tile_size), occupancy)  6.36 us
    convert_element_type x1, local copies, waits for them, and re-layouts, body(): strips = jnp.einsum('rso,rspq->rpoq', pick_band, tiles, preferred_element...  4.6 us
    dot_general x1, matrix products, body(): jnp.einsum('rso,rspq->rpoq', pick_band, tiles, preferred_element_type=jnp...  3.63 us
  transfers between devices with their start and end apart: 12, of which 7 were waited for; matrix products, arithmetic and copies ran while one was open for 11% of the time, Pallas kernels for 0%

profile of v7, /device:TPU:0, one launch (start us, length us, event | category | flops | bytes accessed | tf_op | source)
XLA Modules:
  0.0 127.1 jit_solution(15326372754868427795)
XLA Ops:
  0.7 1.6 %multiply_reduce_fusion = f32[8,17]{0,1:T(8,128)S(1)} fusion(bf16[8,17,4096]{2,0,1:T(8,128)(2,1)} %param.2), kind=kLoop, calls=%fused_computation.4 | loop fusion | flops 1671032 | bytes 1114656 | tf_op jit(solution)/shard_map/reduce_sum | solution.py:91
  2.2 3.4 %reshape.42 = bf16[8,17,64,64]{3,2,0,1:T(8,128)(2,1)S(1)} reshape(bf16[8,17,4096]{2,0,1:T(8,128)(2,1)} %param.2) | data formatting | bytes 2228224 | tf_op jit(solution)/shard_map/reshape | solution.py:95
  5.7 0.9 multiply_reduce_fusion.1
  6.8 3.6 %convert_bitcast_fusion = bf16[8,64,17,64]{3,2,1,0:T(8,128)(2,1)} fusion(bf16[8,17,64,64]{3,2,0,1:T(8,128)(2,1)S(1)} %reshape.42, s32[8,17]{1,0:T(8,128)S(1)} %copy.33, pred[8,17]{1,0:T(8,128)(4,1)S(1)} %copy.32), kind=kOutput, calls=%fused_computation.3 | convolution fusion | flops 19501584 | bytes 2228904 | tf_op jit(solution)/shard_map/rso,rspq->rpoq/dot_general | solution.py:99
  10.5 4.6 %copy.35 = bf16[8,64,17,64]{1,3,2,0:T(8,128)(2,1)} copy(bf16[8,64,17,64]{3,2,1,0:T(8,128)(2,1)} %convert_bitcast_fusion) | data formatting | bytes 2228224 | tf_op jit(solution)/shard_map/convert_element_type | solution.py:101
  15.1 2.8 %copy.36 = bf16[8,64,1088]{2,1,0:T(8,128)(2,1)S(1)} copy(bf16[8,64,1088]{1,2,0:T(8,128)(2,1)} %bitcast.15) | data formatting | bytes 2228224 | tf_op jit(solution)/shard_map/reshape | solution.py:101
  17.9 1.0 copy-done.1
  19.1 2.0 %slice.21 = bf16[8,64,512]{2,1,0:T(8,128)(2,1)} slice(bf16[8,64,1088]{2,1,0:T(8,128)(2,1)} %copy-done.1), slice={[0:8], [0:64], [0:512]} | slice | bytes 1048576 | tf_op jit(solution)/shard_map/slice | solution.py:107
  21.1 8.8 %collective-permute-start.3 = (bf16[8,64,512]{2,1,0:T(8,128)(2,1)}, bf16[8,64,512]{2,1,0:T(8,128)(2,1)}, u32[]{:S(2)}, u32[]{:S(2)}) collective-permute-start(bf16[8,64,512]{2,1,0:T(8,128)(2,1)} %slice.21), channel_id=1, source_target_pairs={{0,254},{1,255},{2,0},{3,1},{4,2},{5,3},{6,4},{7,5},{8,6},{9,7},{1... | collective-permute-start | bytes 1572872 | tf_op jit(solution)/shard_map/ppermute | solution.py:17
  29.9 2.3 %slice.20 = bf16[8,64,1024]{2,1,0:T(8,128)(2,1)} slice(bf16[8,64,1088]{2,1,0:T(8,128)(2,1)} %copy-done.1), slice={[0:8], [0:64], [0:1024]} | slice | bytes 2097152 | tf_op jit(solution)/shard_map/slice | solution.py:106
  32.2 1.4 %collective-permute-start.2 = (bf16[8,64,1024]{2,1,0:T(8,128)(2,1)}, bf16[8,64,1024]{2,1,0:T(8,128)(2,1)S(1)}, u32[]{:S(2)}, u32[]{:S(2)}) collective-permute-start(bf16[8,64,1024]{2,1,0:T(8,128)(2,1)} %slice.20), channel_id=1, source_target_pairs={{0,255},{1,0},{2,1},{3,2},{4,3},{5,4},{6,5},{7,6},{8,7},{9,8},{10,... | collective-permute-start | bytes 3145736 | tf_op jit(solution)/shard_map/ppermute | solution.py:17
  33.6 0.9 pad_slice_fusion
  34.5 0.8 slice_convert_fusion
  35.3 1.9 %copy.41 = f32[8,1,4096]{0,2,1:T(8,128)} copy(f32[8,1,4096]{2,0,1:T(8,128)S(1)} %slice_convert_fusion) | data formatting | bytes 262144 | tf_op jit(solution)/shard_map/convert_element_type | solution.py:88
  37.3 1.5 %gather_fusion = f32[64,8]{1,0:T(8,128)S(1)} fusion(f32[8,64,64]{0,2,1:T(8,128)} %bitcast.16, s32[64]{0:T(128)S(1)} %or_bitcast_fusion), kind=kCustom, calls=%fused_computation | custom fusion | bytes 4608 | tf_op jit(solution)/shard_map/jit(diagonal)/gather | solution.py:89
  38.7 0.6 reduce_sum.27
  40.7 1.0 collective-permute-start.4
  41.7 3.6 %copy.39.tiles_ref = bf16[8,17,64,64]{3,2,1,0:T(8,128)(2,1)} copy(bf16[8,17,64,64]{3,2,0,1:T(8,128)(2,1)} %copy-done) | data formatting | bytes 2228224 | tf_op jit(solution)/shard_map/reshape | solution.py:95
  46.2 2.1 %collective-permute-start.5 = (f32[]{:T(128)}, f32[]{:T(128)}, u32[]{:S(2)}, u32[]{:S(2)}) collective-permute-start(f32[]{:T(128)} %add.63), channel_id=1, source_target_pairs={{0,2},{1,3},{2,0},{3,1},{4,6},{5,7},{6,4},{7,5},{8,10},{9,11},{10,... | collective-permute-start | bytes 20 | tf_op jit(solution)/shard_map/ppermute | solution.py:24
  48.3 22.3 %collective-permute-done.5 = f32[]{:T(128)} collective-permute-done((f32[]{:T(128)}, f32[]{:T(128)}, u32[]{:S(2)}, u32[]{:S(2)}) %collective-permute-start.5) | collective-permute-done | bytes 36 | tf_op jit(solution)/shard_map/ppermute | solution.py:24
  71.3 3.0 %collective-permute-start.6 = (f32[]{:T(128)}, f32[]{:T(128)}, u32[]{:S(2)}, u32[]{:S(2)}) collective-permute-start(f32[]{:T(128)} %add.64), channel_id=1, source_target_pairs={{0,4},{1,5},{2,6},{3,7},{4,0},{5,1},{6,2},{7,3},{8,12},{9,13},{10,... | collective-permute-start | bytes 20 | tf_op jit(solution)/shard_map/ppermute | solution.py:24
  74.3 0.8 collective-permute-done.6
  75.7 4.3 %collective-permute-start.7 = (f32[]{:T(128)}, f32[]{:T(128)}, u32[]{:S(2)}, u32[]{:S(2)}) collective-permute-start(f32[]{:T(128)} %add.65), channel_id=1, source_target_pairs={{0,8},{1,9},{2,10},{3,11},{4,12},{5,13},{6,14},{7,15},{8,0},{9,1},... | collective-permute-start | bytes 20 | tf_op jit(solution)/shard_map/ppermute | solution.py:24
  80.0 1.0 collective-permute-done.7
  81.6 4.4 %collective-permute-start.8 = (f32[]{:T(128)}, f32[]{:T(128)}, u32[]{:S(2)}, u32[]{:S(2)}) collective-permute-start(f32[]{:T(128)} %add.66), channel_id=1, source_target_pairs={{0,16},{1,17},{2,18},{3,19},{4,20},{5,21},{6,22},{7,23},{8,24},{9,... | collective-permute-start | bytes 20 | tf_op jit(solution)/shard_map/ppermute | solution.py:24
  86.0 0.9 collective-permute-done.8
  87.5 3.5 %collective-permute-start.9 = (f32[]{:T(128)}, f32[]{:T(128)}, u32[]{:S(2)}, u32[]{:S(2)}) collective-permute-start(f32[]{:T(128)} %add.67), channel_id=1, source_target_pairs={{0,32},{1,33},{2,34},{3,35},{4,36},{5,37},{6,38},{7,39},{8,40},{9,... | collective-permute-start | bytes 20 | tf_op jit(solution)/shard_map/ppermute | solution.py:24
  92.1 4.7 %collective-permute-start.10 = (f32[]{:T(128)}, f32[]{:T(128)}, u32[]{:S(2)}, u32[]{:S(2)}) collective-permute-start(f32[]{:T(128)} %add.68), channel_id=1, source_target_pairs={{0,64},{1,65},{2,66},{3,67},{4,68},{5,69},{6,70},{7,71},{8,72},{9,... | collective-permute-start | bytes 20 | tf_op jit(solution)/shard_map/ppermute | solution.py:24
  97.7 8.2 %collective-permute-start.11 = (f32[]{:T(128)}, f32[]{:T(128)}, u32[]{:S(2)}, u32[]{:S(2)}) collective-permute-start(f32[]{:T(128)} %add.69), channel_id=1, source_target_pairs={{0,128},{1,129},{2,130},{3,131},{4,132},{5,133},{6,134},{7,135},{8... | collective-permute-start | bytes 20 | tf_op jit(solution)/shard_map/ppermute | solution.py:24
  107.0 12.6 %shard_map.41 = f32[8,17,64,64]{3,2,1,0:T(8,128)} custom-call(s32[136]{0:T(256)S(1)} %reshape.41.sel_ref, s32[136]{0:T(256)S(1)} %reshape.45.lst_ref, bf16[8,17,64,64]{3,2,1,0:T(8,128)(2,1)} %copy.39.tiles_ref, bf16[8,64,1152]{2,1,0:T(8,128)(2,1)S(1)} %pad.4.own_ref, bf16[8,64,640]{2,1,0:T(8,128)(2,1)} %collective-permute-done.p2_ref, ...), custom_call_target="tpu_custom_call" | custom-call | flops 4026531840 | bytes 8388608 | tf_op jit(solution)/shard_map/pallas_call | solution.py:116
  119.6 3.7 %reshape.54 = f32[8,17,4096]{2,1,0:T(8,128)S(1)} reshape(f32[8,17,64,64]{3,2,1,0:T(8,128)} %shard_map.41) | data formatting | bytes 4456448 | tf_op jit(solution)/shard_map/reshape | solution.py:128
  123.3 2.7 %copy.43 = f32[8,17,4096]{2,0,1:T(8,128)} copy(f32[8,17,4096]{2,1,0:T(8,128)S(1)} %reshape.54) | data formatting | bytes 4456448 | tf_op jit(solution)/shard_map/reshape | solution.py:128
  (30 shorter events, 2.0 us)
Async XLA Ops:
  0.6 5.0 %copy-start.3 = (s32[8,17]{1,0:T(8,128)S(1)}, s32[8,17]{1,0:T(8,128)}, u32[]{:S(2)}) copy-start(s32[8,17]{1,0:T(8,128)} %param.3) | copy-start | bytes 1636
  5.6 4.8 %copy-start = (bf16[8,17,64,64]{3,2,0,1:T(8,128)(2,1)}, bf16[8,17,64,64]{3,2,0,1:T(8,128)(2,1)S(1)}, u32[]{:S(2)}) copy-start(bf16[8,17,64,64]{3,2,0,1:T(8,128)(2,1)S(1)} %reshape.42) | copy-start | bytes 3342340
  17.9 1.0 copy-start.1
  19.0 14.5 %copy-start.2 = (bf16[8,64,1088]{2,1,0:T(8,128)(2,1)S(1)}, bf16[8,64,1088]{2,1,0:T(8,128)(2,1)}, u32[]{:S(2)}) copy-start(bf16[8,64,1088]{2,1,0:T(8,128)(2,1)} %copy-done.1) | copy-start | bytes 3342340
  19.1 87.9 %collective-permute-start.1 = (bf16[8,64,1152]{2,1,0:T(8,128)(2,1)S(1)}, bf16[8,64,1152]{2,1,0:T(8,128)(2,1)S(1)}, u32[]{:S(2)}, u32[]{:S(2)}) collective-permute-start(bf16[8,64,1152]{2,1,0:T(8,128)(2,1)S(1)} %pad.4.own_ref), channel_id=1, source_target_pairs={{0,1},{1,2},{2,3},{3,4},{4,5},{5,6},{6,7},{7,8},{8,9},{9,10},{10,1... | collective-permute-start | bytes 3538952 | tf_op jit(solution)/shard_map/ppermute | solution.py:17
  21.1 85.8 %collective-permute-start.3 = (bf16[8,64,512]{2,1,0:T(8,128)(2,1)}, bf16[8,64,512]{2,1,0:T(8,128)(2,1)}, u32[]{:S(2)}, u32[]{:S(2)}) collective-permute-start(bf16[8,64,512]{2,1,0:T(8,128)(2,1)} %slice.21), channel_id=1, source_target_pairs={{0,254},{1,255},{2,0},{3,1},{4,2},{5,3},{6,4},{7,5},{8,6},{9,7},{1... | collective-permute-start | bytes 1572872 | tf_op jit(solution)/shard_map/ppermute | solution.py:17
  32.2 74.8 %collective-permute-start.2 = (bf16[8,64,1024]{2,1,0:T(8,128)(2,1)}, bf16[8,64,1024]{2,1,0:T(8,128)(2,1)S(1)}, u32[]{:S(2)}, u32[]{:S(2)}) collective-permute-start(bf16[8,64,1024]{2,1,0:T(8,128)(2,1)} %slice.20), channel_id=1, source_target_pairs={{0,255},{1,0},{2,1},{3,2},{4,3},{5,4},{6,5},{7,6},{8,7},{9,8},{10,... | collective-permute-start | bytes 3145736 | tf_op jit(solution)/shard_map/ppermute | solution.py:17
  34.5 72.5 %collective-permute-start = (bf16[8,64,640]{2,1,0:T(8,128)(2,1)}, bf16[8,64,640]{2,1,0:T(8,128)(2,1)}, u32[]{:S(2)}, u32[]{:S(2)}) collective-permute-start(bf16[8,64,640]{2,1,0:T(8,128)(2,1)} %pad_slice_fusion), channel_id=1, source_target_pairs={{0,2},{1,3},{2,4},{3,5},{4,6},{5,7},{6,8},{7,9},{8,10},{9,11},{10,... | collective-permute-start | bytes 1966088 | tf_op jit(solution)/shard_map/ppermute | solution.py:17
  40.7 4.9 %collective-permute-start.4 = (f32[]{:T(128)}, f32[]{:T(128)}, u32[]{:S(2)}, u32[]{:S(2)}) collective-permute-start(f32[]{:T(128)} %sub.13), channel_id=1, source_target_pairs={{0,1},{1,0},{2,3},{3,2},{4,5},{5,4},{6,7},{7,6},{8,9},{9,8},{10,11... | collective-permute-start | bytes 20 | tf_op jit(solution)/shard_map/ppermute | solution.py:24
  46.2 24.5 %collective-permute-start.5 = (f32[]{:T(128)}, f32[]{:T(128)}, u32[]{:S(2)}, u32[]{:S(2)}) collective-permute-start(f32[]{:T(128)} %add.63), channel_id=1, source_target_pairs={{0,2},{1,3},{2,0},{3,1},{4,6},{5,7},{6,4},{7,5},{8,10},{9,11},{10,... | collective-permute-start | bytes 20 | tf_op jit(solution)/shard_map/ppermute | solution.py:24
  71.3 3.8 %collective-permute-start.6 = (f32[]{:T(128)}, f32[]{:T(128)}, u32[]{:S(2)}, u32[]{:S(2)}) collective-permute-start(f32[]{:T(128)} %add.64), channel_id=1, source_target_pairs={{0,4},{1,5},{2,6},{3,7},{4,0},{5,1},{6,2},{7,3},{8,12},{9,13},{10,... | collective-permute-start | bytes 20 | tf_op jit(solution)/shard_map/ppermute | solution.py:24
  75.7 5.3 %collective-permute-start.7 = (f32[]{:T(128)}, f32[]{:T(128)}, u32[]{:S(2)}, u32[]{:S(2)}) collective-permute-start(f32[]{:T(128)} %add.65), channel_id=1, source_target_pairs={{0,8},{1,9},{2,10},{3,11},{4,12},{5,13},{6,14},{7,15},{8,0},{9,1},... | collective-permute-start | bytes 20 | tf_op jit(solution)/shard_map/ppermute | solution.py:24
  81.6 5.3 %collective-permute-start.8 = (f32[]{:T(128)}, f32[]{:T(128)}, u32[]{:S(2)}, u32[]{:S(2)}) collective-permute-start(f32[]{:T(128)} %add.66), channel_id=1, source_target_pairs={{0,16},{1,17},{2,18},{3,19},{4,20},{5,21},{6,22},{7,23},{8,24},{9,... | collective-permute-start | bytes 20 | tf_op jit(solution)/shard_map/ppermute | solution.py:24
  87.5 3.9 %collective-permute-start.9 = (f32[]{:T(128)}, f32[]{:T(128)}, u32[]{:S(2)}, u32[]{:S(2)}) collective-permute-start(f32[]{:T(128)} %add.67), channel_id=1, source_target_pairs={{0,32},{1,33},{2,34},{3,35},{4,36},{5,37},{6,38},{7,39},{8,40},{9,... | collective-permute-start | bytes 20 | tf_op jit(solution)/shard_map/ppermute | solution.py:24
  92.1 5.0 %collective-permute-start.10 = (f32[]{:T(128)}, f32[]{:T(128)}, u32[]{:S(2)}, u32[]{:S(2)}) collective-permute-start(f32[]{:T(128)} %add.68), channel_id=1, source_target_pairs={{0,64},{1,65},{2,66},{3,67},{4,68},{5,69},{6,70},{7,71},{8,72},{9,... | collective-permute-start | bytes 20 | tf_op jit(solution)/shard_map/ppermute | solution.py:24
  97.7 8.6 %collective-permute-start.11 = (f32[]{:T(128)}, f32[]{:T(128)}, u32[]{:S(2)}, u32[]{:S(2)}) collective-permute-start(f32[]{:T(128)} %add.69), channel_id=1, source_target_pairs={{0,128},{1,129},{2,130},{3,131},{4,132},{5,133},{6,134},{7,135},{8... | collective-permute-start | bytes 20 | tf_op jit(solution)/shard_map/ppermute | solution.py:24

commit v8 on v7

--- a/solution.py
+++ b/solution.py
@@ -19,10 +19,10 @@
 
 def butterfly_sum(value):
     length = lax.axis_size(AXES)
-    stride = 1
-    while stride < length:
+    strides = [1 << k for k in range(length.bit_length() - 1)]
+    order = strides[:1] + strides[5:] + strides[2:5] + strides[1:2] if length == 256 else strides
+    for stride in order:
         value = value + lax.ppermute(value, AXES, [(i, i ^ stride) for i in range(length)])
-        stride *= 2
     return value
 
 

time: 129 us -> 108 us (0.84)
  starting transfers between devices: 41.4 us -> 30.9 us
  waiting for transfers between devices: 26.2 us -> 16 us
    ppermute x8, starting transfers between devices: 31.2 us -> 20.7 us  [butterfly_sum(): lax.ppermute(value, AXES, [(i, i ^ stride) for i in range(length)])]
    ppermute x8, waiting for transfers between devices: 26.2 us -> 16 us  [butterfly_sum(): lax.ppermute(value, AXES, [(i, i ^ stride) for i in range(length)])]
  transfers between devices with their start and end apart: 12 -> 12, of which waited for: 7 -> 7; matrix products, arithmetic and copies ran while one was open for 11% -> 13% of each run, Pallas kernels for 0% -> 0%
where the time goes in v8:
time: 108 us; the launch traced here: 106 us
  local copies, waits for them, and re-layouts  31 us (29%)
  starting transfers between devices  30.9 us (29%)
  waiting for transfers between devices  16 us (15%)
  Pallas kernels  12.6 us (12%)
  between operations  8.27 us (8%)
  other arithmetic  3.97 us (4%)
  matrix products  3.63 us (3%)
    ppermute x8, starting transfers between devices, butterfly_sum(): lax.ppermute(value, AXES, [(i, i ^ stride) for i in range(length)])  20.7 us
    ppermute x8, waiting for transfers between devices, butterfly_sum(): lax.ppermute(value, AXES, [(i, i ^ stride) for i in range(length)])  16 us
    pallas_call x1, Pallas kernels, body(): pl.pallas_call(functools.partial(strip_kernel, rows_dev, half, block, sou...  12.6 us
    ppermute x4, starting transfers between devices, shifted(): lax.ppermute(shard, AXES, [(i, (i + by) % length) for i in range(length)])  10.3 us
    reshape x2, local copies, waits for them, and re-layouts, body(): tiles = upper_tiles.reshape(rows_dev, slots, block, block)  6.96 us
    reshape x2, local copies, waits for them, and re-layouts, body(): return (new_tiles.reshape(rows_dev, slots, tile_size), occupancy)  6.36 us
    convert_element_type x1, local copies, waits for them, and re-layouts, body(): strips = jnp.einsum('rso,rspq->rpoq', pick_band, tiles, preferred_element...  4.6 us
    dot_general x1, matrix products, body(): jnp.einsum('rso,rspq->rpoq', pick_band, tiles, preferred_element_type=jnp...  3.63 us
  transfers between devices with their start and end apart: 12, of which 7 were waited for; matrix products, arithmetic and copies ran while one was open for 13% of the time, Pallas kernels for 0%

profile of v8, /device:TPU:0, one launch (start us, length us, event | category | flops | bytes accessed | tf_op | source)
XLA Modules:
  0.0 106.5 jit_solution(6100075344633197049)
XLA Ops:
  0.7 1.6 %multiply_reduce_fusion = f32[8,17]{0,1:T(8,128)S(1)} fusion(bf16[8,17,4096]{2,0,1:T(8,128)(2,1)} %param.2), kind=kLoop, calls=%fused_computation.4 | loop fusion | flops 1671032 | bytes 1114656 | tf_op jit(solution)/shard_map/reduce_sum | solution.py:91
  2.2 3.4 %reshape.42 = bf16[8,17,64,64]{3,2,0,1:T(8,128)(2,1)S(1)} reshape(bf16[8,17,4096]{2,0,1:T(8,128)(2,1)} %param.2) | data formatting | bytes 2228224 | tf_op jit(solution)/shard_map/reshape | solution.py:95
  5.7 0.9 multiply_reduce_fusion.1
  6.8 3.6 %convert_bitcast_fusion = bf16[8,64,17,64]{3,2,1,0:T(8,128)(2,1)} fusion(bf16[8,17,64,64]{3,2,0,1:T(8,128)(2,1)S(1)} %reshape.42, s32[8,17]{1,0:T(8,128)S(1)} %copy.33, pred[8,17]{1,0:T(8,128)(4,1)S(1)} %copy.32), kind=kOutput, calls=%fused_computation.3 | convolution fusion | flops 19501584 | bytes 2228904 | tf_op jit(solution)/shard_map/rso,rspq->rpoq/dot_general | solution.py:99
  10.5 4.6 %copy.35 = bf16[8,64,17,64]{1,3,2,0:T(8,128)(2,1)} copy(bf16[8,64,17,64]{3,2,1,0:T(8,128)(2,1)} %convert_bitcast_fusion) | data formatting | bytes 2228224 | tf_op jit(solution)/shard_map/convert_element_type | solution.py:101
  15.1 2.8 %copy.36 = bf16[8,64,1088]{2,1,0:T(8,128)(2,1)S(1)} copy(bf16[8,64,1088]{1,2,0:T(8,128)(2,1)} %bitcast.15) | data formatting | bytes 2228224 | tf_op jit(solution)/shard_map/reshape | solution.py:101
  17.9 1.0 copy-done.1
  19.1 2.0 %slice.21 = bf16[8,64,512]{2,1,0:T(8,128)(2,1)} slice(bf16[8,64,1088]{2,1,0:T(8,128)(2,1)} %copy-done.1), slice={[0:8], [0:64], [0:512]} | slice | bytes 1048576 | tf_op jit(solution)/shard_map/slice | solution.py:107
  21.1 8.8 %collective-permute-start.3 = (bf16[8,64,512]{2,1,0:T(8,128)(2,1)}, bf16[8,64,512]{2,1,0:T(8,128)(2,1)}, u32[]{:S(2)}, u32[]{:S(2)}) collective-permute-start(bf16[8,64,512]{2,1,0:T(8,128)(2,1)} %slice.21), channel_id=1, source_target_pairs={{0,254},{1,255},{2,0},{3,1},{4,2},{5,3},{6,4},{7,5},{8,6},{9,7},{1... | collective-permute-start | bytes 1572872 | tf_op jit(solution)/shard_map/ppermute | solution.py:17
  29.9 2.3 %slice.20 = bf16[8,64,1024]{2,1,0:T(8,128)(2,1)} slice(bf16[8,64,1088]{2,1,0:T(8,128)(2,1)} %copy-done.1), slice={[0:8], [0:64], [0:1024]} | slice | bytes 2097152 | tf_op jit(solution)/shard_map/slice | solution.py:106
  32.2 1.4 %collective-permute-start.2 = (bf16[8,64,1024]{2,1,0:T(8,128)(2,1)}, bf16[8,64,1024]{2,1,0:T(8,128)(2,1)S(1)}, u32[]{:S(2)}, u32[]{:S(2)}) collective-permute-start(bf16[8,64,1024]{2,1,0:T(8,128)(2,1)} %slice.20), channel_id=1, source_target_pairs={{0,255},{1,0},{2,1},{3,2},{4,3},{5,4},{6,5},{7,6},{8,7},{9,8},{10,... | collective-permute-start | bytes 3145736 | tf_op jit(solution)/shard_map/ppermute | solution.py:17
  33.6 0.9 pad_slice_fusion
  34.5 0.8 slice_convert_fusion
  35.3 1.9 %copy.41 = f32[8,1,4096]{0,2,1:T(8,128)} copy(f32[8,1,4096]{2,0,1:T(8,128)S(1)} %slice_convert_fusion) | data formatting | bytes 262144 | tf_op jit(solution)/shard_map/convert_element_type | solution.py:88
  37.3 1.5 %gather_fusion = f32[64,8]{1,0:T(8,128)S(1)} fusion(f32[8,64,64]{0,2,1:T(8,128)} %bitcast.16, s32[64]{0:T(128)S(1)} %or_bitcast_fusion), kind=kCustom, calls=%fused_computation | custom fusion | bytes 4608 | tf_op jit(solution)/shard_map/jit(diagonal)/gather | solution.py:89
  40.7 1.0 collective-permute-start.4
  41.7 3.6 %copy.39.tiles_ref = bf16[8,17,64,64]{3,2,1,0:T(8,128)(2,1)} copy(bf16[8,17,64,64]{3,2,0,1:T(8,128)(2,1)} %copy-done) | data formatting | bytes 2228224 | tf_op jit(solution)/shard_map/reshape | solution.py:95
  46.2 1.4 %collective-permute-start.5 = (f32[]{:T(128)}, f32[]{:T(128)}, u32[]{:S(2)}, u32[]{:S(2)}) collective-permute-start(f32[]{:T(128)} %add.63), channel_id=1, source_target_pairs={{0,32},{1,33},{2,34},{3,35},{4,36},{5,37},{6,38},{7,39},{8,40},{9,... | collective-permute-start | bytes 20 | tf_op jit(solution)/shard_map/ppermute | solution.py:25
  47.6 2.8 %collective-permute-done.5 = f32[]{:T(128)} collective-permute-done((f32[]{:T(128)}, f32[]{:T(128)}, u32[]{:S(2)}, u32[]{:S(2)}) %collective-permute-start.5) | collective-permute-done | bytes 36 | tf_op jit(solution)/shard_map/ppermute | solution.py:25
  51.0 4.7 %collective-permute-start.6 = (f32[]{:T(128)}, f32[]{:T(128)}, u32[]{:S(2)}, u32[]{:S(2)}) collective-permute-start(f32[]{:T(128)} %add.64), channel_id=1, source_target_pairs={{0,64},{1,65},{2,66},{3,67},{4,68},{5,69},{6,70},{7,71},{8,72},{9,... | collective-permute-start | bytes 20 | tf_op jit(solution)/shard_map/ppermute | solution.py:25
  56.7 7.9 %collective-permute-start.7 = (f32[]{:T(128)}, f32[]{:T(128)}, u32[]{:S(2)}, u32[]{:S(2)}) collective-permute-start(f32[]{:T(128)} %add.65), channel_id=1, source_target_pairs={{0,128},{1,129},{2,130},{3,131},{4,132},{5,133},{6,134},{7,135},{8... | collective-permute-start | bytes 20 | tf_op jit(solution)/shard_map/ppermute | solution.py:25
  65.5 1.4 %collective-permute-start.8 = (f32[]{:T(128)}, f32[]{:T(128)}, u32[]{:S(2)}, u32[]{:S(2)}) collective-permute-start(f32[]{:T(128)} %add.66), channel_id=1, source_target_pairs={{0,4},{1,5},{2,6},{3,7},{4,0},{5,1},{6,2},{7,3},{8,12},{9,13},{10,... | collective-permute-start | bytes 20 | tf_op jit(solution)/shard_map/ppermute | solution.py:25
  66.9 2.4 %collective-permute-done.8 = f32[]{:T(128)} collective-permute-done((f32[]{:T(128)}, f32[]{:T(128)}, u32[]{:S(2)}, u32[]{:S(2)}) %collective-permute-start.8) | collective-permute-done | bytes 36 | tf_op jit(solution)/shard_map/ppermute | solution.py:25
  69.9 1.6 %collective-permute-start.9 = (f32[]{:T(128)}, f32[]{:T(128)}, u32[]{:S(2)}, u32[]{:S(2)}) collective-permute-start(f32[]{:T(128)} %add.67), channel_id=1, source_target_pairs={{0,8},{1,9},{2,10},{3,11},{4,12},{5,13},{6,14},{7,15},{8,0},{9,1},... | collective-permute-start | bytes 20 | tf_op jit(solution)/shard_map/ppermute | solution.py:25
  71.5 3.9 %collective-permute-done.9 = f32[]{:T(128)} collective-permute-done((f32[]{:T(128)}, f32[]{:T(128)}, u32[]{:S(2)}, u32[]{:S(2)}) %collective-permute-start.9) | collective-permute-done | bytes 36 | tf_op jit(solution)/shard_map/ppermute | solution.py:25
  76.0 1.4 %collective-permute-start.10 = (f32[]{:T(128)}, f32[]{:T(128)}, u32[]{:S(2)}, u32[]{:S(2)}) collective-permute-start(f32[]{:T(128)} %add.68), channel_id=1, source_target_pairs={{0,16},{1,17},{2,18},{3,19},{4,20},{5,21},{6,22},{7,23},{8,24},{9,... | collective-permute-start | bytes 20 | tf_op jit(solution)/shard_map/ppermute | solution.py:25
  77.4 3.9 %collective-permute-done.10 = f32[]{:T(128)} collective-permute-done((f32[]{:T(128)}, f32[]{:T(128)}, u32[]{:S(2)}, u32[]{:S(2)}) %collective-permute-start.10) | collective-permute-done | bytes 36 | tf_op jit(solution)/shard_map/ppermute | solution.py:25
  81.9 1.4 %collective-permute-start.11 = (f32[]{:T(128)}, f32[]{:T(128)}, u32[]{:S(2)}, u32[]{:S(2)}) collective-permute-start(f32[]{:T(128)} %add.69), channel_id=1, source_target_pairs={{0,2},{1,3},{2,0},{3,1},{4,6},{5,7},{6,4},{7,5},{8,10},{9,11},{10,... | collective-permute-start | bytes 20 | tf_op jit(solution)/shard_map/ppermute | solution.py:25
  83.3 2.4 %collective-permute-done.11 = f32[]{:T(128)} collective-permute-done((f32[]{:T(128)}, f32[]{:T(128)}, u32[]{:S(2)}, u32[]{:S(2)}) %collective-permute-start.11) | collective-permute-done | bytes 36 | tf_op jit(solution)/shard_map/ppermute | solution.py:25
  86.3 12.6 %shard_map.41 = f32[8,17,64,64]{3,2,1,0:T(8,128)} custom-call(s32[136]{0:T(256)S(1)} %reshape.41.sel_ref, s32[136]{0:T(256)S(1)} %reshape.45.lst_ref, bf16[8,17,64,64]{3,2,1,0:T(8,128)(2,1)} %copy.39.tiles_ref, bf16[8,64,1152]{2,1,0:T(8,128)(2,1)S(1)} %pad.4.own_ref, bf16[8,64,640]{2,1,0:T(8,128)(2,1)} %collective-permute-done.p2_ref, ...), custom_call_target="tpu_custom_call" | custom-call | flops 4026531840 | bytes 8388608 | tf_op jit(solution)/shard_map/pallas_call | solution.py:116
  99.0 3.7 %reshape.54 = f32[8,17,4096]{2,1,0:T(8,128)S(1)} reshape(f32[8,17,64,64]{3,2,1,0:T(8,128)} %shard_map.41) | data formatting | bytes 4456448 | tf_op jit(solution)/shard_map/reshape | solution.py:128
  102.7 2.7 %copy.43 = f32[8,17,4096]{2,0,1:T(8,128)} copy(f32[8,17,4096]{2,1,0:T(8,128)S(1)} %reshape.54) | data formatting | bytes 4456448 | tf_op jit(solution)/shard_map/reshape | solution.py:128
  (30 shorter events, 2.2 us)
Async XLA Ops:
  0.6 5.0 %copy-start.3 = (s32[8,17]{1,0:T(8,128)S(1)}, s32[8,17]{1,0:T(8,128)}, u32[]{:S(2)}) copy-start(s32[8,17]{1,0:T(8,128)} %param.3) | copy-start | bytes 1636
  5.6 4.8 %copy-start = (bf16[8,17,64,64]{3,2,0,1:T(8,128)(2,1)}, bf16[8,17,64,64]{3,2,0,1:T(8,128)(2,1)S(1)}, u32[]{:S(2)}) copy-start(bf16[8,17,64,64]{3,2,0,1:T(8,128)(2,1)S(1)} %reshape.42) | copy-start | bytes 3342340
  17.9 1.0 copy-start.1
  19.0 14.5 %copy-start.2 = (bf16[8,64,1088]{2,1,0:T(8,128)(2,1)S(1)}, bf16[8,64,1088]{2,1,0:T(8,128)(2,1)}, u32[]{:S(2)}) copy-start(bf16[8,64,1088]{2,1,0:T(8,128)(2,1)} %copy-done.1) | copy-start | bytes 3342340
  19.1 67.3 %collective-permute-start.1 = (bf16[8,64,1152]{2,1,0:T(8,128)(2,1)S(1)}, bf16[8,64,1152]{2,1,0:T(8,128)(2,1)S(1)}, u32[]{:S(2)}, u32[]{:S(2)}) collective-permute-start(bf16[8,64,1152]{2,1,0:T(8,128)(2,1)S(1)} %pad.4.own_ref), channel_id=1, source_target_pairs={{0,1},{1,2},{2,3},{3,4},{4,5},{5,6},{6,7},{7,8},{8,9},{9,10},{10,1... | collective-permute-start | bytes 3538952 | tf_op jit(solution)/shard_map/ppermute | solution.py:17
  21.1 65.2 %collective-permute-start.3 = (bf16[8,64,512]{2,1,0:T(8,128)(2,1)}, bf16[8,64,512]{2,1,0:T(8,128)(2,1)}, u32[]{:S(2)}, u32[]{:S(2)}) collective-permute-start(bf16[8,64,512]{2,1,0:T(8,128)(2,1)} %slice.21), channel_id=1, source_target_pairs={{0,254},{1,255},{2,0},{3,1},{4,2},{5,3},{6,4},{7,5},{8,6},{9,7},{1... | collective-permute-start | bytes 1572872 | tf_op jit(solution)/shard_map/ppermute | solution.py:17
  32.2 54.1 %collective-permute-start.2 = (bf16[8,64,1024]{2,1,0:T(8,128)(2,1)}, bf16[8,64,1024]{2,1,0:T(8,128)(2,1)S(1)}, u32[]{:S(2)}, u32[]{:S(2)}) collective-permute-start(bf16[8,64,1024]{2,1,0:T(8,128)(2,1)} %slice.20), channel_id=1, source_target_pairs={{0,255},{1,0},{2,1},{3,2},{4,3},{5,4},{6,5},{7,6},{8,7},{9,8},{10,... | collective-permute-start | bytes 3145736 | tf_op jit(solution)/shard_map/ppermute | solution.py:17
  34.5 51.9 %collective-permute-start = (bf16[8,64,640]{2,1,0:T(8,128)(2,1)}, bf16[8,64,640]{2,1,0:T(8,128)(2,1)}, u32[]{:S(2)}, u32[]{:S(2)}) collective-permute-start(bf16[8,64,640]{2,1,0:T(8,128)(2,1)} %pad_slice_fusion), channel_id=1, source_target_pairs={{0,2},{1,3},{2,4},{3,5},{4,6},{5,7},{6,8},{7,9},{8,10},{9,11},{10,... | collective-permute-start | bytes 1966088 | tf_op jit(solution)/shard_map/ppermute | solution.py:17
  40.7 4.9 %collective-permute-start.4 = (f32[]{:T(128)}, f32[]{:T(128)}, u32[]{:S(2)}, u32[]{:S(2)}) collective-permute-start(f32[]{:T(128)} %sub.13), channel_id=1, source_target_pairs={{0,1},{1,0},{2,3},{3,2},{4,5},{5,4},{6,7},{7,6},{8,9},{9,8},{10,11... | collective-permute-start | bytes 20 | tf_op jit(solution)/shard_map/ppermute | solution.py:25
  46.2 4.2 %collective-permute-start.5 = (f32[]{:T(128)}, f32[]{:T(128)}, u32[]{:S(2)}, u32[]{:S(2)}) collective-permute-start(f32[]{:T(128)} %add.63), channel_id=1, source_target_pairs={{0,32},{1,33},{2,34},{3,35},{4,36},{5,37},{6,38},{7,39},{8,40},{9,... | collective-permute-start | bytes 20 | tf_op jit(solution)/shard_map/ppermute | solution.py:25
  51.0 5.0 %collective-permute-start.6 = (f32[]{:T(128)}, f32[]{:T(128)}, u32[]{:S(2)}, u32[]{:S(2)}) collective-permute-start(f32[]{:T(128)} %add.64), channel_id=1, source_target_pairs={{0,64},{1,65},{2,66},{3,67},{4,68},{5,69},{6,70},{7,71},{8,72},{9,... | collective-permute-start | bytes 20 | tf_op jit(solution)/shard_map/ppermute | solution.py:25
  56.7 8.2 %collective-permute-start.7 = (f32[]{:T(128)}, f32[]{:T(128)}, u32[]{:S(2)}, u32[]{:S(2)}) collective-permute-start(f32[]{:T(128)} %add.65), channel_id=1, source_target_pairs={{0,128},{1,129},{2,130},{3,131},{4,132},{5,133},{6,134},{7,135},{8... | collective-permute-start | bytes 20 | tf_op jit(solution)/shard_map/ppermute | solution.py:25
  65.5 3.8 %collective-permute-start.8 = (f32[]{:T(128)}, f32[]{:T(128)}, u32[]{:S(2)}, u32[]{:S(2)}) collective-permute-start(f32[]{:T(128)} %add.66), channel_id=1, source_target_pairs={{0,4},{1,5},{2,6},{3,7},{4,0},{5,1},{6,2},{7,3},{8,12},{9,13},{10,... | collective-permute-start | bytes 20 | tf_op jit(solution)/shard_map/ppermute | solution.py:25
  69.9 5.4 %collective-permute-start.9 = (f32[]{:T(128)}, f32[]{:T(128)}, u32[]{:S(2)}, u32[]{:S(2)}) collective-permute-start(f32[]{:T(128)} %add.67), channel_id=1, source_target_pairs={{0,8},{1,9},{2,10},{3,11},{4,12},{5,13},{6,14},{7,15},{8,0},{9,1},... | collective-permute-start | bytes 20 | tf_op jit(solution)/shard_map/ppermute | solution.py:25
  76.0 5.3 %collective-permute-start.10 = (f32[]{:T(128)}, f32[]{:T(128)}, u32[]{:S(2)}, u32[]{:S(2)}) collective-permute-start(f32[]{:T(128)} %add.68), channel_id=1, source_target_pairs={{0,16},{1,17},{2,18},{3,19},{4,20},{5,21},{6,22},{7,23},{8,24},{9,... | collective-permute-start | bytes 20 | tf_op jit(solution)/shard_map/ppermute | solution.py:25
  81.9 3.8 %collective-permute-start.11 = (f32[]{:T(128)}, f32[]{:T(128)}, u32[]{:S(2)}, u32[]{:S(2)}) collective-permute-start(f32[]{:T(128)} %add.69), channel_id=1, source_target_pairs={{0,2},{1,3},{2,0},{3,1},{4,6},{5,7},{6,4},{7,5},{8,10},{9,11},{10,... | collective-permute-start | bytes 20 | tf_op jit(solution)/shard_map/ppermute | solution.py:25

commit v9 on v8

--- a/solution.py
+++ b/solution.py
@@ -27,7 +27,7 @@
 
 
 def strip_kernel(rows_dev, half, block, sources,
-                 sel_ref, lst_ref, tiles_ref, own_ref, p2_ref, p1_ref, n1_ref, n2_ref,
+                 sel_ref, lst_ref, own_ref, p2_ref, p1_ref, n1_ref, n2_ref,
                  out_ref, strip_ref, band_out_ref):
     slots = half + 1
     window_rows = rows_dev + 2 * half
@@ -65,8 +65,7 @@
 
     for i in range(rows_dev * slots):
         r, s = divmod(i, slots)
-        value = 2.0 * tiles_ref[r, s].astype(jnp.float32) - band_out_ref[sel_ref[i]]
-        out_ref[r, s] = jnp.where(lst_ref[i] > 0, value, 0.0)
+        out_ref[r, s] = jnp.where(lst_ref[i] > 0, band_out_ref[sel_ref[i]], 0.0)
 
 
 def body(upper_tiles, block_columns):
@@ -93,13 +92,13 @@
     occupancy = (total / (nblocks * block)).astype(jnp.float32)
 
     tiles = upper_tiles.reshape(rows_dev, slots, block, block)
-    pick_band = (listed[:, :, None] & (offsets_of[:, :, None] == slot_range[None, None, :])).astype(
+    band_range = jnp.arange(slots + 1, dtype=jnp.int32)
+    pick_band = (listed[:, :, None] & (offsets_of[:, :, None] == band_range[None, None, :])).astype(
         jnp.bfloat16
     )
     strips = jnp.einsum(
         "rso,rspq->rpoq", pick_band, tiles, preferred_element_type=jnp.float32
-    ).astype(jnp.bfloat16).reshape(rows_dev, block, slots * block)
-    strips = jnp.pad(strips, ((0, 0), (0, 0), (0, block)))
+    ).astype(jnp.bfloat16).reshape(rows_dev, block, (slots + 1) * block)
 
     from_prev2 = shifted(strips[:, :, (cut - 1) * block :], 2)
     from_prev1 = shifted(strips, 1)
@@ -116,7 +115,7 @@
     new_tiles = pl.pallas_call(
         functools.partial(strip_kernel, rows_dev, half, block, sources),
         out_shape=jax.ShapeDtypeStruct((rows_dev, slots, block, block), jnp.float32),
-        in_specs=[smem, smem] + [vmem] * 6,
+        in_specs=[smem, smem] + [vmem] * 5,
         out_specs=vmem,
         scratch_shapes=[
             pltpu.VMEM((span_cols * block, window_rows * block), jnp.bfloat16),
@@ -124,8 +123,10 @@
         ],
         compiler_params=pltpu.CompilerParams(vmem_limit_bytes=48 * 1024 * 1024),
         cost_estimate=pl.CostEstimate(flops=flops, bytes_accessed=8 * 1024 * 1024, transcendentals=0),
-    )(sel, lst, tiles, strips, from_prev2, from_prev1, from_next1, from_next2)
-    return (new_tiles.reshape(rows_dev, slots, tile_size), occupancy)
+    )(sel, lst, strips, from_prev2, from_prev1, from_next1, from_next2)
+    picked = new_tiles.reshape(rows_dev, slots, tile_size)
+    new_tiles = jnp.where(listed[:, :, None], 2.0 * upper_tiles.astype(jnp.float32) - picked, 0.0)
+    return (new_tiles, occupancy)
 
 
 def solution(mesh):

time: 108 us -> 103 us (0.954)
  local copies, waits for them, and re-layouts: 31 us -> 17.7 us
  waiting for transfers between devices: 16 us -> 21.8 us
  other arithmetic: 3.97 us -> 7.78 us
    ppermute x8, waiting for transfers between devices: 16 us -> 21.8 us  [butterfly_sum(): lax.ppermute(value, AXES, [(i, i ^ stride) for i in range(length)])]
    convert_element_type x1 -> x0, local copies, waits for them, and re-layouts: 4.6 us -> none  [body(): strips = jnp.einsum('rso,rspq->rpoq', pick_band, tiles, preferred_element...]
    select_n x0 -> x1, other arithmetic: none -> 4.06 us  [body(): jnp.where(listed[:, :, None], 2.0 * upper_tiles.astype(jnp.float32) - pic...]
    reshape x2 -> x1, local copies, waits for them, and re-layouts: 6.96 us -> 3.4 us  [body(): tiles = upper_tiles.reshape(rows_dev, slots, block, block)]
    reshape x2 -> x1, local copies, waits for them, and re-layouts: 6.36 us -> 3.71 us  [body(): picked = new_tiles.reshape(rows_dev, slots, tile_size)]
    slice x1, local copies, waits for them, and re-layouts: 2.28 us -> 1.11 us  [body(): from_next1 = shifted(strips[:, :, :(slots - 1) * block], -1)]
    slice x1, local copies, waits for them, and re-layouts: 1.95 us -> 0.87 us  [body(): from_next2 = shifted(strips[:, :, :(slots - cut) * block], -2)]
  transfers between devices with their start and end apart: 12 -> 12, of which waited for: 7 -> 7; matrix products, arithmetic and copies ran while one was open for 13% -> 8% of each run, Pallas kernels for 0% -> 0%
where the time goes in v9:
time: 103 us; the launch traced here: 101 us
  starting transfers between devices  30.8 us (30%)
  waiting for transfers between devices  21.8 us (21%)
  local copies, waits for them, and re-layouts  17.7 us (17%)
  Pallas kernels  12 us (12%)
  other arithmetic  7.78 us (8%)
  between operations  7.7 us (7%)
  matrix products  3.65 us (4%)
    ppermute x8, waiting for transfers between devices, butterfly_sum(): lax.ppermute(value, AXES, [(i, i ^ stride) for i in range(length)])  21.8 us
    ppermute x8, starting transfers between devices, butterfly_sum(): lax.ppermute(value, AXES, [(i, i ^ stride) for i in range(length)])  20.2 us
    pallas_call x1, Pallas kernels, body(): pl.pallas_call(functools.partial(strip_kernel, rows_dev, half, block, sou...  12 us
    ppermute x4, starting transfers between devices, shifted(): lax.ppermute(shard, AXES, [(i, (i + by) % length) for i in range(length)])  10.6 us
    select_n x1, other arithmetic, body(): jnp.where(listed[:, :, None], 2.0 * upper_tiles.astype(jnp.float32) - pic...  4.06 us
    reshape x1, local copies, waits for them, and re-layouts, body(): picked = new_tiles.reshape(rows_dev, slots, tile_size)  3.71 us
    dot_general x1, matrix products, body(): jnp.einsum('rso,rspq->rpoq', pick_band, tiles, preferred_element_type=jnp...  3.65 us
    reshape x1, local copies, waits for them, and re-layouts, body(): strips = jnp.einsum('rso,rspq->rpoq', pick_band, tiles, preferred_element...  3.53 us
  transfers between devices with their start and end apart: 12, of which 7 were waited for; matrix products, arithmetic and copies ran while one was open for 8% of the time, Pallas kernels for 0%

profile of v9, /device:TPU:0, one launch (start us, length us, event | category | flops | bytes accessed | tf_op | source)
XLA Modules:
  0.0 101.3 jit_solution(10954023433913202324)
XLA Ops:
  0.7 1.6 %fusion.6 = f32[8,17]{0,1:T(8,128)S(1)} fusion(bf16[8,17,4096]{2,0,1:T(8,128)(2,1)} %param.2), kind=kLoop, calls=%fused_computation.8 | loop fusion | flops 1671032 | bytes 1114656 | tf_op jit(solution)/shard_map/reduce_sum | solution.py:90
  2.2 3.4 %reshape.42 = bf16[8,17,64,64]{3,2,0,1:T(8,128)(2,1)S(1)} reshape(bf16[8,17,4096]{2,0,1:T(8,128)(2,1)} %param.2) | data formatting | bytes 2228224 | tf_op jit(solution)/shard_map/reshape | solution.py:94
  5.7 0.7 multiply_reduce_fusion
  6.6 3.6 %convert_bitcast_fusion = bf16[8,64,18,64]{3,2,1,0:T(8,128)(2,1)} fusion(bf16[8,17,64,64]{3,2,0,1:T(8,128)(2,1)S(1)} %reshape.42, s32[8,17]{1,0:T(8,128)S(1)} %copy.24, pred[8,17]{1,0:T(8,128)(4,1)S(1)} %copy.23), kind=kOutput, calls=%fused_computation.3 | convolution fusion | flops 20648736 | bytes 2294440 | tf_op jit(solution)/shard_map/rso,rspq->rpoq/dot_general | solution.py:99
  10.2 3.5 %reshape.43.own_ref = bf16[8,64,1152]{2,1,0:T(8,128)(2,1)S(1)} reshape(bf16[8,64,18,64]{3,2,1,0:T(8,128)(2,1)} %convert_bitcast_fusion) | data formatting | bytes 2359296 | tf_op jit(solution)/shard_map/reshape | solution.py:101
  13.9 1.1 %slice.19 = bf16[8,64,1024]{2,1,0:T(8,128)(2,1)} slice(bf16[8,64,1152]{2,1,0:T(8,128)(2,1)S(1)} %reshape.43.own_ref), slice={[0:8], [0:64], [0:1024]} | slice | bytes 2097152 | tf_op jit(solution)/shard_map/slice | solution.py:105
  15.0 8.2 %collective-permute-start.2 = (bf16[8,64,1024]{2,1,0:T(8,128)(2,1)}, bf16[8,64,1024]{2,1,0:T(8,128)(2,1)S(1)}, u32[]{:S(2)}, u32[]{:S(2)}) collective-permute-start(bf16[8,64,1024]{2,1,0:T(8,128)(2,1)} %slice.19), channel_id=1, source_target_pairs={{0,255},{1,0},{2,1},{3,2},{4,3},{5,4},{6,5},{7,6},{8,7},{9,8},{10,... | collective-permute-start | bytes 3145736 | tf_op jit(solution)/shard_map/ppermute | solution.py:17
  23.2 0.9 slice.20
  24.1 2.3 %collective-permute-start.3 = (bf16[8,64,512]{2,1,0:T(8,128)(2,1)}, bf16[8,64,512]{2,1,0:T(8,128)(2,1)}, u32[]{:S(2)}, u32[]{:S(2)}) collective-permute-start(bf16[8,64,512]{2,1,0:T(8,128)(2,1)} %slice.20), channel_id=1, source_target_pairs={{0,254},{1,255},{2,0},{3,1},{4,2},{5,3},{6,4},{7,5},{8,6},{9,7},{1... | collective-permute-start | bytes 1572872 | tf_op jit(solution)/shard_map/ppermute | solution.py:17
  26.4 0.9 slice.18
  27.3 0.8 slice_convert_fusion
  28.2 1.9 %copy.27 = f32[8,1,4096]{0,2,1:T(8,128)} copy(f32[8,1,4096]{2,0,1:T(8,128)S(1)} %slice_convert_fusion) | data formatting | bytes 262144 | tf_op jit(solution)/shard_map/convert_element_type | solution.py:87
  30.1 1.6 %gather_fusion = f32[64,8]{1,0:T(8,128)S(1)} fusion(f32[8,64,64]{0,2,1:T(8,128)} %bitcast.14, s32[64]{0:T(128)S(1)} %or_bitcast_fusion), kind=kCustom, calls=%fused_computation | custom fusion | bytes 4608 | tf_op jit(solution)/shard_map/jit(diagonal)/gather | solution.py:88
  31.7 0.6 reduce_sum.27
  33.6 1.0 %collective-permute-start.4 = (f32[]{:T(128)}, f32[]{:T(128)}, u32[]{:S(2)}, u32[]{:S(2)}) collective-permute-start(f32[]{:T(128)} %sub.17), channel_id=1, source_target_pairs={{0,1},{1,0},{2,3},{3,2},{4,5},{5,4},{6,7},{7,6},{8,9},{9,8},{10,11... | collective-permute-start | bytes 20 | tf_op jit(solution)/shard_map/ppermute | solution.py:25
  35.5 1.4 %collective-permute-start.5 = (f32[]{:T(128)}, f32[]{:T(128)}, u32[]{:S(2)}, u32[]{:S(2)}) collective-permute-start(f32[]{:T(128)} %add.61), channel_id=1, source_target_pairs={{0,32},{1,33},{2,34},{3,35},{4,36},{5,37},{6,38},{7,39},{8,40},{9,... | collective-permute-start | bytes 20 | tf_op jit(solution)/shard_map/ppermute | solution.py:25
  36.9 8.5 %collective-permute-done.5 = f32[]{:T(128)} collective-permute-done((f32[]{:T(128)}, f32[]{:T(128)}, u32[]{:S(2)}, u32[]{:S(2)}) %collective-permute-start.5) | collective-permute-done | bytes 36 | tf_op jit(solution)/shard_map/ppermute | solution.py:25
  46.0 4.7 %collective-permute-start.6 = (f32[]{:T(128)}, f32[]{:T(128)}, u32[]{:S(2)}, u32[]{:S(2)}) collective-permute-start(f32[]{:T(128)} %add.62), channel_id=1, source_target_pairs={{0,64},{1,65},{2,66},{3,67},{4,68},{5,69},{6,70},{7,71},{8,72},{9,... | collective-permute-start | bytes 20 | tf_op jit(solution)/shard_map/ppermute | solution.py:25
  50.7 0.4 collective-permute-done.6
  51.6 7.3 %collective-permute-start.7 = (f32[]{:T(128)}, f32[]{:T(128)}, u32[]{:S(2)}, u32[]{:S(2)}) collective-permute-start(f32[]{:T(128)} %add.63), channel_id=1, source_target_pairs={{0,128},{1,129},{2,130},{3,131},{4,132},{5,133},{6,134},{7,135},{8... | collective-permute-start | bytes 20 | tf_op jit(solution)/shard_map/ppermute | solution.py:25
  59.0 0.4 collective-permute-done.7
  59.9 1.4 %collective-permute-start.8 = (f32[]{:T(128)}, f32[]{:T(128)}, u32[]{:S(2)}, u32[]{:S(2)}) collective-permute-start(f32[]{:T(128)} %add.64), channel_id=1, source_target_pairs={{0,4},{1,5},{2,6},{3,7},{4,0},{5,1},{6,2},{7,3},{8,12},{9,13},{10,... | collective-permute-start | bytes 20 | tf_op jit(solution)/shard_map/ppermute | solution.py:25
  61.3 2.4 %collective-permute-done.8 = f32[]{:T(128)} collective-permute-done((f32[]{:T(128)}, f32[]{:T(128)}, u32[]{:S(2)}, u32[]{:S(2)}) %collective-permute-start.8) | collective-permute-done | bytes 36 | tf_op jit(solution)/shard_map/ppermute | solution.py:25
  64.2 1.4 %collective-permute-start.9 = (f32[]{:T(128)}, f32[]{:T(128)}, u32[]{:S(2)}, u32[]{:S(2)}) collective-permute-start(f32[]{:T(128)} %add.65), channel_id=1, source_target_pairs={{0,8},{1,9},{2,10},{3,11},{4,12},{5,13},{6,14},{7,15},{8,0},{9,1},... | collective-permute-start | bytes 20 | tf_op jit(solution)/shard_map/ppermute | solution.py:25
  65.6 3.9 %collective-permute-done.9 = f32[]{:T(128)} collective-permute-done((f32[]{:T(128)}, f32[]{:T(128)}, u32[]{:S(2)}, u32[]{:S(2)}) %collective-permute-start.9) | collective-permute-done | bytes 36 | tf_op jit(solution)/shard_map/ppermute | solution.py:25
  70.0 1.4 %collective-permute-start.10 = (f32[]{:T(128)}, f32[]{:T(128)}, u32[]{:S(2)}, u32[]{:S(2)}) collective-permute-start(f32[]{:T(128)} %add.66), channel_id=1, source_target_pairs={{0,16},{1,17},{2,18},{3,19},{4,20},{5,21},{6,22},{7,23},{8,24},{9,... | collective-permute-start | bytes 20 | tf_op jit(solution)/shard_map/ppermute | solution.py:25
  71.4 3.9 %collective-permute-done.10 = f32[]{:T(128)} collective-permute-done((f32[]{:T(128)}, f32[]{:T(128)}, u32[]{:S(2)}, u32[]{:S(2)}) %collective-permute-start.10) | collective-permute-done | bytes 36 | tf_op jit(solution)/shard_map/ppermute | solution.py:25
  75.9 1.6 %collective-permute-start.11 = (f32[]{:T(128)}, f32[]{:T(128)}, u32[]{:S(2)}, u32[]{:S(2)}) collective-permute-start(f32[]{:T(128)} %add.67), channel_id=1, source_target_pairs={{0,2},{1,3},{2,0},{3,1},{4,6},{5,7},{6,4},{7,5},{8,10},{9,11},{10,... | collective-permute-start | bytes 20 | tf_op jit(solution)/shard_map/ppermute | solution.py:25
  77.4 2.4 %collective-permute-done.11 = f32[]{:T(128)} collective-permute-done((f32[]{:T(128)}, f32[]{:T(128)}, u32[]{:S(2)}, u32[]{:S(2)}) %collective-permute-start.11) | collective-permute-done | bytes 36 | tf_op jit(solution)/shard_map/ppermute | solution.py:25
  80.4 12.0 %shard_map.41 = f32[8,17,64,64]{3,2,1,0:T(8,128)} custom-call(s32[136]{0:T(256)S(1)} %reshape.41.sel_ref, s32[136]{0:T(256)S(1)} %reshape.45.lst_ref, bf16[8,64,1152]{2,1,0:T(8,128)(2,1)S(1)} %reshape.43.own_ref, bf16[8,64,640]{2,1,0:T(8,128)(2,1)} %collective-permute-done.p2_ref, bf16[8,64,1152]{2,1,0:T(8,128)(2,1)S(1)} %collective-permute-done.1.p1_ref, ...), custom_call_target="tpu_custom_call" | custom-call | flops 4026531840 | bytes 8388608 | tf_op jit(solution)/shard_map/pallas_call | solution.py:115
  92.4 3.7 %reshape.54 = f32[8,17,4096]{2,1,0:T(8,128)S(1)} reshape(f32[8,17,64,64]{3,2,1,0:T(8,128)} %shard_map.41) | data formatting | bytes 4456448 | tf_op jit(solution)/shard_map/reshape | solution.py:127
  96.1 4.1 %fusion.5 = f32[8,17,4096]{2,0,1:T(8,128)} fusion(bf16[8,17,4096]{2,0,1:T(8,128)(2,1)} %param.2, f32[8,17,4096]{2,1,0:T(8,128)S(1)} %reshape.54, pred[8,17]{0,1:T(8,128)(4,1)S(1)} %get-tuple-element.3), kind=kLoop, calls=%fused_computation.7 | loop fusion | flops 2228224 | bytes 5570696 | tf_op jit(solution)/shard_map/jit(_where)/select_n | solution.py:128
  (21 shorter events, 0.7 us)
Async XLA Ops:
  0.6 5.0 %copy-start = (s32[8,17]{1,0:T(8,128)S(1)}, s32[8,17]{1,0:T(8,128)}, u32[]{:S(2)}) copy-start(s32[8,17]{1,0:T(8,128)} %param.3) | copy-start | bytes 1636
  13.8 66.6 %collective-permute-start.1 = (bf16[8,64,1152]{2,1,0:T(8,128)(2,1)S(1)}, bf16[8,64,1152]{2,1,0:T(8,128)(2,1)S(1)}, u32[]{:S(2)}, u32[]{:S(2)}) collective-permute-start(bf16[8,64,1152]{2,1,0:T(8,128)(2,1)S(1)} %reshape.43.own_ref), channel_id=1, source_target_pairs={{0,1},{1,2},{2,3},{3,4},{4,5},{5,6},{6,7},{7,8},{8,9},{9,10},{10,1... | collective-permute-start | bytes 3538952 | tf_op jit(solution)/shard_map/ppermute | solution.py:17
  15.0 65.4 %collective-permute-start.2 = (bf16[8,64,1024]{2,1,0:T(8,128)(2,1)}, bf16[8,64,1024]{2,1,0:T(8,128)(2,1)S(1)}, u32[]{:S(2)}, u32[]{:S(2)}) collective-permute-start(bf16[8,64,1024]{2,1,0:T(8,128)(2,1)} %slice.19), channel_id=1, source_target_pairs={{0,255},{1,0},{2,1},{3,2},{4,3},{5,4},{6,5},{7,6},{8,7},{9,8},{10,... | collective-permute-start | bytes 3145736 | tf_op jit(solution)/shard_map/ppermute | solution.py:17
  24.1 56.3 %collective-permute-start.3 = (bf16[8,64,512]{2,1,0:T(8,128)(2,1)}, bf16[8,64,512]{2,1,0:T(8,128)(2,1)}, u32[]{:S(2)}, u32[]{:S(2)}) collective-permute-start(bf16[8,64,512]{2,1,0:T(8,128)(2,1)} %slice.20), channel_id=1, source_target_pairs={{0,254},{1,255},{2,0},{3,1},{4,2},{5,3},{6,4},{7,5},{8,6},{9,7},{1... | collective-permute-start | bytes 1572872 | tf_op jit(solution)/shard_map/ppermute | solution.py:17
  27.3 53.1 %collective-permute-start = (bf16[8,64,640]{2,1,0:T(8,128)(2,1)}, bf16[8,64,640]{2,1,0:T(8,128)(2,1)}, u32[]{:S(2)}, u32[]{:S(2)}) collective-permute-start(bf16[8,64,640]{2,1,0:T(8,128)(2,1)} %slice.18), channel_id=1, source_target_pairs={{0,2},{1,3},{2,4},{3,5},{4,6},{5,7},{6,8},{7,9},{8,10},{9,11},{10,... | collective-permute-start | bytes 1966088 | tf_op jit(solution)/shard_map/ppermute | solution.py:17
  33.6 1.4 %collective-permute-start.4 = (f32[]{:T(128)}, f32[]{:T(128)}, u32[]{:S(2)}, u32[]{:S(2)}) collective-permute-start(f32[]{:T(128)} %sub.17), channel_id=1, source_target_pairs={{0,1},{1,0},{2,3},{3,2},{4,5},{5,4},{6,7},{7,6},{8,9},{9,8},{10,11... | collective-permute-start | bytes 20 | tf_op jit(solution)/shard_map/ppermute | solution.py:25
  35.5 9.9 %collective-permute-start.5 = (f32[]{:T(128)}, f32[]{:T(128)}, u32[]{:S(2)}, u32[]{:S(2)}) collective-permute-start(f32[]{:T(128)} %add.61), channel_id=1, source_target_pairs={{0,32},{1,33},{2,34},{3,35},{4,36},{5,37},{6,38},{7,39},{8,40},{9,... | collective-permute-start | bytes 20 | tf_op jit(solution)/shard_map/ppermute | solution.py:25
  46.0 5.0 %collective-permute-start.6 = (f32[]{:T(128)}, f32[]{:T(128)}, u32[]{:S(2)}, u32[]{:S(2)}) collective-permute-start(f32[]{:T(128)} %add.62), channel_id=1, source_target_pairs={{0,64},{1,65},{2,66},{3,67},{4,68},{5,69},{6,70},{7,71},{8,72},{9,... | collective-permute-start | bytes 20 | tf_op jit(solution)/shard_map/ppermute | solution.py:25
  51.6 7.7 %collective-permute-start.7 = (f32[]{:T(128)}, f32[]{:T(128)}, u32[]{:S(2)}, u32[]{:S(2)}) collective-permute-start(f32[]{:T(128)} %add.63), channel_id=1, source_target_pairs={{0,128},{1,129},{2,130},{3,131},{4,132},{5,133},{6,134},{7,135},{8... | collective-permute-start | bytes 20 | tf_op jit(solution)/shard_map/ppermute | solution.py:25
  59.9 3.8 %collective-permute-start.8 = (f32[]{:T(128)}, f32[]{:T(128)}, u32[]{:S(2)}, u32[]{:S(2)}) collective-permute-start(f32[]{:T(128)} %add.64), channel_id=1, source_target_pairs={{0,4},{1,5},{2,6},{3,7},{4,0},{5,1},{6,2},{7,3},{8,12},{9,13},{10,... | collective-permute-start | bytes 20 | tf_op jit(solution)/shard_map/ppermute | solution.py:25
  64.2 5.3 %collective-permute-start.9 = (f32[]{:T(128)}, f32[]{:T(128)}, u32[]{:S(2)}, u32[]{:S(2)}) collective-permute-start(f32[]{:T(128)} %add.65), channel_id=1, source_target_pairs={{0,8},{1,9},{2,10},{3,11},{4,12},{5,13},{6,14},{7,15},{8,0},{9,1},... | collective-permute-start | bytes 20 | tf_op jit(solution)/shard_map/ppermute | solution.py:25
  70.0 5.3 %collective-permute-start.10 = (f32[]{:T(128)}, f32[]{:T(128)}, u32[]{:S(2)}, u32[]{:S(2)}) collective-permute-start(f32[]{:T(128)} %add.66), channel_id=1, source_target_pairs={{0,16},{1,17},{2,18},{3,19},{4,20},{5,21},{6,22},{7,23},{8,24},{9,... | collective-permute-start | bytes 20 | tf_op jit(solution)/shard_map/ppermute | solution.py:25
  75.9 3.9 %collective-permute-start.11 = (f32[]{:T(128)}, f32[]{:T(128)}, u32[]{:S(2)}, u32[]{:S(2)}) collective-permute-start(f32[]{:T(128)} %add.67), channel_id=1, source_target_pairs={{0,2},{1,3},{2,0},{3,1},{4,6},{5,7},{6,4},{7,5},{8,10},{9,11},{10,... | collective-permute-start | bytes 20 | tf_op jit(solution)/shard_map/ppermute | solution.py:25

commit v10 on v9

--- a/solution.py
+++ b/solution.py
@@ -61,7 +61,8 @@
             for cc in range(per):
                 o = ct * per + cc - r
                 if 0 <= o <= half:
-                    band_out_ref[r * slots + o] = res[r * block:(r + 1) * block, cc * block:(cc + 1) * block]
+                    piece = res[r * block:(r + 1) * block, cc * block:(cc + 1) * block]
+                    band_out_ref[r * slots + o] = piece.reshape(SUB, LANE)
 
     for i in range(rows_dev * slots):
         r, s = divmod(i, slots)
@@ -114,12 +115,12 @@
     flops = 2 * rows_dev * block * window_rows * block * span_cols * block
     new_tiles = pl.pallas_call(
         functools.partial(strip_kernel, rows_dev, half, block, sources),
-        out_shape=jax.ShapeDtypeStruct((rows_dev, slots, block, block), jnp.float32),
+        out_shape=jax.ShapeDtypeStruct((rows_dev, slots, SUB, LANE), jnp.float32),
         in_specs=[smem, smem] + [vmem] * 5,
         out_specs=vmem,
         scratch_shapes=[
             pltpu.VMEM((span_cols * block, window_rows * block), jnp.bfloat16),
-            pltpu.VMEM((rows_dev * slots, block, block), jnp.float32),
+            pltpu.VMEM((rows_dev * slots, SUB, LANE), jnp.float32),
         ],
         compiler_params=pltpu.CompilerParams(vmem_limit_bytes=48 * 1024 * 1024),
         cost_estimate=pl.CostEstimate(flops=flops, bytes_accessed=8 * 1024 * 1024, transcendentals=0),

time: 103 us -> 109 us (1.058)
  Pallas kernels: 12 us -> 18.5 us
  other arithmetic: 7.78 us -> 5.46 us
  local copies, waits for them, and re-layouts: 17.7 us -> 19.6 us
    pallas_call x1, Pallas kernels: 12 us -> 18.5 us  [body(): pl.pallas_call(functools.partial(strip_kernel, rows_dev, half, block, sou...]
    pallas_call x0 -> x1, local copies, waits for them, and re-layouts: none -> 3.26 us  [body(): pl.pallas_call(functools.partial(strip_kernel, rows_dev, half, block, sou...]
    select_n x1, other arithmetic: 4.06 us -> 1.74 us  [body(): jnp.where(listed[:, :, None], 2.0 * upper_tiles.astype(jnp.float32) - pic...]
    reshape x1, local copies, waits for them, and re-layouts: 3.71 us -> 2.5 us  [body(): picked = new_tiles.reshape(rows_dev, slots, tile_size)]
where the time goes in v10:
time: 109 us; the launch traced here: 108 us
  starting transfers between devices  30.8 us (28%)
  waiting for transfers between devices  21.8 us (20%)
  local copies, waits for them, and re-layouts  19.6 us (18%)
  Pallas kernels  18.5 us (17%)
  between operations  7.79 us (7%)
  other arithmetic  5.46 us (5%)
  matrix products  3.64 us (3%)
    ppermute x8, waiting for transfers between devices, butterfly_sum(): lax.ppermute(value, AXES, [(i, i ^ stride) for i in range(length)])  21.8 us
    ppermute x8, starting transfers between devices, butterfly_sum(): lax.ppermute(value, AXES, [(i, i ^ stride) for i in range(length)])  20.2 us
    pallas_call x1, Pallas kernels, body(): pl.pallas_call(functools.partial(strip_kernel, rows_dev, half, block, sou...  18.5 us
    ppermute x4, starting transfers between devices, shifted(): lax.ppermute(shard, AXES, [(i, (i + by) % length) for i in range(length)])  10.6 us
    dot_general x1, matrix products, body(): jnp.einsum('rso,rspq->rpoq', pick_band, tiles, preferred_element_type=jnp...  3.64 us
    reshape x1, local copies, waits for them, and re-layouts, body(): strips = jnp.einsum('rso,rspq->rpoq', pick_band, tiles, preferred_element...  3.53 us
    reshape x1, local copies, waits for them, and re-layouts, body(): tiles = upper_tiles.reshape(rows_dev, slots, block, block)  3.4 us
    pallas_call x1, local copies, waits for them, and re-layouts, body(): pl.pallas_call(functools.partial(strip_kernel, rows_dev, half, block, sou...  3.26 us
  transfers between devices with their start and end apart: 12, of which 7 were waited for; matrix products, arithmetic and copies ran while one was open for 8% of the time, Pallas kernels for 0%

profile of v10, /device:TPU:0, one launch (start us, length us, event | category | flops | bytes accessed | tf_op | source)
XLA Modules:
  0.0 107.6 jit_solution(13863028175994100830)
XLA Ops:
  0.7 1.6 %fusion.6 = f32[8,17]{0,1:T(8,128)S(1)} fusion(bf16[8,17,4096]{2,0,1:T(8,128)(2,1)} %param.2), kind=kLoop, calls=%fused_computation.8 | loop fusion | flops 1671032 | bytes 1114656 | tf_op jit(solution)/shard_map/reduce_sum | solution.py:91
  2.2 3.4 %reshape.42 = bf16[8,17,64,64]{3,2,0,1:T(8,128)(2,1)S(1)} reshape(bf16[8,17,4096]{2,0,1:T(8,128)(2,1)} %param.2) | data formatting | bytes 2228224 | tf_op jit(solution)/shard_map/reshape | solution.py:95
  5.7 0.7 multiply_reduce_fusion
  6.6 3.6 %convert_bitcast_fusion = bf16[8,64,18,64]{3,2,1,0:T(8,128)(2,1)} fusion(bf16[8,17,64,64]{3,2,0,1:T(8,128)(2,1)S(1)} %reshape.42, s32[8,17]{1,0:T(8,128)S(1)} %copy.24, pred[8,17]{1,0:T(8,128)(4,1)S(1)} %copy.23), kind=kOutput, calls=%fused_computation.3 | convolution fusion | flops 20648736 | bytes 2294440 | tf_op jit(solution)/shard_map/rso,rspq->rpoq/dot_general | solution.py:100
  10.2 3.5 %reshape.43.own_ref = bf16[8,64,1152]{2,1,0:T(8,128)(2,1)S(1)} reshape(bf16[8,64,18,64]{3,2,1,0:T(8,128)(2,1)} %convert_bitcast_fusion) | data formatting | bytes 2359296 | tf_op jit(solution)/shard_map/reshape | solution.py:102
  13.9 1.1 %slice.19 = bf16[8,64,1024]{2,1,0:T(8,128)(2,1)} slice(bf16[8,64,1152]{2,1,0:T(8,128)(2,1)S(1)} %reshape.43.own_ref), slice={[0:8], [0:64], [0:1024]} | slice | bytes 2097152 | tf_op jit(solution)/shard_map/slice | solution.py:106
  15.0 8.2 %collective-permute-start.2 = (bf16[8,64,1024]{2,1,0:T(8,128)(2,1)}, bf16[8,64,1024]{2,1,0:T(8,128)(2,1)S(1)}, u32[]{:S(2)}, u32[]{:S(2)}) collective-permute-start(bf16[8,64,1024]{2,1,0:T(8,128)(2,1)} %slice.19), channel_id=1, source_target_pairs={{0,255},{1,0},{2,1},{3,2},{4,3},{5,4},{6,5},{7,6},{8,7},{9,8},{10,... | collective-permute-start | bytes 3145736 | tf_op jit(solution)/shard_map/ppermute | solution.py:17
  23.2 0.9 slice.20
  24.1 2.3 %collective-permute-start.3 = (bf16[8,64,512]{2,1,0:T(8,128)(2,1)}, bf16[8,64,512]{2,1,0:T(8,128)(2,1)}, u32[]{:S(2)}, u32[]{:S(2)}) collective-permute-start(bf16[8,64,512]{2,1,0:T(8,128)(2,1)} %slice.20), channel_id=1, source_target_pairs={{0,254},{1,255},{2,0},{3,1},{4,2},{5,3},{6,4},{7,5},{8,6},{9,7},{1... | collective-permute-start | bytes 1572872 | tf_op jit(solution)/shard_map/ppermute | solution.py:17
  26.3 0.9 slice.18
  27.3 0.8 slice_convert_fusion
  28.1 1.9 %copy.27 = f32[8,1,4096]{0,2,1:T(8,128)} copy(f32[8,1,4096]{2,0,1:T(8,128)S(1)} %slice_convert_fusion) | data formatting | bytes 262144 | tf_op jit(solution)/shard_map/convert_element_type | solution.py:88
  30.0 1.6 %gather_fusion = f32[64,8]{1,0:T(8,128)S(1)} fusion(f32[8,64,64]{0,2,1:T(8,128)} %bitcast.16, s32[64]{0:T(128)S(1)} %or_bitcast_fusion), kind=kCustom, calls=%fused_computation | custom fusion | bytes 4608 | tf_op jit(solution)/shard_map/jit(diagonal)/gather | solution.py:89
  31.6 0.6 reduce_sum.27
  33.5 1.0 collective-permute-start.4
  35.5 1.4 %collective-permute-start.5 = (f32[]{:T(128)}, f32[]{:T(128)}, u32[]{:S(2)}, u32[]{:S(2)}) collective-permute-start(f32[]{:T(128)} %add.61), channel_id=1, source_target_pairs={{0,32},{1,33},{2,34},{3,35},{4,36},{5,37},{6,38},{7,39},{8,40},{9,... | collective-permute-start | bytes 20 | tf_op jit(solution)/shard_map/ppermute | solution.py:25
  36.9 8.6 %collective-permute-done.5 = f32[]{:T(128)} collective-permute-done((f32[]{:T(128)}, f32[]{:T(128)}, u32[]{:S(2)}, u32[]{:S(2)}) %collective-permute-start.5) | collective-permute-done | bytes 36 | tf_op jit(solution)/shard_map/ppermute | solution.py:25
  46.0 4.7 %collective-permute-start.6 = (f32[]{:T(128)}, f32[]{:T(128)}, u32[]{:S(2)}, u32[]{:S(2)}) collective-permute-start(f32[]{:T(128)} %add.62), channel_id=1, source_target_pairs={{0,64},{1,65},{2,66},{3,67},{4,68},{5,69},{6,70},{7,71},{8,72},{9,... | collective-permute-start | bytes 20 | tf_op jit(solution)/shard_map/ppermute | solution.py:25
  50.7 0.4 collective-permute-done.6
  51.6 7.3 %collective-permute-start.7 = (f32[]{:T(128)}, f32[]{:T(128)}, u32[]{:S(2)}, u32[]{:S(2)}) collective-permute-start(f32[]{:T(128)} %add.63), channel_id=1, source_target_pairs={{0,128},{1,129},{2,130},{3,131},{4,132},{5,133},{6,134},{7,135},{8... | collective-permute-start | bytes 20 | tf_op jit(solution)/shard_map/ppermute | solution.py:25
  59.9 1.4 %collective-permute-start.8 = (f32[]{:T(128)}, f32[]{:T(128)}, u32[]{:S(2)}, u32[]{:S(2)}) collective-permute-start(f32[]{:T(128)} %add.64), channel_id=1, source_target_pairs={{0,4},{1,5},{2,6},{3,7},{4,0},{5,1},{6,2},{7,3},{8,12},{9,13},{10,... | collective-permute-start | bytes 20 | tf_op jit(solution)/shard_map/ppermute | solution.py:25
  61.3 2.4 %collective-permute-done.8 = f32[]{:T(128)} collective-permute-done((f32[]{:T(128)}, f32[]{:T(128)}, u32[]{:S(2)}, u32[]{:S(2)}) %collective-permute-start.8) | collective-permute-done | bytes 36 | tf_op jit(solution)/shard_map/ppermute | solution.py:25
  64.2 1.4 %collective-permute-start.9 = (f32[]{:T(128)}, f32[]{:T(128)}, u32[]{:S(2)}, u32[]{:S(2)}) collective-permute-start(f32[]{:T(128)} %add.65), channel_id=1, source_target_pairs={{0,8},{1,9},{2,10},{3,11},{4,12},{5,13},{6,14},{7,15},{8,0},{9,1},... | collective-permute-start | bytes 20 | tf_op jit(solution)/shard_map/ppermute | solution.py:25
  65.6 3.9 %collective-permute-done.9 = f32[]{:T(128)} collective-permute-done((f32[]{:T(128)}, f32[]{:T(128)}, u32[]{:S(2)}, u32[]{:S(2)}) %collective-permute-start.9) | collective-permute-done | bytes 36 | tf_op jit(solution)/shard_map/ppermute | solution.py:25
  70.1 1.4 %collective-permute-start.10 = (f32[]{:T(128)}, f32[]{:T(128)}, u32[]{:S(2)}, u32[]{:S(2)}) collective-permute-start(f32[]{:T(128)} %add.66), channel_id=1, source_target_pairs={{0,16},{1,17},{2,18},{3,19},{4,20},{5,21},{6,22},{7,23},{8,24},{9,... | collective-permute-start | bytes 20 | tf_op jit(solution)/shard_map/ppermute | solution.py:25
  71.5 3.9 %collective-permute-done.10 = f32[]{:T(128)} collective-permute-done((f32[]{:T(128)}, f32[]{:T(128)}, u32[]{:S(2)}, u32[]{:S(2)}) %collective-permute-start.10) | collective-permute-done | bytes 36 | tf_op jit(solution)/shard_map/ppermute | solution.py:25
  75.9 1.6 %collective-permute-start.11 = (f32[]{:T(128)}, f32[]{:T(128)}, u32[]{:S(2)}, u32[]{:S(2)}) collective-permute-start(f32[]{:T(128)} %add.67), channel_id=1, source_target_pairs={{0,2},{1,3},{2,0},{3,1},{4,6},{5,7},{6,4},{7,5},{8,10},{9,11},{10,... | collective-permute-start | bytes 20 | tf_op jit(solution)/shard_map/ppermute | solution.py:25
  77.5 2.4 %collective-permute-done.11 = f32[]{:T(128)} collective-permute-done((f32[]{:T(128)}, f32[]{:T(128)}, u32[]{:S(2)}, u32[]{:S(2)}) %collective-permute-start.11) | collective-permute-done | bytes 36 | tf_op jit(solution)/shard_map/ppermute | solution.py:25
  80.5 18.5 %shard_map.41 = f32[8,17,32,128]{3,2,1,0:T(8,128)} custom-call(s32[136]{0:T(256)S(1)} %reshape.41.sel_ref, s32[136]{0:T(256)S(1)} %reshape.45.lst_ref, bf16[8,64,1152]{2,1,0:T(8,128)(2,1)S(1)} %reshape.43.own_ref, bf16[8,64,640]{2,1,0:T(8,128)(2,1)} %collective-permute-done.p2_ref, bf16[8,64,1152]{2,1,0:T(8,128)(2,1)S(1)} %collective-permute-done.1.p1_ref, ...), custom_call_target="tpu_custom_call" | custom-call | flops 4026531840 | bytes 8388608 | tf_op jit(solution)/shard_map/pallas_call | solution.py:116
  99.0 3.3 %copy.26 = f32[8,17,32,128]{3,2,0,1:T(8,128)} copy(f32[8,17,32,128]{3,2,1,0:T(8,128)} %shard_map.41) | data formatting | bytes 4456448 | tf_op jit(solution)/shard_map/pallas_call | solution.py:116
  102.2 2.5 %reshape.44 = f32[8,17,4096]{2,0,1:T(8,128)S(1)} reshape(f32[8,17,32,128]{3,2,0,1:T(8,128)} %copy.26) | data formatting | bytes 4456448 | tf_op jit(solution)/shard_map/reshape | solution.py:128
  104.8 1.7 %fusion.5 = f32[8,17,4096]{2,0,1:T(8,128)} fusion(f32[8,17,4096]{2,0,1:T(8,128)S(1)} %reshape.44, bf16[8,17,4096]{2,0,1:T(8,128)(2,1)S(1)} %copy-done, pred[8,17]{0,1:T(8,128)(4,1)S(1)} %get-tuple-element.3), kind=kLoop, calls=%fused_computation.7 | loop fusion | flops 2228224 | bytes 5570696 | tf_op jit(solution)/shard_map/jit(_where)/select_n | solution.py:129
  (24 shorter events, 1.1 us)
Async XLA Ops:
  0.6 5.0 %copy-start.1 = (s32[8,17]{1,0:T(8,128)S(1)}, s32[8,17]{1,0:T(8,128)}, u32[]{:S(2)}) copy-start(s32[8,17]{1,0:T(8,128)} %param.3) | copy-start | bytes 1636
  13.8 66.7 %collective-permute-start.1 = (bf16[8,64,1152]{2,1,0:T(8,128)(2,1)S(1)}, bf16[8,64,1152]{2,1,0:T(8,128)(2,1)S(1)}, u32[]{:S(2)}, u32[]{:S(2)}) collective-permute-start(bf16[8,64,1152]{2,1,0:T(8,128)(2,1)S(1)} %reshape.43.own_ref), channel_id=1, source_target_pairs={{0,1},{1,2},{2,3},{3,4},{4,5},{5,6},{6,7},{7,8},{8,9},{9,10},{10,1... | collective-permute-start | bytes 3538952 | tf_op jit(solution)/shard_map/ppermute | solution.py:17
  15.0 65.5 %collective-permute-start.2 = (bf16[8,64,1024]{2,1,0:T(8,128)(2,1)}, bf16[8,64,1024]{2,1,0:T(8,128)(2,1)S(1)}, u32[]{:S(2)}, u32[]{:S(2)}) collective-permute-start(bf16[8,64,1024]{2,1,0:T(8,128)(2,1)} %slice.19), channel_id=1, source_target_pairs={{0,255},{1,0},{2,1},{3,2},{4,3},{5,4},{6,5},{7,6},{8,7},{9,8},{10,... | collective-permute-start | bytes 3145736 | tf_op jit(solution)/shard_map/ppermute | solution.py:17
  24.1 56.4 %collective-permute-start.3 = (bf16[8,64,512]{2,1,0:T(8,128)(2,1)}, bf16[8,64,512]{2,1,0:T(8,128)(2,1)}, u32[]{:S(2)}, u32[]{:S(2)}) collective-permute-start(bf16[8,64,512]{2,1,0:T(8,128)(2,1)} %slice.20), channel_id=1, source_target_pairs={{0,254},{1,255},{2,0},{3,1},{4,2},{5,3},{6,4},{7,5},{8,6},{9,7},{1... | collective-permute-start | bytes 1572872 | tf_op jit(solution)/shard_map/ppermute | solution.py:17
  27.3 53.2 %collective-permute-start = (bf16[8,64,640]{2,1,0:T(8,128)(2,1)}, bf16[8,64,640]{2,1,0:T(8,128)(2,1)}, u32[]{:S(2)}, u32[]{:S(2)}) collective-permute-start(bf16[8,64,640]{2,1,0:T(8,128)(2,1)} %slice.18), channel_id=1, source_target_pairs={{0,2},{1,3},{2,4},{3,5},{4,6},{5,7},{6,8},{7,9},{8,10},{9,11},{10,... | collective-permute-start | bytes 1966088 | tf_op jit(solution)/shard_map/ppermute | solution.py:17
  33.5 1.4 %collective-permute-start.4 = (f32[]{:T(128)}, f32[]{:T(128)}, u32[]{:S(2)}, u32[]{:S(2)}) collective-permute-start(f32[]{:T(128)} %sub.17), channel_id=1, source_target_pairs={{0,1},{1,0},{2,3},{3,2},{4,5},{5,4},{6,7},{7,6},{8,9},{9,8},{10,11... | collective-permute-start | bytes 20 | tf_op jit(solution)/shard_map/ppermute | solution.py:25
  35.5 10.0 %collective-permute-start.5 = (f32[]{:T(128)}, f32[]{:T(128)}, u32[]{:S(2)}, u32[]{:S(2)}) collective-permute-start(f32[]{:T(128)} %add.61), channel_id=1, source_target_pairs={{0,32},{1,33},{2,34},{3,35},{4,36},{5,37},{6,38},{7,39},{8,40},{9,... | collective-permute-start | bytes 20 | tf_op jit(solution)/shard_map/ppermute | solution.py:25
  46.0 5.0 %collective-permute-start.6 = (f32[]{:T(128)}, f32[]{:T(128)}, u32[]{:S(2)}, u32[]{:S(2)}) collective-permute-start(f32[]{:T(128)} %add.62), channel_id=1, source_target_pairs={{0,64},{1,65},{2,66},{3,67},{4,68},{5,69},{6,70},{7,71},{8,72},{9,... | collective-permute-start | bytes 20 | tf_op jit(solution)/shard_map/ppermute | solution.py:25
  51.6 7.7 %collective-permute-start.7 = (f32[]{:T(128)}, f32[]{:T(128)}, u32[]{:S(2)}, u32[]{:S(2)}) collective-permute-start(f32[]{:T(128)} %add.63), channel_id=1, source_target_pairs={{0,128},{1,129},{2,130},{3,131},{4,132},{5,133},{6,134},{7,135},{8... | collective-permute-start | bytes 20 | tf_op jit(solution)/shard_map/ppermute | solution.py:25
  59.9 3.8 %collective-permute-start.8 = (f32[]{:T(128)}, f32[]{:T(128)}, u32[]{:S(2)}, u32[]{:S(2)}) collective-permute-start(f32[]{:T(128)} %add.64), channel_id=1, source_target_pairs={{0,4},{1,5},{2,6},{3,7},{4,0},{5,1},{6,2},{7,3},{8,12},{9,13},{10,... | collective-permute-start | bytes 20 | tf_op jit(solution)/shard_map/ppermute | solution.py:25
  64.2 5.3 %collective-permute-start.9 = (f32[]{:T(128)}, f32[]{:T(128)}, u32[]{:S(2)}, u32[]{:S(2)}) collective-permute-start(f32[]{:T(128)} %add.65), channel_id=1, source_target_pairs={{0,8},{1,9},{2,10},{3,11},{4,12},{5,13},{6,14},{7,15},{8,0},{9,1},... | collective-permute-start | bytes 20 | tf_op jit(solution)/shard_map/ppermute | solution.py:25
  70.1 5.3 %collective-permute-start.10 = (f32[]{:T(128)}, f32[]{:T(128)}, u32[]{:S(2)}, u32[]{:S(2)}) collective-permute-start(f32[]{:T(128)} %add.66), channel_id=1, source_target_pairs={{0,16},{1,17},{2,18},{3,19},{4,20},{5,21},{6,22},{7,23},{8,24},{9,... | collective-permute-start | bytes 20 | tf_op jit(solution)/shard_map/ppermute | solution.py:25
  75.9 3.9 %collective-permute-start.11 = (f32[]{:T(128)}, f32[]{:T(128)}, u32[]{:S(2)}, u32[]{:S(2)}) collective-permute-start(f32[]{:T(128)} %add.67), channel_id=1, source_target_pairs={{0,2},{1,3},{2,0},{3,1},{4,6},{5,7},{6,4},{7,5},{8,10},{9,11},{10,... | collective-permute-start | bytes 20 | tf_op jit(solution)/shard_map/ppermute | solution.py:25
  102.2 2.5 %copy-start = (bf16[8,17,4096]{2,0,1:T(8,128)(2,1)S(1)}, bf16[8,17,4096]{2,0,1:T(8,128)(2,1)}, u32[]{:S(2)}) copy-start(bf16[8,17,4096]{2,0,1:T(8,128)(2,1)} %param.2) | copy-start | bytes 3342340

commit v11 on v9

--- a/solution.py
+++ b/solution.py
@@ -84,12 +84,13 @@
     listed = block_columns >= 0
     offsets_of = jnp.mod(block_columns - row_ids[:, None], nblocks)
 
-    diag_own = upper_tiles[:, 0].astype(jnp.float32).reshape(rows_dev, block, block)
-    own_trace = 2.0 * jnp.sum(jnp.diagonal(diag_own, axis1=1, axis2=2))
+    values = upper_tiles.astype(jnp.float32)
     weight = jnp.where(listed, jnp.where(slot_range[None, :] == 0, 1.0, 2.0), 0.0)
-    squares = jnp.sum(jnp.square(upper_tiles.astype(jnp.float32)), axis=2)
-    total = butterfly_sum(own_trace - jnp.sum(weight * squares))
-    occupancy = (total / (nblocks * block)).astype(jnp.float32)
+    on_diag = (lax.broadcasted_iota(jnp.int32, (1, slots, tile_size), 2) % (block + 1) == 0) & (
+        lax.broadcasted_iota(jnp.int32, (1, slots, tile_size), 1) == 0
+    )
+    terms = jnp.where(on_diag, 2.0 * values, 0.0) - weight[:, :, None] * jnp.square(values)
+    total = butterfly_sum(jnp.sum(terms))
 
     tiles = upper_tiles.reshape(rows_dev, slots, block, block)
     band_range = jnp.arange(slots + 1, dtype=jnp.int32)
@@ -106,6 +107,11 @@
     from_next2 = shifted(strips[:, :, : (slots - cut) * block], -2)
     sources = (("p2", cut - 1, slots - cut + 1), ("p1", 0, slots), ("own", 0, slots),
                ("n1", 0, slots - 1), ("n2", 0, slots - cut))
+
+    total, from_prev2, from_prev1, from_next1, from_next2 = lax.optimization_barrier(
+        (total, from_prev2, from_prev1, from_next1, from_next2)
+    )
+    occupancy = (total / (nblocks * block)).astype(jnp.float32)
 
     sel = jnp.where(listed, local_rows[:, None] * slots + offsets_of, 0).reshape(-1).astype(jnp.int32)
     lst = listed.reshape(-1).astype(jnp.int32)

time: 103 us -> 100 us (0.971)
  starting transfers between devices: 30.8 us -> 34.9 us
  local copies, waits for them, and re-layouts: 17.7 us -> 13.9 us
  waiting for transfers between devices: 21.8 us -> 19.4 us
    ppermute x4, starting transfers between devices: 10.6 us -> 15.8 us  [shifted(): lax.ppermute(shard, AXES, [(i, (i + by) % length) for i in range(length)])]
    ppermute x8, waiting for transfers between devices: 21.8 us -> 19.4 us  [butterfly_sum(): lax.ppermute(value, AXES, [(i, i ^ stride) for i in range(length)])]
    convert_element_type x1 -> x0, local copies, waits for them, and re-layouts: 1.93 us -> none  [body(): upper_tiles[:, 0].astype(jnp.float32).reshape(rows_dev, block, block)]
    gather x1 -> x0, local copies, waits for them, and re-layouts: 1.58 us -> none  [body(): own_trace = 2.0 * jnp.sum(jnp.diagonal(diag_own, axis1=1, axis2=2))]
    ppermute x8, starting transfers between devices: 20.2 us -> 19.1 us  [butterfly_sum(): lax.ppermute(value, AXES, [(i, i ^ stride) for i in range(length)])]
    reduce_sum x3 -> x1, other arithmetic: 2.84 us -> 2.59 us  [body(): total = butterfly_sum(jnp.sum(terms))]
  transfers between devices with their start and end apart: 12 -> 12, of which waited for: 7 -> 8; matrix products, arithmetic and copies ran while one was open for 8% -> 6% of each run, Pallas kernels for 0% -> 0%
where the time goes in v11:
time: 100 us; the launch traced here: 98.6 us
  starting transfers between devices  34.9 us (35%)
  waiting for transfers between devices  19.4 us (19%)
  local copies, waits for them, and re-layouts  13.9 us (14%)
  Pallas kernels  12 us (12%)
  between operations  7.97 us (8%)
  other arithmetic  6.89 us (7%)
  matrix products  3.63 us (4%)
    ppermute x8, waiting for transfers between devices, butterfly_sum(): lax.ppermute(value, AXES, [(i, i ^ stride) for i in range(length)])  19.4 us
    ppermute x8, starting transfers between devices, butterfly_sum(): lax.ppermute(value, AXES, [(i, i ^ stride) for i in range(length)])  19.1 us
    ppermute x4, starting transfers between devices, shifted(): lax.ppermute(shard, AXES, [(i, (i + by) % length) for i in range(length)])  15.8 us
    pallas_call x1, Pallas kernels, body(): pl.pallas_call(functools.partial(strip_kernel, rows_dev, half, block, sou...  12 us
    select_n x1, other arithmetic, body(): jnp.where(listed[:, :, None], 2.0 * upper_tiles.astype(jnp.float32) - pic...  4.06 us
    reshape x1, local copies, waits for them, and re-layouts, body(): picked = new_tiles.reshape(rows_dev, slots, tile_size)  3.71 us
    dot_general x1, matrix products, body(): jnp.einsum('rso,rspq->rpoq', pick_band, tiles, preferred_element_type=jnp...  3.63 us
    reshape x1, local copies, waits for them, and re-layouts, body(): strips = jnp.einsum('rso,rspq->rpoq', pick_band, tiles, preferred_element...  3.53 us
  transfers between devices with their start and end apart: 12, of which 8 were waited for; matrix products, arithmetic and copies ran while one was open for 6% of the time, Pallas kernels for 0%

profile of v11, /device:TPU:0, one launch (start us, length us, event | category | flops | bytes accessed | tf_op | source)
XLA Modules:
  0.0 98.6 jit_solution(9644358601716043898)
XLA Ops:
  0.7 3.4 %reshape.99 = bf16[8,17,64,64]{3,2,0,1:T(8,128)(2,1)S(1)} reshape(bf16[8,17,4096]{2,0,1:T(8,128)(2,1)} %param.2) | data formatting | bytes 2228224 | tf_op jit(solution)/shard_map/reshape | solution.py:95
  4.1 0.1 add_select_fusion.1
  4.2 3.6 %convert_bitcast_fusion = bf16[8,64,18,64]{3,2,1,0:T(8,128)(2,1)} fusion(bf16[8,17,64,64]{3,2,0,1:T(8,128)(2,1)S(1)} %reshape.99, s32[8,17]{1,0:T(8,128)S(1)} %get-tuple-element.15, pred[8,17]{1,0:T(8,128)(4,1)S(1)} %get-tuple-element.13), kind=kOutput, calls=%fused_computation.2 | convolution fusion | flops 20648736 | bytes 2294440 | tf_op jit(solution)/shard_map/rso,rspq->rpoq/dot_general | solution.py:100
  7.8 3.5 %reshape.100.own_ref = bf16[8,64,1152]{2,1,0:T(8,128)(2,1)S(1)} reshape(bf16[8,64,18,64]{3,2,1,0:T(8,128)(2,1)} %convert_bitcast_fusion) | data formatting | bytes 2359296 | tf_op jit(solution)/shard_map/reshape | solution.py:102
  11.4 0.1 collective-permute-start.9
  11.4 1.1 %slice.13 = bf16[8,64,1024]{2,1,0:T(8,128)(2,1)} slice(bf16[8,64,1152]{2,1,0:T(8,128)(2,1)S(1)} %reshape.100.own_ref), slice={[0:8], [0:64], [0:1024]} | slice | bytes 2097152 | tf_op jit(solution)/shard_map/slice | solution.py:106
  12.6 8.2 %collective-permute-start.10 = (bf16[8,64,1024]{2,1,0:T(8,128)(2,1)}, bf16[8,64,1024]{2,1,0:T(8,128)(2,1)S(1)}, u32[]{:S(2)}, u32[]{:S(2)}) collective-permute-start(bf16[8,64,1024]{2,1,0:T(8,128)(2,1)} %slice.13), channel_id=1, source_target_pairs={{0,255},{1,0},{2,1},{3,2},{4,3},{5,4},{6,5},{7,6},{8,7},{9,8},{10,... | collective-permute-start | bytes 3145736 | tf_op jit(solution)/shard_map/ppermute | solution.py:17
  20.8 0.9 slice.12
  21.7 0.9 slice.14
  22.6 7.5 %collective-permute-start.11 = (bf16[8,64,512]{2,1,0:T(8,128)(2,1)}, bf16[8,64,512]{2,1,0:T(8,128)(2,1)}, u32[]{:S(2)}, u32[]{:S(2)}) collective-permute-start(bf16[8,64,512]{2,1,0:T(8,128)(2,1)} %slice.14), channel_id=1, source_target_pairs={{0,254},{1,255},{2,0},{3,1},{4,2},{5,3},{6,4},{7,5},{8,6},{9,7},{1... | collective-permute-start | bytes 1572872 | tf_op jit(solution)/shard_map/ppermute | solution.py:17
  30.1 0.1 fusion.10
  30.2 0.1 copy.10
  30.3 2.6 %fusion.7 = f32[]{:T(128)} fusion(bf16[8,17,4096]{2,0,1:T(8,128)(2,1)} %param.2, f32[8,17]{0,1:T(8,128)S(1)} %copy.10, pred[17,4096]{1,0:T(8,128)(4,1)S(1)} %fusion.10), kind=kLoop, calls=%fused_computation.8 | loop fusion | flops 3899391 | bytes 1184292 | tf_op jit(solution)/shard_map/reduce_sum | solution.py:93
  32.9 0.1 copy.8
  33.1 1.0 %collective-permute-done = f32[]{:T(128)} collective-permute-done((f32[]{:T(128)}, f32[]{:T(128)}, u32[]{:S(2)}, u32[]{:S(2)}) %collective-permute-start) | collective-permute-done | bytes 36 | tf_op jit(solution)/shard_map/ppermute | solution.py:25
  35.4 1.4 %collective-permute-start.1 = (f32[]{:T(128)}, f32[]{:T(128)}, u32[]{:S(2)}, u32[]{:S(2)}) collective-permute-start(f32[]{:T(128)} %add.65), channel_id=1, source_target_pairs={{0,32},{1,33},{2,34},{3,35},{4,36},{5,37},{6,38},{7,39},{8,40},{9,... | collective-permute-start | bytes 20 | tf_op jit(solution)/shard_map/ppermute | solution.py:25
  36.8 6.1 %collective-permute-done.1 = f32[]{:T(128)} collective-permute-done((f32[]{:T(128)}, f32[]{:T(128)}, u32[]{:S(2)}, u32[]{:S(2)}) %collective-permute-start.1) | collective-permute-done | bytes 36 | tf_op jit(solution)/shard_map/ppermute | solution.py:25
  43.6 4.7 %collective-permute-start.2 = (f32[]{:T(128)}, f32[]{:T(128)}, u32[]{:S(2)}, u32[]{:S(2)}) collective-permute-start(f32[]{:T(128)} %add.66), channel_id=1, source_target_pairs={{0,64},{1,65},{2,66},{3,67},{4,68},{5,69},{6,70},{7,71},{8,72},{9,... | collective-permute-start | bytes 20 | tf_op jit(solution)/shard_map/ppermute | solution.py:25
  48.2 0.2 collective-permute-done.2
  49.1 7.3 %collective-permute-start.3 = (f32[]{:T(128)}, f32[]{:T(128)}, u32[]{:S(2)}, u32[]{:S(2)}) collective-permute-start(f32[]{:T(128)} %add.67), channel_id=1, source_target_pairs={{0,128},{1,129},{2,130},{3,131},{4,132},{5,133},{6,134},{7,135},{8... | collective-permute-start | bytes 20 | tf_op jit(solution)/shard_map/ppermute | solution.py:25
  56.4 0.2 collective-permute-done.3
  57.3 1.4 %collective-permute-start.4 = (f32[]{:T(128)}, f32[]{:T(128)}, u32[]{:S(2)}, u32[]{:S(2)}) collective-permute-start(f32[]{:T(128)} %add.68), channel_id=1, source_target_pairs={{0,4},{1,5},{2,6},{3,7},{4,0},{5,1},{6,2},{7,3},{8,12},{9,13},{10,... | collective-permute-start | bytes 20 | tf_op jit(solution)/shard_map/ppermute | solution.py:25
  58.7 2.2 %collective-permute-done.4 = f32[]{:T(128)} collective-permute-done((f32[]{:T(128)}, f32[]{:T(128)}, u32[]{:S(2)}, u32[]{:S(2)}) %collective-permute-start.4) | collective-permute-done | bytes 36 | tf_op jit(solution)/shard_map/ppermute | solution.py:25
  61.6 1.4 %collective-permute-start.5 = (f32[]{:T(128)}, f32[]{:T(128)}, u32[]{:S(2)}, u32[]{:S(2)}) collective-permute-start(f32[]{:T(128)} %add.69), channel_id=1, source_target_pairs={{0,8},{1,9},{2,10},{3,11},{4,12},{5,13},{6,14},{7,15},{8,0},{9,1},... | collective-permute-start | bytes 20 | tf_op jit(solution)/shard_map/ppermute | solution.py:25
  63.0 3.7 %collective-permute-done.5 = f32[]{:T(128)} collective-permute-done((f32[]{:T(128)}, f32[]{:T(128)}, u32[]{:S(2)}, u32[]{:S(2)}) %collective-permute-start.5) | collective-permute-done | bytes 36 | tf_op jit(solution)/shard_map/ppermute | solution.py:25
  67.4 1.4 %collective-permute-start.6 = (f32[]{:T(128)}, f32[]{:T(128)}, u32[]{:S(2)}, u32[]{:S(2)}) collective-permute-start(f32[]{:T(128)} %add.70), channel_id=1, source_target_pairs={{0,16},{1,17},{2,18},{3,19},{4,20},{5,21},{6,22},{7,23},{8,24},{9,... | collective-permute-start | bytes 20 | tf_op jit(solution)/shard_map/ppermute | solution.py:25
  68.8 3.7 %collective-permute-done.6 = f32[]{:T(128)} collective-permute-done((f32[]{:T(128)}, f32[]{:T(128)}, u32[]{:S(2)}, u32[]{:S(2)}) %collective-permute-start.6) | collective-permute-done | bytes 36 | tf_op jit(solution)/shard_map/ppermute | solution.py:25
  73.2 1.6 %collective-permute-start.7 = (f32[]{:T(128)}, f32[]{:T(128)}, u32[]{:S(2)}, u32[]{:S(2)}) collective-permute-start(f32[]{:T(128)} %add.71), channel_id=1, source_target_pairs={{0,2},{1,3},{2,0},{3,1},{4,6},{5,7},{6,4},{7,5},{8,10},{9,11},{10,... | collective-permute-start | bytes 20 | tf_op jit(solution)/shard_map/ppermute | solution.py:25
  74.8 2.2 %collective-permute-done.7 = f32[]{:T(128)} collective-permute-done((f32[]{:T(128)}, f32[]{:T(128)}, u32[]{:S(2)}, u32[]{:S(2)}) %collective-permute-start.7) | collective-permute-done | bytes 36 | tf_op jit(solution)/shard_map/ppermute | solution.py:25
  77.7 12.0 %shard_map.41 = f32[8,17,64,64]{3,2,1,0:T(8,128)} custom-call(s32[136]{0:T(256)S(1)} %reshape.98.sel_ref, s32[136]{0:T(256)S(1)} %reshape.102.lst_ref, bf16[8,64,1152]{2,1,0:T(8,128)(2,1)S(1)} %reshape.100.own_ref, bf16[8,64,640]{2,1,0:T(8,128)(2,1)} %collective-permute-done.8.p2_ref, bf16[8,64,1152]{2,1,0:T(8,128)(2,1)S(1)} %collective-permute-done.9.p1_ref, ...), custom_call_target="tpu_custom_call" | custom-call | flops 4026531840 | bytes 8388608 | tf_op jit(solution)/shard_map/pallas_call | solution.py:121
  89.7 3.7 %reshape.104 = f32[8,17,4096]{2,1,0:T(8,128)S(1)} reshape(f32[8,17,64,64]{3,2,1,0:T(8,128)} %shard_map.41) | data formatting | bytes 4456448 | tf_op jit(solution)/shard_map/reshape | solution.py:133
  93.4 4.1 %fusion.8 = f32[8,17,4096]{2,0,1:T(8,128)} fusion(bf16[8,17,4096]{2,0,1:T(8,128)(2,1)} %param.2, f32[8,17,4096]{2,1,0:T(8,128)S(1)} %reshape.104, pred[8,17]{0,1:T(8,128)(4,1)S(1)} %copy.8), kind=kLoop, calls=%fused_computation.9 | loop fusion | flops 2228224 | bytes 5570696 | tf_op jit(solution)/shard_map/jit(_where)/select_n | solution.py:134
  (17 shorter events, 0.2 us)
Async XLA Ops:
  0.6 3.5 %copy-start = (s32[8,17]{1,0:T(8,128)S(1)}, s32[8,17]{1,0:T(8,128)}, u32[]{:S(2)}) copy-start(s32[8,17]{1,0:T(8,128)} %param.3) | copy-start | bytes 1636
  11.4 66.3 %collective-permute-start.9 = (bf16[8,64,1152]{2,1,0:T(8,128)(2,1)S(1)}, bf16[8,64,1152]{2,1,0:T(8,128)(2,1)S(1)}, u32[]{:S(2)}, u32[]{:S(2)}) collective-permute-start(bf16[8,64,1152]{2,1,0:T(8,128)(2,1)S(1)} %reshape.100.own_ref), channel_id=1, source_target_pairs={{0,1},{1,2},{2,3},{3,4},{4,5},{5,6},{6,7},{7,8},{8,9},{9,10},{10,1... | collective-permute-start | bytes 3538952 | tf_op jit(solution)/shard_map/ppermute | solution.py:17
  12.6 65.1 %collective-permute-start.10 = (bf16[8,64,1024]{2,1,0:T(8,128)(2,1)}, bf16[8,64,1024]{2,1,0:T(8,128)(2,1)S(1)}, u32[]{:S(2)}, u32[]{:S(2)}) collective-permute-start(bf16[8,64,1024]{2,1,0:T(8,128)(2,1)} %slice.13), channel_id=1, source_target_pairs={{0,255},{1,0},{2,1},{3,2},{4,3},{5,4},{6,5},{7,6},{8,7},{9,8},{10,... | collective-permute-start | bytes 3145736 | tf_op jit(solution)/shard_map/ppermute | solution.py:17
  21.7 56.0 %collective-permute-start.8 = (bf16[8,64,640]{2,1,0:T(8,128)(2,1)}, bf16[8,64,640]{2,1,0:T(8,128)(2,1)}, u32[]{:S(2)}, u32[]{:S(2)}) collective-permute-start(bf16[8,64,640]{2,1,0:T(8,128)(2,1)} %slice.12), channel_id=1, source_target_pairs={{0,2},{1,3},{2,4},{3,5},{4,6},{5,7},{6,8},{7,9},{8,10},{9,11},{10,... | collective-permute-start | bytes 1966088 | tf_op jit(solution)/shard_map/ppermute | solution.py:17
  22.6 55.1 %collective-permute-start.11 = (bf16[8,64,512]{2,1,0:T(8,128)(2,1)}, bf16[8,64,512]{2,1,0:T(8,128)(2,1)}, u32[]{:S(2)}, u32[]{:S(2)}) collective-permute-start(bf16[8,64,512]{2,1,0:T(8,128)(2,1)} %slice.14), channel_id=1, source_target_pairs={{0,254},{1,255},{2,0},{3,1},{4,2},{5,3},{6,4},{7,5},{8,6},{9,7},{1... | collective-permute-start | bytes 1572872 | tf_op jit(solution)/shard_map/ppermute | solution.py:17
  32.9 1.3 %collective-permute-start = (f32[]{:T(128)}, f32[]{:T(128)}, u32[]{:S(2)}, u32[]{:S(2)}) collective-permute-start(f32[]{:T(128)} %fusion.7), channel_id=1, source_target_pairs={{0,1},{1,0},{2,3},{3,2},{4,5},{5,4},{6,7},{7,6},{8,9},{9,8},{10,11... | collective-permute-start | bytes 20 | tf_op jit(solution)/shard_map/ppermute | solution.py:25
  35.4 7.5 %collective-permute-start.1 = (f32[]{:T(128)}, f32[]{:T(128)}, u32[]{:S(2)}, u32[]{:S(2)}) collective-permute-start(f32[]{:T(128)} %add.65), channel_id=1, source_target_pairs={{0,32},{1,33},{2,34},{3,35},{4,36},{5,37},{6,38},{7,39},{8,40},{9,... | collective-permute-start | bytes 20 | tf_op jit(solution)/shard_map/ppermute | solution.py:25
  43.6 4.9 %collective-permute-start.2 = (f32[]{:T(128)}, f32[]{:T(128)}, u32[]{:S(2)}, u32[]{:S(2)}) collective-permute-start(f32[]{:T(128)} %add.66), channel_id=1, source_target_pairs={{0,64},{1,65},{2,66},{3,67},{4,68},{5,69},{6,70},{7,71},{8,72},{9,... | collective-permute-start | bytes 20 | tf_op jit(solution)/shard_map/ppermute | solution.py:25
  49.1 7.5 %collective-permute-start.3 = (f32[]{:T(128)}, f32[]{:T(128)}, u32[]{:S(2)}, u32[]{:S(2)}) collective-permute-start(f32[]{:T(128)} %add.67), channel_id=1, source_target_pairs={{0,128},{1,129},{2,130},{3,131},{4,132},{5,133},{6,134},{7,135},{8... | collective-permute-start | bytes 20 | tf_op jit(solution)/shard_map/ppermute | solution.py:25
  57.3 3.6 %collective-permute-start.4 = (f32[]{:T(128)}, f32[]{:T(128)}, u32[]{:S(2)}, u32[]{:S(2)}) collective-permute-start(f32[]{:T(128)} %add.68), channel_id=1, source_target_pairs={{0,4},{1,5},{2,6},{3,7},{4,0},{5,1},{6,2},{7,3},{8,12},{9,13},{10,... | collective-permute-start | bytes 20 | tf_op jit(solution)/shard_map/ppermute | solution.py:25
  61.6 5.1 %collective-permute-start.5 = (f32[]{:T(128)}, f32[]{:T(128)}, u32[]{:S(2)}, u32[]{:S(2)}) collective-permute-start(f32[]{:T(128)} %add.69), channel_id=1, source_target_pairs={{0,8},{1,9},{2,10},{3,11},{4,12},{5,13},{6,14},{7,15},{8,0},{9,1},... | collective-permute-start | bytes 20 | tf_op jit(solution)/shard_map/ppermute | solution.py:25
  67.4 5.1 %collective-permute-start.6 = (f32[]{:T(128)}, f32[]{:T(128)}, u32[]{:S(2)}, u32[]{:S(2)}) collective-permute-start(f32[]{:T(128)} %add.70), channel_id=1, source_target_pairs={{0,16},{1,17},{2,18},{3,19},{4,20},{5,21},{6,22},{7,23},{8,24},{9,... | collective-permute-start | bytes 20 | tf_op jit(solution)/shard_map/ppermute | solution.py:25
  73.2 3.8 %collective-permute-start.7 = (f32[]{:T(128)}, f32[]{:T(128)}, u32[]{:S(2)}, u32[]{:S(2)}) collective-permute-start(f32[]{:T(128)} %add.71), channel_id=1, source_target_pairs={{0,2},{1,3},{2,0},{3,1},{4,6},{5,7},{6,4},{7,5},{8,10},{9,11},{10,... | collective-permute-start | bytes 20 | tf_op jit(solution)/shard_map/ppermute | solution.py:25
